TPU v7x, 512 devices: a whole 4x8x8 slice. The times are simulated.
512 devices in a mesh: tiles: 128 (over y, z, core), days: 4 (over x).
Axes of the slice: x: 4, y: 8, z: 8, core: 2. Of those that a mesh axis runs over, the one named last changes fastest.
Arguments:
- observed: bfloat16 [32, 4096, 256], P('days', 'tiles'), may hold values from -4 to 4
- knot_base: bfloat16 [2048, 2, 512], P('tiles', None, 'days'), may hold values from -3 to -2
- knot_steps: bfloat16 [2048, 2, 99, 512], P('tiles', None, None, 'days'), may hold values from 0.019897461 to 0.08984375
- block_route: int32 [2048], P('tiles'), may hold values from 0 to 2047, as said below
- land_mask: int32 [4096, 256], P('tiles'), may hold values 0 or 1
- terrain: float32 [4096, 256], P('tiles'), may hold values from 0.5 to 2
Outputs:
- adjusted: float32 [32, 4096, 256], P('days', 'tiles')
Inputs may be any that keep to these rules, and one draw needn't show every extreme that they name: block_route is a permutation of the blocks; the positions of one tiles device serve blocks of exactly 16 tile owners, 1 block of each.
All inputs are finite; a program needn't handle non-finite values. No bound on the sum of `land_mask` on one device may be relied on, other than what follows from the above.
Results may differ from a plain program's by a relative error of at most 0.005.
Values may be sent and summed in bfloat16 or wider, within the bound.
No kernel may reach another device: no remote copies, remote signals or barrier semaphores. Data moves between devices by JAX's collectives and lax.ppermute only.
A program may use at most 64 MiB of HBM per device.

v0:
```python
import jax
import jax.numpy as jnp
from jax import lax
from jax.sharding import PartitionSpec as P

PASSES = 4


center_share = 0.5


def split_up(value, dim, peers):
    shape = value.shape
    pieces = value.reshape(*shape[:dim], peers, shape[dim] // peers, *shape[dim + 1 :])
    return jnp.moveaxis(pieces, dim, 0)


def joined_along(pieces, dim):
    shape = list(pieces.shape[1:])
    shape[dim] *= pieces.shape[0]
    return jnp.moveaxis(pieces, 0, dim).reshape(shape)


def joined_exchange(value, axis, axes, splits, concats):
    sizes = [lax.axis_size(a) for a in axes]
    pieces = split_up(value, splits[0], sizes[0])
    pieces = jnp.moveaxis(split_up(pieces, splits[1] + 1, sizes[1]), 0, 1)
    inside = pieces.shape[2:]
    pieces = pieces.reshape(-1, *inside)
    pieces = lax.all_to_all(pieces, axis, split_axis=0, concat_axis=0, tiled=True)
    pieces = joined_along(pieces.reshape(*sizes, *inside), concats[0] + 1)
    return joined_along(pieces, concats[1])


def padded_2(cells, sides, width):
    for axis, dim in sides:
        count = lax.axis_size(axis)
        ends = count - 1
        head = lax.slice_in_dim(cells, 0, width, axis=dim)
        tail = lax.slice_in_dim(cells, cells.shape[dim] - width, cells.shape[dim], axis=dim)
        cells = jnp.concatenate(
            [
                lax.ppermute(tail, axis, [(i, (i + 1) % count) for i in range(ends)]),
                cells,
                lax.ppermute(head, axis, [((i + 1) % count, i) for i in range(ends)]),
            ],
            axis=dim,
        )
    return cells


def quantile_map(values, anchor, increments):
    step_x = increments[:, 0].astype(jnp.float32)
    step_y = increments[:, 1].astype(jnp.float32)
    position = anchor[:, 0][:, None, :].astype(jnp.float32) + jnp.cumsum(step_x, axis=1) - step_x
    slopes = step_y / step_x
    covered = jnp.clip(
        values.astype(jnp.float32)[:, :, None, :] - position[None], 0.0, step_x[None]
    )
    return anchor[:, 1].astype(jnp.float32)[None] + jnp.sum(slopes[None] * covered, axis=2)


def map_blocks(values, anchor, increments):
    day_count, nblocks, width = values.shape
    groups = nblocks // 8
    value_groups = values.reshape(day_count, groups, 8, width).transpose(1, 0, 2, 3)
    anchor_groups = anchor.reshape(groups, 8, 2, width)
    step_groups = increments.reshape(groups, 8, 2, -1, width)

    def one_group(group_args):
        return quantile_map(group_args[0], group_args[1], group_args[2]).astype(jnp.bfloat16)

    result = lax.map(one_group, (value_groups, anchor_groups, step_groups))
    return result.transpose(1, 0, 2, 3).reshape(day_count, nblocks, width)


def neighbour_sum(padded):
    return (
        padded[..., :-2, 1:-1]
        + padded[..., 2:, 1:-1]
        + padded[..., 1:-1, :-2]
        + padded[..., 1:-1, 2:]
    )


def body(observed, knot_base, knot_steps, block_route, land_mask, terrain):
    day_count, row_count, columns = observed.shape
    nblocks = block_route.shape[0]
    block_cells = 2 * columns
    ntiles = lax.axis_size("tiles")
    capacity = max(1, nblocks // ntiles)
    target = block_route // nblocks
    place_slot = block_route % nblocks
    onehot = (target[:, None] == jnp.arange(ntiles, dtype=jnp.int32)[None, :]).astype(jnp.int32)
    order_rank = jnp.sum(jnp.cumsum(onehot, axis=0) * onehot, axis=1) - 1
    pair_index = target * capacity + order_rank
    slot_table = jnp.full((ntiles * capacity,), nblocks, jnp.int32).at[pair_index].set(place_slot)
    slot_table = slot_table.reshape(ntiles, capacity)
    local_days = observed.reshape(day_count, nblocks, block_cells)
    recv_slot = lax.all_to_all(
        slot_table, "tiles", split_axis=0, concat_axis=0, tiled=True
    ).reshape(-1)
    picked = jnp.minimum(recv_slot, nblocks - 1)
    outgoing = jnp.take(local_days, picked, axis=1).reshape(
        day_count, ntiles, capacity, block_cells
    )
    arrived = joined_exchange(outgoing, ("tiles", "days"), ("tiles", "days"), (1, 3), (1, 0))
    day_total = arrived.shape[0]
    quarter = arrived.shape[3]
    own_rows = arrived.reshape(day_total, ntiles * capacity, quarter)[:, pair_index, :]
    mapped_part = map_blocks(own_rows, knot_base, knot_steps)
    packed = (
        jnp.zeros((day_total, ntiles * capacity, quarter), jnp.bfloat16)
        .at[:, pair_index, :]
        .set(mapped_part)
    )
    packed = packed.reshape(day_total, ntiles, capacity, quarter)
    returned = joined_exchange(packed, ("tiles", "days"), ("tiles", "days"), (1, 0), (1, 3))
    returned = returned.reshape(day_count, ntiles * capacity, block_cells)
    mapped = (
        jnp.zeros((day_count, nblocks, block_cells), jnp.bfloat16)
        .at[:, recv_slot, :]
        .set(returned, mode="drop")
    )
    weights = terrain * land_mask.astype(jnp.float32)
    field = mapped.reshape(day_count, row_count, columns).astype(jnp.float32)
    depth = PASSES
    stacked = jnp.concatenate((field, weights[None], terrain[None]), axis=0)
    extended = padded_2(stacked.astype(jnp.bfloat16), (("tiles", 1),), depth).astype(stacked.dtype)
    wide_field = extended[:day_count]
    wide_weights = extended[day_count]
    wide_center = center_share * extended[day_count + 1]
    wide_denom = wide_center + neighbour_sum(jnp.pad(wide_weights, 1))
    wide_denom = jnp.where(wide_denom > 0.0, wide_denom, 1.0)
    for sweep in range(PASSES):
        padded = jnp.pad(wide_field * wide_weights[None], ((0, 0), (1, 1), (1, 1)))
        wide_field = (wide_center[None] * wide_field + neighbour_sum(padded)) / wide_denom[None]
    field = wide_field[:, depth : depth + row_count, :]
    return field


def solution(mesh):
    return jax.shard_map(
        body,
        mesh=mesh,
        in_specs=(
            P("days", "tiles", None),
            P("tiles", None, "days"),
            P("tiles", None, None, "days"),
            P("tiles"),
            P("tiles", None),
            P("tiles", None),
        ),
        out_specs=P("days", "tiles", None),
        check_vma=False,
    )
```

profile of v0, /device:TPU:1, one launch (start us, length us, event | category | flops | bytes accessed | tf_op | source)
XLA Modules:
  0.0 147.2 jit_solution(15478635783839566218)
XLA Ops:
  0.0 0.7 and_select_fusion
  0.7 0.1 fusion.35
  0.8 0.2 select_reduce_fusion
  1.0 0.6 scatter_custom_fusion
  1.6 0.7 copy.66
  2.3 18.4 %all-to-all-start = ((s32[128,1,1]{2,1,0:T(1,128)}), s32[128,1,1]{2,1,0:T(1,128)S(1)}, u32[]{:S(2)}, u32[]{:S(2)}) async-start(s32[128,1,1]{2,1,0:T(1,128)} %copy.66), calls=%async_computation | async-start | bytes 131072 | tf_op jit(solution)/shard_map/all_to_all | solution.py:100
  20.8 1.0 reshape.158
  21.7 0.1 copy.69
  21.8 10.4 %all-to-all-done = s32[128,1,1]{2,1,0:T(1,128)S(1)} async-done(((s32[128,1,1]{2,1,0:T(1,128)}), s32[128,1,1]{2,1,0:T(1,128)S(1)}, u32[]{:S(2)}, u32[]{:S(2)}) %all-to-all-start) | async-done | bytes 544 | tf_op jit(solution)/shard_map/all_to_all | solution.py:100
  32.2 4.7 %minimum_reduce_fusion = (s32[128]{0:T(128)S(1)}, s32[128]{0:T(128)S(1)}) fusion(s32[128,1,1]{2,1,0:T(1,128)S(1)} %all-to-all-done), kind=kLoop, calls=%fused_computation.78 | loop fusion | flops 128 | bytes 1536 | tf_op jit(solution)/shard_map/min | solution.py:103
  36.9 0.6 gather_fusion
  37.6 0.2 fusion.11
  37.8 0.2 fusion.44
  38.0 1.2 pad_maximum_fusion
  39.2 0.0 copy-start
  39.2 0.0 copy-start.1
  39.2 8.9 %all-to-all-start.1 = ((bf16[512,8,1,1,128]{4,1,3,2,0:T(8,128)(2,1)}), bf16[512,8,1,1,128]{4,1,3,2,0:T(8,128)(2,1)S(1)}, u32[]{:S(2)}, u32[]{:S(2)}) async-start(bf16[512,8,1,1,128]{4,1,3,2,0:T(8,128)(2,1)} %bitcast.22), calls=%async_computation.1 | async-start | bytes 2097152 | tf_op jit(solution)/shard_map/all_to_all | solution.py:30
  48.1 32.6 %all-to-all-done.1 = bf16[512,8,1,1,128]{4,1,3,2,0:T(8,128)(2,1)S(1)} async-done(((bf16[512,8,1,1,128]{4,1,3,2,0:T(8,128)(2,1)}), bf16[512,8,1,1,128]{4,1,3,2,0:T(8,128)(2,1)S(1)}, u32[]{:S(2)}, u32[]{:S(2)}) %all-to-all-start.1) | async-done | bytes 1048608 | tf_op jit(solution)/shard_map/all_to_all | solution.py:30
  80.7 0.6 gather_fusion.1
  81.3 0.0 copy-done
  81.3 0.0 copy-done.1
  81.3 5.7 %while.10 = (s32[]{:T(128)}, bf16[2,32,8,128]{3,2,0,1:T(8,128)(2,1)S(1)}, bf16[2,8,2,128]{3,2,1,0:T(2,128)(2,1)S(1)}, bf16[2,8,2,99,128]{4,2,3,1,0:T(2,128)(2,1)...) while((s32[]{:T(128)}, bf16[2,32,8,128]{3,2,0,1:T(8,128)(2,1)S(1)}, ...), condition=%wide.region_6.7_spmd, body=%wide.region_3.6_spmd.sunk | while | flops 27033600 | bytes 5892181 | solution.py:73
  81.3 0.3 constant_dynamic-slice_fusion.7
  81.6 0.1 copy.101
  81.7 0.1 add_subtract_fusion.2
  81.9 0.1 convert_divide_fusion.2
  82.0 2.1 %multiply_reduce_fusion.2 = f32[32,8,128]{2,1,0:T(8,128)S(1)} fusion(f32[8,99,128]{2,0,1:T(8,128)S(1)} %add_subtract_fusion.2, f32[32,8,128]{2,1,0:T(8,128)S(1)} %fusion.52, f32[8,99,128]{2,0,1:T(8,128)S(1)} %fusion.53, f32[8,99,128]{2,0,1:T(8,128)S(1)} %convert_divide_fusion.2), kind=kLoop, calls=%fused_computation.5.clone.1 | loop fusion | flops 16187392 | bytes 1478656 | tf_op jit(solution)/shard_map/while/body/eval_jaxpr/reduce_sum | solution.py:60
  84.2 0.3 constant_dynamic-slice_fusion.7
  84.5 0.1 copy.101
  84.6 0.1 add_subtract_fusion.2
  84.7 0.1 convert_divide_fusion.2
  84.9 2.1 %multiply_reduce_fusion.2 = f32[32,8,128]{2,1,0:T(8,128)S(1)} fusion(f32[8,99,128]{2,0,1:T(8,128)S(1)} %add_subtract_fusion.2, f32[32,8,128]{2,1,0:T(8,128)S(1)} %fusion.52, f32[8,99,128]{2,0,1:T(8,128)S(1)} %fusion.53, f32[8,99,128]{2,0,1:T(8,128)S(1)} %convert_divide_fusion.2), kind=kLoop, calls=%fused_computation.5.clone.1 | loop fusion | flops 16187392 | bytes 1478656 | tf_op jit(solution)/shard_map/while/body/eval_jaxpr/reduce_sum | solution.py:60
  87.1 1.1 broadcast_in_dim.37
  88.2 2.2 %scatter_fusion = bf16[32,128,128]{2,0,1:T(8,128)(2,1)} fusion(bf16[32,128,128]{2,0,1:T(8,128)(2,1)} %broadcast_in_dim.37, s32[16]{0:T(128)S(1)} %compare_select_fusion.4, bf16[16,32,128]{2,1,0:T(8,128)(2,1)S(1)} %copy.76), kind=kCustom, calls=%fused_computation.3 | custom fusion | bytes 393280 | tf_op jit(solution)/shard_map/scatter | solution.py:115
  90.4 0.0 copy-start.2
  90.4 0.0 copy-start.3
  90.4 9.3 %all-to-all-start.2 = ((bf16[512,8,1,1,128]{4,1,3,2,0:T(8,128)(2,1)}), bf16[512,8,1,1,128]{4,1,3,2,0:T(8,128)(2,1)S(1)}, u32[]{:S(2)}, u32[]{:S(2)}) async-start(bf16[512,8,1,1,128]{4,1,3,2,0:T(8,128)(2,1)} %bitcast.36), calls=%async_computation.2 | async-start | bytes 2097152 | tf_op jit(solution)/shard_map/all_to_all | solution.py:30
  99.7 0.0 copy-done.2
  99.7 0.0 copy-done.3
  99.8 32.5 %all-to-all-done.2 = bf16[512,8,1,1,128]{4,1,3,2,0:T(8,128)(2,1)S(1)} async-done(((bf16[512,8,1,1,128]{4,1,3,2,0:T(8,128)(2,1)}), bf16[512,8,1,1,128]{4,1,3,2,0:T(8,128)(2,1)S(1)}, u32[]{:S(2)}, u32[]{:S(2)}) %all-to-all-start.2) | async-done | bytes 1048608 | tf_op jit(solution)/shard_map/all_to_all | solution.py:30
  132.3 4.6 %scatter_fusion.1 = bf16[8,16,512]{2,0,1:T(8,128)(2,1)S(1)} fusion(bf16[8,16,512]{2,0,1:T(8,128)(2,1)S(1)} %broadcast_in_dim.35, s32[128]{0:T(128)S(1)} %get-tuple-element.93, bf16[128,8,512]{2,1,0:T(8,128)(2,1)S(1)} %bitcast.142), kind=kCustom, calls=%fused_computation.4 | custom fusion | bytes 3146240 | tf_op jit(solution)/shard_map/scatter | solution.py:123
  137.0 2.9 %collective-permute-start = (bf16[10,4,256]{2,1,0:T(4,128)(2,1)S(1)}, bf16[10,4,256]{2,1,0:T(4,128)(2,1)S(1)}, u32[]{:S(2)}, u32[]{:S(2)}) collective-permute-start(bf16[10,4,256]{2,1,0:T(4,128)(2,1)S(1)} %get-tuple-element.88), channel_id=1, source_target_pairs={{0,4},{4,8},{8,12},{12,16},{16,20},{20,24},{24,28},{28,32},{32,36}... | collective-permute-start | bytes 61448 | tf_op jit(solution)/shard_map/ppermute | solution.py:43
  139.9 1.9 %collective-permute-start.1 = (bf16[10,4,256]{2,1,0:T(4,128)(2,1)S(1)}, bf16[10,4,256]{2,1,0:T(4,128)(2,1)S(1)}, u32[]{:S(2)}, u32[]{:S(2)}) collective-permute-start(bf16[10,4,256]{2,1,0:T(4,128)(2,1)S(1)} %get-tuple-element.89), channel_id=1, source_target_pairs={{4,0},{8,4},{12,8},{16,12},{20,16},{24,20},{28,24},{32,28},{36,32}... | collective-permute-start | bytes 61448 | tf_op jit(solution)/shard_map/ppermute | solution.py:45
  141.9 0.0 collective-permute-done
  141.9 3.2 %collective-permute-done.1 = bf16[10,4,256]{2,1,0:T(4,128)(2,1)S(1)} collective-permute-done((bf16[10,4,256]{2,1,0:T(4,128)(2,1)S(1)}, bf16[10,4,256]{2,1,0:T(4,128)(2,1)S(1)}, u32[]{:S(2)}, u32[]{:S(2)}) %collective-permute-start.1) | collective-permute-done | bytes 20512 | tf_op jit(solution)/shard_map/ppermute | solution.py:45
  145.0 0.1 maximum_convert_fusion
  145.2 0.1 compare_select_fusion
  145.3 0.3 broadcast_multiply_fusion.2
  145.6 0.3 broadcast_multiply_fusion.1
  145.8 0.3 broadcast_multiply_fusion
  146.1 0.2 pad_slice_fusion.3
  146.3 0.9 fusion.28
  (31 shorter events, 0.5 us)
Async XLA Ops:
  2.3 29.9 %all-to-all-start = ((s32[128,1,1]{2,1,0:T(1,128)}), s32[128,1,1]{2,1,0:T(1,128)S(1)}, u32[]{:S(2)}, u32[]{:S(2)}) async-start(s32[128,1,1]{2,1,0:T(1,128)} %copy.66), calls=%async_computation | async-start | bytes 131072 | tf_op jit(solution)/shard_map/all_to_all | solution.py:100
  39.2 42.2 %copy-start = (bf16[16,2,99,128]{3,1,2,0:T(2,128)(2,1)S(1)}, bf16[16,2,99,128]{3,1,2,0:T(2,128)(2,1)}, u32[]{:S(2)}) copy-start(bf16[16,2,99,128]{3,1,2,0:T(2,128)(2,1)} %param.10) | copy-start | bytes 2433028
  39.2 42.2 %copy-start.1 = (bf16[16,2,128]{2,1,0:T(2,128)(2,1)S(1)}, bf16[16,2,128]{2,1,0:T(2,128)(2,1)}, u32[]{:S(2)}) copy-start(bf16[16,2,128]{2,1,0:T(2,128)(2,1)} %param.9) | copy-start | bytes 24580
  39.2 41.6 %all-to-all-start.1 = ((bf16[512,8,1,1,128]{4,1,3,2,0:T(8,128)(2,1)}), bf16[512,8,1,1,128]{4,1,3,2,0:T(8,128)(2,1)S(1)}, u32[]{:S(2)}, u32[]{:S(2)}) async-start(bf16[512,8,1,1,128]{4,1,3,2,0:T(8,128)(2,1)} %bitcast.22), calls=%async_computation.1 | async-start | bytes 2097152 | tf_op jit(solution)/shard_map/all_to_all | solution.py:30
  90.4 9.3 %copy-start.2 = (f32[32,256]{1,0:T(8,128)S(1)}, f32[32,256]{1,0:T(8,128)}, u32[]{:S(2)}) copy-start(f32[32,256]{1,0:T(8,128)} %param.13) | copy-start | bytes 98308
  90.4 9.3 %copy-start.3 = (s32[32,256]{1,0:T(8,128)S(1)}, s32[32,256]{1,0:T(8,128)}, u32[]{:S(2)}) copy-start(s32[32,256]{1,0:T(8,128)} %param.12) | copy-start | bytes 98308
  90.4 41.8 %all-to-all-start.2 = ((bf16[512,8,1,1,128]{4,1,3,2,0:T(8,128)(2,1)}), bf16[512,8,1,1,128]{4,1,3,2,0:T(8,128)(2,1)S(1)}, u32[]{:S(2)}, u32[]{:S(2)}) async-start(bf16[512,8,1,1,128]{4,1,3,2,0:T(8,128)(2,1)} %bitcast.36), calls=%async_computation.2 | async-start | bytes 2097152 | tf_op jit(solution)/shard_map/all_to_all | solution.py:30
  137.0 4.8 %collective-permute-start = (bf16[10,4,256]{2,1,0:T(4,128)(2,1)S(1)}, bf16[10,4,256]{2,1,0:T(4,128)(2,1)S(1)}, u32[]{:S(2)}, u32[]{:S(2)}) collective-permute-start(bf16[10,4,256]{2,1,0:T(4,128)(2,1)S(1)} %get-tuple-element.88), channel_id=1, source_target_pairs={{0,4},{4,8},{8,12},{12,16},{16,20},{20,24},{24,28},{28,32},{32,36}... | collective-permute-start | bytes 61448 | tf_op jit(solution)/shard_map/ppermute | solution.py:43
  139.9 5.1 %collective-permute-start.1 = (bf16[10,4,256]{2,1,0:T(4,128)(2,1)S(1)}, bf16[10,4,256]{2,1,0:T(4,128)(2,1)S(1)}, u32[]{:S(2)}, u32[]{:S(2)}) collective-permute-start(bf16[10,4,256]{2,1,0:T(4,128)(2,1)S(1)} %get-tuple-element.89), channel_id=1, source_target_pairs={{4,0},{8,4},{12,8},{16,12},{20,16},{24,20},{28,24},{32,28},{36,32}... | collective-permute-start | bytes 61448 | tf_op jit(solution)/shard_map/ppermute | solution.py:45
where the time goes:
time: 148 us; the launch traced here: 147 us
  waiting for transfers between devices  78.7 us (53%)
  starting transfers between devices  41.4 us (28%)
  other arithmetic  13.7 us (9%)
  local copies, waits for them, and re-layouts  12.9 us (9%)
    all_to_all x2, waiting for transfers between devices, joined_exchange(): lax.all_to_all(pieces, axis, split_axis=0, concat_axis=0, tiled=True)  65.1 us
    all_to_all x1, starting transfers between devices, body(): lax.all_to_all(slot_table, 'tiles', split_axis=0, concat_axis=0, tiled=True)  18.4 us
    all_to_all x2, starting transfers between devices, joined_exchange(): lax.all_to_all(pieces, axis, split_axis=0, concat_axis=0, tiled=True)  18.2 us
    all_to_all x1, waiting for transfers between devices, body(): lax.all_to_all(slot_table, 'tiles', split_axis=0, concat_axis=0, tiled=True)  10.4 us
    min x1, other arithmetic, body(): picked = jnp.minimum(recv_slot, nblocks - 1)  4.67 us
    scatter x2, local copies, waits for them, and re-layouts, body(): mapped = jnp.zeros((day_count, nblocks, block_cells), jnp.bfloat16).at[:,...  4.67 us
    reduce_sum x2, other arithmetic, quantile_map(): jnp.sum(slopes[None] * covered, axis=2)  4.28 us
    ppermute x1, waiting for transfers between devices, padded_2(): lax.ppermute(head, axis, [((i + 1) % count, i) for i in range(ends)])  3.16 us
  transfers between devices with their start and end apart: 5, of which 4 were waited for; matrix products, arithmetic and copies ran while one was open for 1% of the time, Pallas kernels for 0%

commit v1 on v0

v1 whole, which is shorter than its diff:
```python
import jax
import jax.numpy as jnp
from jax import lax
from jax.sharding import PartitionSpec as P

PASSES = 4


center_share = 0.5


def neighbour_sum(padded):
    return (
        padded[..., :-2, 1:-1]
        + padded[..., 2:, 1:-1]
        + padded[..., 1:-1, :-2]
        + padded[..., 1:-1, 2:]
    )


def with_halo(cells, width):
    count = lax.axis_size("tiles")
    head = cells[..., :width, :]
    tail = cells[..., cells.shape[-2] - width :, :]
    from_above = lax.ppermute(tail, "tiles", [(i, i + 1) for i in range(count - 1)])
    from_below = lax.ppermute(head, "tiles", [(i + 1, i) for i in range(count - 1)])
    return jnp.concatenate([from_above, cells, from_below], axis=-2)


def quantile_map(values, anchor, increments):
    step_x = increments[:, 0].astype(jnp.float32)
    step_y = increments[:, 1].astype(jnp.float32)
    position = anchor[:, 0][:, None, :].astype(jnp.float32) + jnp.cumsum(step_x, axis=1) - step_x
    slopes = step_y / step_x
    covered = jnp.clip(
        values.astype(jnp.float32)[:, :, None, :] - position[:, None], 0.0, step_x[:, None]
    )
    total = jnp.sum(slopes[:, None] * covered, axis=2)
    return (anchor[:, 1].astype(jnp.float32)[:, None, :] + total).astype(jnp.bfloat16)


def body(observed, knot_base, knot_steps, block_route, land_mask, terrain):
    day_count, row_count, columns = observed.shape
    ntiles = lax.axis_size("tiles")
    ndays = lax.axis_size("days")
    owned = row_count // 2
    quarter = knot_base.shape[2]
    served = block_route.shape[0]
    tile_ids = jnp.arange(ntiles, dtype=jnp.int32)

    target = block_route // owned
    place_slot = block_route % owned
    match = target[None, :] == tile_ids[:, None]
    has = jnp.any(match, axis=1)
    slot_table = jnp.where(has, jnp.sum(jnp.where(match, place_slot[None, :], 0), axis=1), owned)
    local_of = jnp.sum(jnp.where(match, jnp.arange(served, dtype=jnp.int32)[None, :], 0), axis=1)

    recv_slot = lax.all_to_all(
        slot_table.reshape(ntiles, 1).astype(jnp.int32), "tiles", 0, 0, tiled=True
    ).reshape(ntiles)

    picked = jnp.minimum(recv_slot, owned - 1)
    holder = jnp.sum(
        jnp.where(
            recv_slot[None, :] == jnp.arange(owned, dtype=jnp.int32)[:, None], tile_ids[None, :], 0
        ),
        axis=1,
    )

    local = observed.reshape(day_count, owned, ndays, quarter)
    outgoing = jnp.take(local, picked, axis=1)
    outgoing = outgoing.transpose(1, 2, 0, 3).reshape(ntiles * ndays, day_count, quarter)
    arrived = lax.all_to_all(outgoing, ("tiles", "days"), 0, 0, tiled=True)
    arrived = arrived.reshape(ntiles, ndays * day_count, quarter)
    own_rows = jnp.take(arrived, target, axis=0)

    mapped_part = quantile_map(own_rows, knot_base, knot_steps)

    packed = jnp.take(mapped_part, local_of, axis=0)
    packed = packed.reshape(ntiles * ndays, day_count, quarter)
    returned = lax.all_to_all(packed, ("tiles", "days"), 0, 0, tiled=True)
    returned = returned.reshape(ntiles, ndays, day_count, quarter)
    blocks = jnp.take(returned, holder, axis=0)
    mapped = blocks.transpose(2, 0, 1, 3).reshape(day_count, row_count, columns)

    depth = PASSES
    weights = terrain * land_mask.astype(jnp.float32)
    wide_maps = with_halo(jnp.stack([weights, terrain]), depth)
    wide_weights = wide_maps[0]
    wide_center = center_share * wide_maps[1]
    wide_denom = wide_center + neighbour_sum(jnp.pad(wide_weights, 1))
    wide_denom = jnp.where(wide_denom > 0.0, wide_denom, 1.0)
    wide_field = with_halo(mapped, depth).astype(jnp.float32)
    for sweep in range(PASSES):
        padded = jnp.pad(wide_field * wide_weights[None], ((0, 0), (1, 1), (1, 1)))
        wide_field = (wide_center[None] * wide_field + neighbour_sum(padded)) / wide_denom[None]
    return wide_field[:, depth : depth + row_count, :]


def solution(mesh):
    return jax.shard_map(
        body,
        mesh=mesh,
        in_specs=(
            P("days", "tiles", None),
            P("tiles", None, "days"),
            P("tiles", None, None, "days"),
            P("tiles"),
            P("tiles", None),
            P("tiles", None),
        ),
        out_specs=P("days", "tiles", None),
        check_vma=False,
    )
```

time: 148 us -> 145 us (0.980)
  waiting for transfers between devices: 78.7 us -> 65.9 us
  starting transfers between devices: 41.4 us -> 51.5 us
  other arithmetic: 13.7 us -> 18.1 us
  local copies, waits for them, and re-layouts: 12.9 us -> 8.63 us
    all_to_all x3, waiting for transfers between devices: 75.6 us -> 61.2 us  [the longest x1 27.6 us: body(): arrived = lax.all_to_all(outgoing, ('tiles', 'days'), 0, 0, tiled=True)]
    scatter x4 -> x0, local copies, waits for them, and re-layouts: 7.49 us -> none  [the longest x2 4.67 us: body(): mapped = jnp.zeros((day_count, nblocks, block_cells), jnp.bfloat16).at[:,...]
    ppermute x2 -> x4, starting transfers between devices: 4.82 us -> 12.2 us  [the longest x2 6.7 us: with_halo(): lax.ppermute(tail, 'tiles', [(i, i + 1) for i in range(count - 1)])]
    all_to_all x0 -> x1, other arithmetic: none -> 4.67 us  [body(): lax.all_to_all(slot_table.reshape(ntiles, 1).astype(jnp.int32), 'tiles',...]
    min x1, other arithmetic: 4.67 us -> 0.06 us  [quantile_map(): jnp.clip(values.astype(jnp.float32)[:, :, None, :] - position[:, None], 0...]
    select_n x3 -> x9, other arithmetic: 0.68 us -> 4.61 us  [the longest x2 2.61 us: body(): packed = jnp.take(mapped_part, local_of, axis=0)]
    gather x2 -> x4, local copies, waits for them, and re-layouts: 1.22 us -> 3.89 us  [the longest x1 1.8 us: body(): own_rows = jnp.take(arrived, target, axis=0)]
    all_to_all x3, starting transfers between devices: 36.6 us -> 39.3 us  [the longest x1 18.4 us: body(): lax.all_to_all(slot_table.reshape(ntiles, 1).astype(jnp.int32), 'tiles',...]
  transfers between devices with their start and end apart: 5 -> 7, of which waited for: 4 -> 5; matrix products, arithmetic and copies ran while one was open for 1% -> 3% of each run, Pallas kernels for 0% -> 0%
where the time goes in v1:
time: 145 us; the launch traced here: 144 us
  waiting for transfers between devices  65.9 us (45%)
  starting transfers between devices  51.5 us (36%)
  other arithmetic  18.1 us (12%)
  local copies, waits for them, and re-layouts  8.63 us (6%)
    all_to_all x1, waiting for transfers between devices, body(): arrived = lax.all_to_all(outgoing, ('tiles', 'days'), 0, 0, tiled=True)  27.6 us
    all_to_all x1, waiting for transfers between devices, body(): returned = lax.all_to_all(packed, ('tiles', 'days'), 0, 0, tiled=True)  23.2 us
    all_to_all x1, starting transfers between devices, body(): lax.all_to_all(slot_table.reshape(ntiles, 1).astype(jnp.int32), 'tiles',...  18.4 us
    all_to_all x1, starting transfers between devices, body(): arrived = lax.all_to_all(outgoing, ('tiles', 'days'), 0, 0, tiled=True)  11.6 us
    all_to_all x1, waiting for transfers between devices, body(): lax.all_to_all(slot_table.reshape(ntiles, 1).astype(jnp.int32), 'tiles',...  10.4 us
    all_to_all x1, starting transfers between devices, body(): returned = lax.all_to_all(packed, ('tiles', 'days'), 0, 0, tiled=True)  9.29 us
    ppermute x2, starting transfers between devices, with_halo(): lax.ppermute(tail, 'tiles', [(i, i + 1) for i in range(count - 1)])  6.7 us
    ppermute x2, starting transfers between devices, with_halo(): lax.ppermute(head, 'tiles', [(i + 1, i) for i in range(count - 1)])  5.49 us
  transfers between devices with their start and end apart: 7, of which 5 were waited for; matrix products, arithmetic and copies ran while one was open for 3% of the time, Pallas kernels for 0%

profile of v1, /device:TPU:1, one launch (start us, length us, event | category | flops | bytes accessed | tf_op | source)
XLA Modules:
  0.0 144.5 jit_solution(11020177579001124288)
XLA Ops:
  0.0 0.7 compare_and_fusion.1
  0.7 0.7 and_select_fusion
  1.3 0.1 fusion.26
  1.4 0.1 select_reduce_fusion
  1.5 0.7 copy.46
  2.3 18.4 %all-to-all-start = ((s32[128,1,1]{2,1,0:T(1,128)}), s32[128,1,1]{2,1,0:T(1,128)S(1)}, u32[]{:S(2)}, u32[]{:S(2)}) async-start(s32[128,1,1]{2,1,0:T(1,128)} %copy.46), calls=%async_computation | async-start | bytes 131072 | tf_op jit(solution)/shard_map/all_to_all | solution.py:58
  20.7 0.9 reshape.122
  21.6 0.1 copy.51
  21.7 10.4 %all-to-all-done = s32[128,1,1]{2,1,0:T(1,128)S(1)} async-done(((s32[128,1,1]{2,1,0:T(1,128)}), s32[128,1,1]{2,1,0:T(1,128)S(1)}, u32[]{:S(2)}, u32[]{:S(2)}) %all-to-all-start) | async-done | bytes 544 | tf_op jit(solution)/shard_map/all_to_all | solution.py:58
  32.1 4.7 %fusion.33 = (s32[128]{0:T(128)S(1)}, s32[128]{0:T(128)S(1)}) fusion(s32[128,1,1]{2,1,0:T(1,128)S(1)} %all-to-all-done), kind=kLoop, calls=%fused_computation.110 | loop fusion | flops 128 | bytes 1536 | tf_op jit(solution)/shard_map/all_to_all | solution.py:58
  36.9 0.8 gather_fusion
  37.6 1.2 broadcast_select_fusion
  38.9 0.0 copy-start
  38.9 11.6 %all-to-all-start.1 = ((bf16[512,8,128]{2,1,0:T(8,128)(2,1)}), bf16[512,8,128]{2,1,0:T(8,128)(2,1)}, u32[]{:S(2)}, u32[]{:S(2)}) async-start(bf16[512,8,128]{2,1,0:T(8,128)(2,1)} %bitcast.9), calls=%async_computation.1 | async-start | bytes 2097152 | tf_op jit(solution)/shard_map/all_to_all | solution.py:73
  50.4 0.0 copy-done
  50.4 1.1 fusion.37
  51.6 0.2 fusion.2
  51.8 0.0 copy-start.3
  51.8 0.3 copy.49
  52.1 0.4 copy-done.3
  52.5 0.1 fusion.3
  52.6 0.3 copy.52
  52.9 0.1 convert_bitcast_fusion
  53.0 0.3 copy.50
  53.3 0.1 broadcast_in_dim.112
  53.3 0.1 broadcast_in_dim.113
  53.5 27.6 %all-to-all-done.1 = bf16[512,8,128]{2,1,0:T(8,128)(2,1)} async-done(((bf16[512,8,128]{2,1,0:T(8,128)(2,1)}), bf16[512,8,128]{2,1,0:T(8,128)(2,1)}, u32[]{:S(2)}, u32[]{:S(2)}) %all-to-all-start.1) | async-done | bytes 1048608 | tf_op jit(solution)/shard_map/all_to_all | solution.py:73
  81.1 1.8 %gather_fusion.1 = bf16[16,32,128]{2,1,0:T(8,128)(2,1)S(1)} fusion(bf16[128,32,128]{2,1,0:T(8,128)(2,1)} %bitcast.10, s32[1024]{0:T(1024)S(1)} %pad_clamp_fusion.2), kind=kCustom, calls=%fused_computation.1 | custom fusion | bytes 262208 | tf_op jit(solution)/shard_map/jit(_take)/gather | solution.py:75
  82.9 0.1 select_convert_fusion
  83.0 5.4 %multiply_reduce_fusion = f32[16,32,128]{2,1,0:T(8,128)S(1)} fusion(f32[16,99,128]{2,1,0:T(8,128)S(1)} %copy.52, f32[16,32,128]{2,1,0:T(8,128)S(1)} %select_convert_fusion, f32[16,99,128]{2,1,0:T(8,128)S(1)} %copy.50, f32[16,99,128]{2,1,0:T(8,128)S(1)} %copy.49), kind=kLoop, calls=%fused_computation.4 | loop fusion | flops 32374784 | bytes 2957312 | tf_op jit(solution)/shard_map/reduce_sum | solution.py:38
  88.4 0.8 gather_fusion.2
  89.2 2.6 %broadcast_select_fusion.1 = bf16[512,8,128]{2,1,0:T(8,128)(2,1)} fusion(bf16[512,8,128]{2,1,0:T(8,128)(2,1)S(1)} %bitcast.39, pred[512]{0:T(512)(128)(4,1)S(1)} %broadcast_in_dim.113), kind=kLoop, calls=%fused_computation.11 | loop fusion | flops 524288 | bytes 2097664 | tf_op jit(solution)/shard_map/jit(_take)/select_n | solution.py:79
  91.8 0.0 copy-start.1
  91.8 0.0 copy-start.2
  91.8 9.3 %all-to-all-start.2 = ((bf16[512,8,128]{2,1,0:T(8,128)(2,1)}), bf16[512,8,128]{2,1,0:T(8,128)(2,1)S(1)}, u32[]{:S(2)}, u32[]{:S(2)}) async-start(bf16[512,8,128]{2,1,0:T(8,128)(2,1)} %broadcast_select_fusion.1), calls=%async_computation.2 | async-start | bytes 2097152 | tf_op jit(solution)/shard_map/all_to_all | solution.py:81
  101.1 0.0 copy-done.1
  101.1 0.0 copy-done.2
  101.2 3.9 %collective-permute-start = (f32[2,4,256]{2,1,0:T(4,128)S(1)}, f32[2,4,256]{2,1,0:T(4,128)S(1)}, u32[]{:S(2)}, u32[]{:S(2)}) collective-permute-start(f32[2,4,256]{2,1,0:T(4,128)S(1)} %get-tuple-element.27), channel_id=1, source_target_pairs={{0,4},{4,8},{8,12},{12,16},{16,20},{20,24},{24,28},{28,32},{32,36}... | collective-permute-start | bytes 24584 | tf_op jit(solution)/shard_map/ppermute | solution.py:25
  105.1 3.6 %collective-permute-start.1 = (f32[2,4,256]{2,1,0:T(4,128)S(1)}, f32[2,4,256]{2,1,0:T(4,128)S(1)}, u32[]{:S(2)}, u32[]{:S(2)}) collective-permute-start(f32[2,4,256]{2,1,0:T(4,128)S(1)} %get-tuple-element.28), channel_id=1, source_target_pairs={{4,0},{8,4},{12,8},{16,12},{20,16},{24,20},{28,24},{32,28},{36,32}... | collective-permute-start | bytes 24584 | tf_op jit(solution)/shard_map/ppermute | solution.py:26
  108.7 0.1 select_reduce_fusion.1
  108.8 0.0 collective-permute-done
  108.8 1.7 %collective-permute-done.1 = f32[2,4,256]{2,1,0:T(4,128)S(1)} collective-permute-done((f32[2,4,256]{2,1,0:T(4,128)S(1)}, f32[2,4,256]{2,1,0:T(4,128)S(1)}, u32[]{:S(2)}, u32[]{:S(2)}) %collective-permute-start.1) | collective-permute-done | bytes 8224 | tf_op jit(solution)/shard_map/ppermute | solution.py:26
  110.6 23.2 %all-to-all-done.2 = bf16[512,8,128]{2,1,0:T(8,128)(2,1)S(1)} async-done(((bf16[512,8,128]{2,1,0:T(8,128)(2,1)}), bf16[512,8,128]{2,1,0:T(8,128)(2,1)S(1)}, u32[]{:S(2)}, u32[]{:S(2)}) %all-to-all-start.2) | async-done | bytes 1048608 | tf_op jit(solution)/shard_map/all_to_all | solution.py:81
  133.8 0.6 gather_fusion.3
  134.4 0.1 select_bitcast_fusion
  134.5 0.1 copy.53
  134.5 0.1 reshape.126
  134.6 2.8 %collective-permute-start.2 = (bf16[8,4,256]{2,1,0:T(4,128)(2,1)S(1)}, bf16[8,4,256]{2,1,0:T(4,128)(2,1)S(1)}, u32[]{:S(2)}, u32[]{:S(2)}) collective-permute-start(bf16[8,4,256]{2,1,0:T(4,128)(2,1)S(1)} %get-tuple-element.23), channel_id=1, source_target_pairs={{0,4},{4,8},{8,12},{12,16},{16,20},{20,24},{24,28},{28,32},{32,36}... | collective-permute-start | bytes 49160 | tf_op jit(solution)/shard_map/ppermute | solution.py:25
  137.4 1.9 %collective-permute-start.3 = (bf16[8,4,256]{2,1,0:T(4,128)(2,1)S(1)}, bf16[8,4,256]{2,1,0:T(4,128)(2,1)S(1)}, u32[]{:S(2)}, u32[]{:S(2)}) collective-permute-start(bf16[8,4,256]{2,1,0:T(4,128)(2,1)S(1)} %get-tuple-element.24), channel_id=1, source_target_pairs={{4,0},{8,4},{12,8},{16,12},{20,16},{24,20},{28,24},{32,28},{36,32}... | collective-permute-start | bytes 49160 | tf_op jit(solution)/shard_map/ppermute | solution.py:26
  139.3 0.1 compare_select_fusion
  139.5 0.0 collective-permute-done.2
  139.5 3.0 %collective-permute-done.3 = bf16[8,4,256]{2,1,0:T(4,128)(2,1)S(1)} collective-permute-done((bf16[8,4,256]{2,1,0:T(4,128)(2,1)S(1)}, bf16[8,4,256]{2,1,0:T(4,128)(2,1)S(1)}, u32[]{:S(2)}, u32[]{:S(2)}) %collective-permute-start.3) | collective-permute-done | bytes 16416 | tf_op jit(solution)/shard_map/ppermute | solution.py:26
  142.5 0.1 convert_multiply_fusion
  142.5 0.3 broadcast_multiply_fusion.2
  142.9 0.3 broadcast_multiply_fusion.1
  143.1 0.3 broadcast_multiply_fusion
  143.4 0.2 pad_slice_fusion.3
  143.6 0.9 fusion.20
  (21 shorter events, 0.2 us)
Async XLA Ops:
  2.3 29.9 %all-to-all-start = ((s32[128,1,1]{2,1,0:T(1,128)}), s32[128,1,1]{2,1,0:T(1,128)S(1)}, u32[]{:S(2)}, u32[]{:S(2)}) async-start(s32[128,1,1]{2,1,0:T(1,128)} %copy.46), calls=%async_computation | async-start | bytes 131072 | tf_op jit(solution)/shard_map/all_to_all | solution.py:58
  38.9 11.6 %copy-start = (bf16[16,2,99,128]{3,1,2,0:T(2,128)(2,1)S(1)}, bf16[16,2,99,128]{3,1,2,0:T(2,128)(2,1)}, u32[]{:S(2)}) copy-start(bf16[16,2,99,128]{3,1,2,0:T(2,128)(2,1)} %param.8) | copy-start | bytes 2433028
  38.9 42.3 %all-to-all-start.1 = ((bf16[512,8,128]{2,1,0:T(8,128)(2,1)}), bf16[512,8,128]{2,1,0:T(8,128)(2,1)}, u32[]{:S(2)}, u32[]{:S(2)}) async-start(bf16[512,8,128]{2,1,0:T(8,128)(2,1)} %bitcast.9), calls=%async_computation.1 | async-start | bytes 2097152 | tf_op jit(solution)/shard_map/all_to_all | solution.py:73
  51.8 0.7 copy-start.3
  91.8 9.3 %copy-start.1 = (f32[32,256]{1,0:T(8,128)S(1)}, f32[32,256]{1,0:T(8,128)}, u32[]{:S(2)}) copy-start(f32[32,256]{1,0:T(8,128)} %param.11) | copy-start | bytes 98308
  91.8 9.3 %copy-start.2 = (s32[32,256]{1,0:T(8,128)S(1)}, s32[32,256]{1,0:T(8,128)}, u32[]{:S(2)}) copy-start(s32[32,256]{1,0:T(8,128)} %param.10) | copy-start | bytes 98308
  91.8 42.0 %all-to-all-start.2 = ((bf16[512,8,128]{2,1,0:T(8,128)(2,1)}), bf16[512,8,128]{2,1,0:T(8,128)(2,1)S(1)}, u32[]{:S(2)}, u32[]{:S(2)}) async-start(bf16[512,8,128]{2,1,0:T(8,128)(2,1)} %broadcast_select_fusion.1), calls=%async_computation.2 | async-start | bytes 2097152 | tf_op jit(solution)/shard_map/all_to_all | solution.py:81
  101.2 7.7 %collective-permute-start = (f32[2,4,256]{2,1,0:T(4,128)S(1)}, f32[2,4,256]{2,1,0:T(4,128)S(1)}, u32[]{:S(2)}, u32[]{:S(2)}) collective-permute-start(f32[2,4,256]{2,1,0:T(4,128)S(1)} %get-tuple-element.27), channel_id=1, source_target_pairs={{0,4},{4,8},{8,12},{12,16},{16,20},{20,24},{24,28},{28,32},{32,36}... | collective-permute-start | bytes 24584 | tf_op jit(solution)/shard_map/ppermute | solution.py:25
  105.1 5.5 %collective-permute-start.1 = (f32[2,4,256]{2,1,0:T(4,128)S(1)}, f32[2,4,256]{2,1,0:T(4,128)S(1)}, u32[]{:S(2)}, u32[]{:S(2)}) collective-permute-start(f32[2,4,256]{2,1,0:T(4,128)S(1)} %get-tuple-element.28), channel_id=1, source_target_pairs={{4,0},{8,4},{12,8},{16,12},{20,16},{24,20},{28,24},{32,28},{36,32}... | collective-permute-start | bytes 24584 | tf_op jit(solution)/shard_map/ppermute | solution.py:26
  134.6 4.8 %collective-permute-start.2 = (bf16[8,4,256]{2,1,0:T(4,128)(2,1)S(1)}, bf16[8,4,256]{2,1,0:T(4,128)(2,1)S(1)}, u32[]{:S(2)}, u32[]{:S(2)}) collective-permute-start(bf16[8,4,256]{2,1,0:T(4,128)(2,1)S(1)} %get-tuple-element.23), channel_id=1, source_target_pairs={{0,4},{4,8},{8,12},{12,16},{16,20},{20,24},{24,28},{28,32},{32,36}... | collective-permute-start | bytes 49160 | tf_op jit(solution)/shard_map/ppermute | solution.py:25
  137.4 5.1 %collective-permute-start.3 = (bf16[8,4,256]{2,1,0:T(4,128)(2,1)S(1)}, bf16[8,4,256]{2,1,0:T(4,128)(2,1)S(1)}, u32[]{:S(2)}, u32[]{:S(2)}) collective-permute-start(bf16[8,4,256]{2,1,0:T(4,128)(2,1)S(1)} %get-tuple-element.24), channel_id=1, source_target_pairs={{4,0},{8,4},{12,8},{16,12},{20,16},{24,20},{28,24},{32,28},{36,32}... | collective-permute-start | bytes 49160 | tf_op jit(solution)/shard_map/ppermute | solution.py:26

commit v2 on v1

--- a/solution.py
+++ b/solution.py
@@ -55,32 +55,32 @@
     slot_table = jnp.where(has, jnp.sum(jnp.where(match, place_slot[None, :], 0), axis=1), owned)
     local_of = jnp.sum(jnp.where(match, jnp.arange(served, dtype=jnp.int32)[None, :], 0), axis=1)
 
-    recv_slot = lax.all_to_all(
-        slot_table.reshape(ntiles, 1).astype(jnp.int32), "tiles", 0, 0, tiled=True
-    ).reshape(ntiles)
+    lanes = 128
+    recv_rows = lax.all_to_all(
+        jnp.broadcast_to(slot_table.astype(jnp.int32)[:, None], (ntiles, lanes)),
+        "tiles", 0, 0, tiled=True,
+    )
 
-    picked = jnp.minimum(recv_slot, owned - 1)
+    picked = jnp.minimum(recv_rows[:, 0], owned - 1)
+    slot_ids = jnp.arange(owned, dtype=jnp.int32)
     holder = jnp.sum(
-        jnp.where(
-            recv_slot[None, :] == jnp.arange(owned, dtype=jnp.int32)[:, None], tile_ids[None, :], 0
-        ),
-        axis=1,
+        jnp.where(recv_rows[:, :owned] == slot_ids[None, :], tile_ids[:, None], 0), axis=0
     )
 
     local = observed.reshape(day_count, owned, ndays, quarter)
-    outgoing = jnp.take(local, picked, axis=1)
+    outgoing = jnp.take(local, picked, axis=1, mode="clip")
     outgoing = outgoing.transpose(1, 2, 0, 3).reshape(ntiles * ndays, day_count, quarter)
     arrived = lax.all_to_all(outgoing, ("tiles", "days"), 0, 0, tiled=True)
     arrived = arrived.reshape(ntiles, ndays * day_count, quarter)
-    own_rows = jnp.take(arrived, target, axis=0)
+    own_rows = jnp.take(arrived, target, axis=0, mode="clip")
 
     mapped_part = quantile_map(own_rows, knot_base, knot_steps)
 
-    packed = jnp.take(mapped_part, local_of, axis=0)
+    packed = jnp.take(mapped_part, local_of, axis=0, mode="clip")
     packed = packed.reshape(ntiles * ndays, day_count, quarter)
     returned = lax.all_to_all(packed, ("tiles", "days"), 0, 0, tiled=True)
     returned = returned.reshape(ntiles, ndays, day_count, quarter)
-    blocks = jnp.take(returned, holder, axis=0)
+    blocks = jnp.take(returned, holder, axis=0, mode="clip")
     mapped = blocks.transpose(2, 0, 1, 3).reshape(day_count, row_count, columns)
 
     depth = PASSES

time: 145 us -> 138 us (0.952)
  other arithmetic: 18.1 us -> 8.74 us
  local copies, waits for them, and re-layouts: 8.63 us -> 10.4 us
    all_to_all x1 -> x0, other arithmetic: 4.67 us -> none  [body(): lax.all_to_all(slot_table.reshape(ntiles, 1).astype(jnp.int32), 'tiles',...]
    select_n x7 -> x0, other arithmetic: 3.94 us -> none  [the longest x2 2.61 us: body(): packed = jnp.take(mapped_part, local_of, axis=0)]
    gather x4, local copies, waits for them, and re-layouts: 3.89 us -> 5.74 us  [the longest x1 1.8 us: body(): own_rows = jnp.take(arrived, target, axis=0, mode='clip')]
where the time goes in v2:
time: 138 us; the launch traced here: 137 us
  waiting for transfers between devices  66.3 us (48%)
  starting transfers between devices  51.5 us (37%)
  local copies, waits for them, and re-layouts  10.4 us (8%)
  other arithmetic  8.74 us (6%)
    all_to_all x1, waiting for transfers between devices, body(): arrived = lax.all_to_all(outgoing, ('tiles', 'days'), 0, 0, tiled=True)  27.9 us
    all_to_all x1, waiting for transfers between devices, body(): returned = lax.all_to_all(packed, ('tiles', 'days'), 0, 0, tiled=True)  23.1 us
    all_to_all x1, starting transfers between devices, body(): lax.all_to_all(jnp.broadcast_to(slot_table.astype(jnp.int32)[:, None], (n...  18.4 us
    all_to_all x1, starting transfers between devices, body(): arrived = lax.all_to_all(outgoing, ('tiles', 'days'), 0, 0, tiled=True)  11.6 us
    all_to_all x1, waiting for transfers between devices, body(): lax.all_to_all(jnp.broadcast_to(slot_table.astype(jnp.int32)[:, None], (n...  10.4 us
    all_to_all x1, starting transfers between devices, body(): returned = lax.all_to_all(packed, ('tiles', 'days'), 0, 0, tiled=True)  9.29 us
    ppermute x2, starting transfers between devices, with_halo(): lax.ppermute(tail, 'tiles', [(i, i + 1) for i in range(count - 1)])  6.7 us
    ppermute x2, starting transfers between devices, with_halo(): lax.ppermute(head, 'tiles', [(i + 1, i) for i in range(count - 1)])  5.49 us
  transfers between devices with their start and end apart: 7, of which 5 were waited for; matrix products, arithmetic and copies ran while one was open for 3% of the time, Pallas kernels for 0%

profile of v2, /device:TPU:1, one launch (start us, length us, event | category | flops | bytes accessed | tf_op | source)
XLA Modules:
  0.0 137.2 jit_solution(613924163239725847)
XLA Ops:
  0.0 0.7 and_select_fusion
  0.7 0.1 fusion.22
  0.8 0.1 select_reduce_fusion.1
  0.9 0.8 broadcast_in_dim.78
  1.7 18.4 %all-to-all-start = ((s32[128,1,128]{2,1,0:T(1,128)}), s32[128,1,128]{2,1,0:T(1,128)S(1)}, u32[]{:S(2)}, u32[]{:S(2)}) async-start(s32[128,1,128]{2,1,0:T(1,128)} %broadcast_in_dim.78), calls=%async_computation | async-start | bytes 131072 | tf_op jit(solution)/shard_map/all_to_all | solution.py:59
  20.2 0.9 reshape.45
  21.1 0.1 copy.48
  21.2 10.4 %all-to-all-done = s32[128,1,128]{2,1,0:T(1,128)S(1)} async-done(((s32[128,1,128]{2,1,0:T(1,128)}), s32[128,1,128]{2,1,0:T(1,128)S(1)}, u32[]{:S(2)}, u32[]{:S(2)}) %all-to-all-start) | async-done | bytes 65568 | tf_op jit(solution)/shard_map/all_to_all | solution.py:59
  31.6 0.1 fusion.21
  31.7 1.7 %gather_fusion = bf16[128,8,4,128]{3,1,2,0:T(8,128)(2,1)} fusion(bf16[8,16,4,128]{3,0,2,1:T(8,128)(2,1)S(1)} %copy.48, s32[1024]{0:T(1024)S(1)} %pad_clamp_fusion.3), kind=kCustom, calls=%fused_computation | custom fusion | bytes 2097664 | tf_op jit(solution)/shard_map/jit(_take)/gather | solution.py:71
  33.5 0.0 copy-start
  33.5 11.6 %all-to-all-start.1 = ((bf16[512,8,128]{2,1,0:T(8,128)(2,1)}), bf16[512,8,128]{2,1,0:T(8,128)(2,1)}, u32[]{:S(2)}, u32[]{:S(2)}) async-start(bf16[512,8,128]{2,1,0:T(8,128)(2,1)} %bitcast.8), calls=%async_computation.1 | async-start | bytes 2097152 | tf_op jit(solution)/shard_map/all_to_all | solution.py:73
  45.1 0.0 copy-done
  45.1 1.1 fusion.34
  46.2 0.2 fusion.2
  46.4 0.0 copy-start.3
  46.4 0.3 copy.46
  46.7 0.4 copy-done.3
  47.1 0.1 fusion.3
  47.3 0.3 copy.49
  47.5 0.1 convert_bitcast_fusion
  47.6 0.3 copy.47
  47.9 27.9 %all-to-all-done.1 = bf16[512,8,128]{2,1,0:T(8,128)(2,1)} async-done(((bf16[512,8,128]{2,1,0:T(8,128)(2,1)}), bf16[512,8,128]{2,1,0:T(8,128)(2,1)}, u32[]{:S(2)}, u32[]{:S(2)}) %all-to-all-start.1) | async-done | bytes 1048608 | tf_op jit(solution)/shard_map/all_to_all | solution.py:73
  75.7 1.8 %gather_fusion.1 = bf16[16,32,128]{2,1,0:T(8,128)(2,1)S(1)} fusion(bf16[128,32,128]{2,1,0:T(8,128)(2,1)} %bitcast.9, s32[1024]{0:T(1024)S(1)} %pad_clamp_fusion.2), kind=kCustom, calls=%fused_computation.1 | custom fusion | bytes 262208 | tf_op jit(solution)/shard_map/jit(_take)/gather | solution.py:75
  77.6 5.4 %multiply_reduce_fusion = f32[16,32,128]{2,1,0:T(8,128)S(1)} fusion(f32[16,99,128]{2,1,0:T(8,128)S(1)} %copy.49, f32[16,32,128]{2,1,0:T(8,128)S(1)} %convert_element_type.40, f32[16,99,128]{2,1,0:T(8,128)S(1)} %copy.47, f32[16,99,128]{2,1,0:T(8,128)S(1)} %copy.46), kind=kLoop, calls=%fused_computation.4 | loop fusion | flops 32374784 | bytes 2957312 | tf_op jit(solution)/shard_map/reduce_sum | solution.py:38
  83.0 1.7 %gather_fusion.2 = bf16[128,32,128]{2,1,0:T(8,128)(2,1)} fusion(bf16[16,32,128]{2,1,0:T(8,128)(2,1)S(1)} %add_convert_fusion, s32[1024]{0:T(1024)S(1)} %pad_clamp_fusion.1), kind=kCustom, calls=%fused_computation.2 | custom fusion | bytes 2097664 | tf_op jit(solution)/shard_map/jit(_take)/gather | solution.py:79
  84.6 0.0 copy-start.1
  84.6 0.0 copy-start.2
  84.6 9.3 %all-to-all-start.2 = ((bf16[512,8,128]{2,1,0:T(8,128)(2,1)}), bf16[512,8,128]{2,1,0:T(8,128)(2,1)S(1)}, u32[]{:S(2)}, u32[]{:S(2)}) async-start(bf16[512,8,128]{2,1,0:T(8,128)(2,1)} %bitcast.12), calls=%async_computation.2 | async-start | bytes 2097152 | tf_op jit(solution)/shard_map/all_to_all | solution.py:81
  93.9 0.0 copy-done.1
  94.0 0.0 copy-done.2
  94.0 3.9 %collective-permute-start = (f32[2,4,256]{2,1,0:T(4,128)S(1)}, f32[2,4,256]{2,1,0:T(4,128)S(1)}, u32[]{:S(2)}, u32[]{:S(2)}) collective-permute-start(f32[2,4,256]{2,1,0:T(4,128)S(1)} %get-tuple-element.23), channel_id=1, source_target_pairs={{0,4},{4,8},{8,12},{12,16},{16,20},{20,24},{24,28},{28,32},{32,36}... | collective-permute-start | bytes 24584 | tf_op jit(solution)/shard_map/ppermute | solution.py:25
  97.9 3.6 %collective-permute-start.1 = (f32[2,4,256]{2,1,0:T(4,128)S(1)}, f32[2,4,256]{2,1,0:T(4,128)S(1)}, u32[]{:S(2)}, u32[]{:S(2)}) collective-permute-start(f32[2,4,256]{2,1,0:T(4,128)S(1)} %get-tuple-element.24), channel_id=1, source_target_pairs={{4,0},{8,4},{12,8},{16,12},{20,16},{24,20},{28,24},{32,28},{36,32}... | collective-permute-start | bytes 24584 | tf_op jit(solution)/shard_map/ppermute | solution.py:26
  101.5 0.0 collective-permute-done
  101.5 1.9 %collective-permute-done.1 = f32[2,4,256]{2,1,0:T(4,128)S(1)} collective-permute-done((f32[2,4,256]{2,1,0:T(4,128)S(1)}, f32[2,4,256]{2,1,0:T(4,128)S(1)}, u32[]{:S(2)}, u32[]{:S(2)}) %collective-permute-start.1) | collective-permute-done | bytes 8224 | tf_op jit(solution)/shard_map/ppermute | solution.py:26
  103.5 23.1 %all-to-all-done.2 = bf16[512,8,128]{2,1,0:T(8,128)(2,1)S(1)} async-done(((bf16[512,8,128]{2,1,0:T(8,128)(2,1)}), bf16[512,8,128]{2,1,0:T(8,128)(2,1)S(1)}, u32[]{:S(2)}, u32[]{:S(2)}) %all-to-all-start.2) | async-done | bytes 1048608 | tf_op jit(solution)/shard_map/all_to_all | solution.py:81
  126.6 0.6 gather_fusion.3
  127.2 0.1 copy.50
  127.3 0.1 reshape.50
  127.4 2.8 %collective-permute-start.2 = (bf16[8,4,256]{2,1,0:T(4,128)(2,1)S(1)}, bf16[8,4,256]{2,1,0:T(4,128)(2,1)S(1)}, u32[]{:S(2)}, u32[]{:S(2)}) collective-permute-start(bf16[8,4,256]{2,1,0:T(4,128)(2,1)S(1)} %get-tuple-element.19), channel_id=1, source_target_pairs={{0,4},{4,8},{8,12},{12,16},{16,20},{20,24},{24,28},{28,32},{32,36}... | collective-permute-start | bytes 49160 | tf_op jit(solution)/shard_map/ppermute | solution.py:25
  130.2 1.9 %collective-permute-start.3 = (bf16[8,4,256]{2,1,0:T(4,128)(2,1)S(1)}, bf16[8,4,256]{2,1,0:T(4,128)(2,1)S(1)}, u32[]{:S(2)}, u32[]{:S(2)}) collective-permute-start(bf16[8,4,256]{2,1,0:T(4,128)(2,1)S(1)} %get-tuple-element.20), channel_id=1, source_target_pairs={{4,0},{8,4},{12,8},{16,12},{20,16},{24,20},{28,24},{32,28},{36,32}... | collective-permute-start | bytes 49160 | tf_op jit(solution)/shard_map/ppermute | solution.py:26
  132.1 0.1 compare_select_fusion
  132.2 0.0 collective-permute-done.2
  132.2 3.0 %collective-permute-done.3 = bf16[8,4,256]{2,1,0:T(4,128)(2,1)S(1)} collective-permute-done((bf16[8,4,256]{2,1,0:T(4,128)(2,1)S(1)}, bf16[8,4,256]{2,1,0:T(4,128)(2,1)S(1)}, u32[]{:S(2)}, u32[]{:S(2)}) %collective-permute-start.3) | collective-permute-done | bytes 16416 | tf_op jit(solution)/shard_map/ppermute | solution.py:26
  135.2 0.1 convert_multiply_fusion
  135.3 0.3 broadcast_multiply_fusion.2
  135.6 0.3 broadcast_multiply_fusion.1
  135.8 0.3 broadcast_multiply_fusion
  136.1 0.2 pad_slice_fusion.3
  136.3 0.9 fusion.20
  (16 shorter events, 0.2 us)
Async XLA Ops:
  1.7 29.9 %all-to-all-start = ((s32[128,1,128]{2,1,0:T(1,128)}), s32[128,1,128]{2,1,0:T(1,128)S(1)}, u32[]{:S(2)}, u32[]{:S(2)}) async-start(s32[128,1,128]{2,1,0:T(1,128)} %broadcast_in_dim.78), calls=%async_computation | async-start | bytes 131072 | tf_op jit(solution)/shard_map/all_to_all | solution.py:59
  33.5 11.6 %copy-start = (bf16[16,2,99,128]{3,1,2,0:T(2,128)(2,1)S(1)}, bf16[16,2,99,128]{3,1,2,0:T(2,128)(2,1)}, u32[]{:S(2)}) copy-start(bf16[16,2,99,128]{3,1,2,0:T(2,128)(2,1)} %param.8) | copy-start | bytes 2433028
  33.5 42.3 %all-to-all-start.1 = ((bf16[512,8,128]{2,1,0:T(8,128)(2,1)}), bf16[512,8,128]{2,1,0:T(8,128)(2,1)}, u32[]{:S(2)}, u32[]{:S(2)}) async-start(bf16[512,8,128]{2,1,0:T(8,128)(2,1)} %bitcast.8), calls=%async_computation.1 | async-start | bytes 2097152 | tf_op jit(solution)/shard_map/all_to_all | solution.py:73
  46.4 0.7 copy-start.3
  84.6 9.3 %copy-start.1 = (f32[32,256]{1,0:T(8,128)S(1)}, f32[32,256]{1,0:T(8,128)}, u32[]{:S(2)}) copy-start(f32[32,256]{1,0:T(8,128)} %param.11) | copy-start | bytes 98308
  84.6 9.3 %copy-start.2 = (s32[32,256]{1,0:T(8,128)S(1)}, s32[32,256]{1,0:T(8,128)}, u32[]{:S(2)}) copy-start(s32[32,256]{1,0:T(8,128)} %param.10) | copy-start | bytes 98308
  84.6 42.0 %all-to-all-start.2 = ((bf16[512,8,128]{2,1,0:T(8,128)(2,1)}), bf16[512,8,128]{2,1,0:T(8,128)(2,1)S(1)}, u32[]{:S(2)}, u32[]{:S(2)}) async-start(bf16[512,8,128]{2,1,0:T(8,128)(2,1)} %bitcast.12), calls=%async_computation.2 | async-start | bytes 2097152 | tf_op jit(solution)/shard_map/all_to_all | solution.py:81
  94.0 7.5 %collective-permute-start = (f32[2,4,256]{2,1,0:T(4,128)S(1)}, f32[2,4,256]{2,1,0:T(4,128)S(1)}, u32[]{:S(2)}, u32[]{:S(2)}) collective-permute-start(f32[2,4,256]{2,1,0:T(4,128)S(1)} %get-tuple-element.23), channel_id=1, source_target_pairs={{0,4},{4,8},{8,12},{12,16},{16,20},{20,24},{24,28},{28,32},{32,36}... | collective-permute-start | bytes 24584 | tf_op jit(solution)/shard_map/ppermute | solution.py:25
  97.9 5.5 %collective-permute-start.1 = (f32[2,4,256]{2,1,0:T(4,128)S(1)}, f32[2,4,256]{2,1,0:T(4,128)S(1)}, u32[]{:S(2)}, u32[]{:S(2)}) collective-permute-start(f32[2,4,256]{2,1,0:T(4,128)S(1)} %get-tuple-element.24), channel_id=1, source_target_pairs={{4,0},{8,4},{12,8},{16,12},{20,16},{24,20},{28,24},{32,28},{36,32}... | collective-permute-start | bytes 24584 | tf_op jit(solution)/shard_map/ppermute | solution.py:26
  127.4 4.8 %collective-permute-start.2 = (bf16[8,4,256]{2,1,0:T(4,128)(2,1)S(1)}, bf16[8,4,256]{2,1,0:T(4,128)(2,1)S(1)}, u32[]{:S(2)}, u32[]{:S(2)}) collective-permute-start(bf16[8,4,256]{2,1,0:T(4,128)(2,1)S(1)} %get-tuple-element.19), channel_id=1, source_target_pairs={{0,4},{4,8},{8,12},{12,16},{16,20},{20,24},{24,28},{28,32},{32,36}... | collective-permute-start | bytes 49160 | tf_op jit(solution)/shard_map/ppermute | solution.py:25
  130.2 5.1 %collective-permute-start.3 = (bf16[8,4,256]{2,1,0:T(4,128)(2,1)S(1)}, bf16[8,4,256]{2,1,0:T(4,128)(2,1)S(1)}, u32[]{:S(2)}, u32[]{:S(2)}) collective-permute-start(bf16[8,4,256]{2,1,0:T(4,128)(2,1)S(1)} %get-tuple-element.20), channel_id=1, source_target_pairs={{4,0},{8,4},{12,8},{16,12},{20,16},{24,20},{28,24},{32,28},{36,32}... | collective-permute-start | bytes 49160 | tf_op jit(solution)/shard_map/ppermute | solution.py:26

commit v3 on v2

--- a/solution.py
+++ b/solution.py
@@ -18,6 +18,13 @@
     )
 
 
+def smoothed(field, weights, center, denom):
+    for sweep in range(PASSES):
+        padded = jnp.pad(field * weights[None], ((0, 0), (1, 1), (1, 1)))
+        field = (center[None] * field + neighbour_sum(padded)) / denom[None]
+    return field
+
+
 def with_halo(cells, width):
     count = lax.axis_size("tiles")
     head = cells[..., :width, :]
@@ -31,12 +38,14 @@
     step_x = increments[:, 0].astype(jnp.float32)
     step_y = increments[:, 1].astype(jnp.float32)
     position = anchor[:, 0][:, None, :].astype(jnp.float32) + jnp.cumsum(step_x, axis=1) - step_x
+    upper = position + step_x
     slopes = step_y / step_x
-    covered = jnp.clip(
-        values.astype(jnp.float32)[:, :, None, :] - position[:, None], 0.0, step_x[:, None]
+    offset = anchor[:, 1].astype(jnp.float32) - jnp.sum(slopes * position, axis=1)
+    clamped = jnp.minimum(
+        jnp.maximum(values.astype(jnp.float32)[:, :, None, :], position[:, None]), upper[:, None]
     )
-    total = jnp.sum(slopes[:, None] * covered, axis=2)
-    return (anchor[:, 1].astype(jnp.float32)[:, None, :] + total).astype(jnp.bfloat16)
+    total = jnp.sum(slopes[:, None] * clamped, axis=2)
+    return (offset[:, None, :] + total).astype(jnp.bfloat16)
 
 
 def body(observed, knot_base, knot_steps, block_route, land_mask, terrain):
@@ -90,11 +99,24 @@
     wide_center = center_share * wide_maps[1]
     wide_denom = wide_center + neighbour_sum(jnp.pad(wide_weights, 1))
     wide_denom = jnp.where(wide_denom > 0.0, wide_denom, 1.0)
+    own_weights = wide_weights[depth : depth + row_count]
+    own_center = wide_center[depth : depth + row_count]
+    own_denom = wide_denom[depth : depth + row_count]
+    field = mapped.astype(jnp.float32)
+    inner = smoothed(field, own_weights, own_center, own_denom)
     wide_field = with_halo(mapped, depth).astype(jnp.float32)
-    for sweep in range(PASSES):
-        padded = jnp.pad(wide_field * wide_weights[None], ((0, 0), (1, 1), (1, 1)))
-        wide_field = (wide_center[None] * wide_field + neighbour_sum(padded)) / wide_denom[None]
-    return wide_field[:, depth : depth + row_count, :]
+    strip = 3 * depth
+    top = smoothed(
+        wide_field[:, :strip], wide_weights[:strip], wide_center[:strip], wide_denom[:strip]
+    )
+    low = row_count + 2 * depth - strip
+    bottom = smoothed(
+        wide_field[:, low:], wide_weights[low:], wide_center[low:], wide_denom[low:]
+    )
+    return jnp.concatenate(
+        [top[:, depth : 2 * depth], inner[:, depth : row_count - depth], bottom[:, depth : 2 * depth]],
+        axis=1,
+    )
 
 
 def solution(mesh):

time: 138 us -> 137 us (level)
  waiting for transfers between devices: 66.3 us -> 64.7 us
where the time goes in v3:
time: 137 us; the launch traced here: 136 us
  waiting for transfers between devices  64.7 us (47%)
  starting transfers between devices  51.5 us (38%)
  local copies, waits for them, and re-layouts  11 us (8%)
  other arithmetic  8.73 us (6%)
    all_to_all x1, waiting for transfers between devices, body(): arrived = lax.all_to_all(outgoing, ('tiles', 'days'), 0, 0, tiled=True)  27.7 us
    all_to_all x1, waiting for transfers between devices, body(): returned = lax.all_to_all(packed, ('tiles', 'days'), 0, 0, tiled=True)  22.9 us
    all_to_all x1, starting transfers between devices, body(): lax.all_to_all(jnp.broadcast_to(slot_table.astype(jnp.int32)[:, None], (n...  18.4 us
    all_to_all x1, starting transfers between devices, body(): arrived = lax.all_to_all(outgoing, ('tiles', 'days'), 0, 0, tiled=True)  11.6 us
    all_to_all x1, waiting for transfers between devices, body(): lax.all_to_all(jnp.broadcast_to(slot_table.astype(jnp.int32)[:, None], (n...  10.4 us
    all_to_all x1, starting transfers between devices, body(): returned = lax.all_to_all(packed, ('tiles', 'days'), 0, 0, tiled=True)  9.29 us
    ppermute x2, starting transfers between devices, with_halo(): lax.ppermute(tail, 'tiles', [(i, i + 1) for i in range(count - 1)])  6.7 us
    ppermute x2, starting transfers between devices, with_halo(): lax.ppermute(head, 'tiles', [(i + 1, i) for i in range(count - 1)])  5.49 us
  transfers between devices with their start and end apart: 7, of which 5 were waited for; matrix products, arithmetic and copies ran while one was open for 3% of the time, Pallas kernels for 0%

profile of v3, /device:TPU:1, one launch (start us, length us, event | category | flops | bytes accessed | tf_op | source)
XLA Modules:
  0.0 136.4 jit_solution(10617219391007467579)
XLA Ops:
  0.0 0.7 and_select_fusion
  0.7 0.1 fusion.56
  0.8 0.1 select_reduce_fusion.1
  0.9 0.8 broadcast_in_dim.55
  1.7 18.4 %all-to-all-start = ((s32[128,1,128]{2,1,0:T(1,128)}), s32[128,1,128]{2,1,0:T(1,128)S(1)}, u32[]{:S(2)}, u32[]{:S(2)}) async-start(s32[128,1,128]{2,1,0:T(1,128)} %broadcast_in_dim.55), calls=%async_computation | async-start | bytes 131072 | tf_op jit(solution)/shard_map/all_to_all | solution.py:68
  20.2 0.9 reshape.65
  21.1 0.1 copy.47
  21.2 10.4 %all-to-all-done = s32[128,1,128]{2,1,0:T(1,128)S(1)} async-done(((s32[128,1,128]{2,1,0:T(1,128)}), s32[128,1,128]{2,1,0:T(1,128)S(1)}, u32[]{:S(2)}, u32[]{:S(2)}) %all-to-all-start) | async-done | bytes 65568 | tf_op jit(solution)/shard_map/all_to_all | solution.py:68
  31.6 0.1 fusion.55
  31.7 1.7 %gather_fusion = bf16[128,8,4,128]{3,1,2,0:T(8,128)(2,1)} fusion(bf16[8,16,4,128]{3,0,2,1:T(8,128)(2,1)S(1)} %copy.47, s32[1024]{0:T(1024)S(1)} %pad_clamp_fusion.3), kind=kCustom, calls=%fused_computation | custom fusion | bytes 2097664 | tf_op jit(solution)/shard_map/jit(_take)/gather | solution.py:80
  33.4 0.0 copy-start
  33.5 11.6 %all-to-all-start.1 = ((bf16[512,8,128]{2,1,0:T(8,128)(2,1)}), bf16[512,8,128]{2,1,0:T(8,128)(2,1)}, u32[]{:S(2)}, u32[]{:S(2)}) async-start(bf16[512,8,128]{2,1,0:T(8,128)(2,1)} %bitcast.11), calls=%async_computation.1 | async-start | bytes 2097152 | tf_op jit(solution)/shard_map/all_to_all | solution.py:82
  45.1 0.0 copy-done
  45.1 1.1 fusion.76
  46.2 0.2 fusion.4
  46.4 0.0 copy-start.4
  46.4 0.3 copy.46
  46.7 0.4 copy-done.4
  47.1 0.2 fusion.6
  47.3 0.1 fusion.7
  47.5 0.3 copy.48
  47.7 0.3 copy.49
  48.1 27.7 %all-to-all-done.1 = bf16[512,8,128]{2,1,0:T(8,128)(2,1)} async-done(((bf16[512,8,128]{2,1,0:T(8,128)(2,1)}), bf16[512,8,128]{2,1,0:T(8,128)(2,1)}, u32[]{:S(2)}, u32[]{:S(2)}) %all-to-all-start.1) | async-done | bytes 1048608 | tf_op jit(solution)/shard_map/all_to_all | solution.py:82
  75.7 1.8 %gather_fusion.1 = bf16[16,32,128]{2,1,0:T(8,128)(2,1)S(1)} fusion(bf16[128,32,128]{2,1,0:T(8,128)(2,1)} %bitcast.12, s32[1024]{0:T(1024)S(1)} %pad_clamp_fusion.2), kind=kCustom, calls=%fused_computation.1 | custom fusion | bytes 262208 | tf_op jit(solution)/shard_map/jit(_take)/gather | solution.py:84
  77.6 4.6 %multiply_reduce_fusion = f32[16,32,128]{2,1,0:T(8,128)S(1)} fusion(f32[16,99,128]{2,1,0:T(8,128)S(1)} %copy.49, f32[16,99,128]{2,1,0:T(8,128)S(1)} %copy.48, f32[16,32,128]{2,1,0:T(8,128)S(1)} %convert_element_type.68, f32[16,99,128]{2,1,0:T(8,128)S(1)} %copy.46), kind=kLoop, calls=%fused_computation.4 | loop fusion | flops 25886720 | bytes 2957312 | tf_op jit(solution)/shard_map/reduce_sum | solution.py:47
  82.2 1.7 %gather_fusion.2 = bf16[128,32,128]{2,1,0:T(8,128)(2,1)} fusion(bf16[16,32,128]{2,1,0:T(8,128)(2,1)S(1)} %add_convert_fusion, s32[1024]{0:T(1024)S(1)} %pad_clamp_fusion.1), kind=kCustom, calls=%fused_computation.2 | custom fusion | bytes 2097664 | tf_op jit(solution)/shard_map/jit(_take)/gather | solution.py:88
  83.9 0.0 copy-start.1
  83.9 0.0 copy-start.3
  83.9 9.3 %all-to-all-start.2 = ((bf16[512,8,128]{2,1,0:T(8,128)(2,1)}), bf16[512,8,128]{2,1,0:T(8,128)(2,1)S(1)}, u32[]{:S(2)}, u32[]{:S(2)}) async-start(bf16[512,8,128]{2,1,0:T(8,128)(2,1)} %bitcast.16), calls=%async_computation.2 | async-start | bytes 2097152 | tf_op jit(solution)/shard_map/all_to_all | solution.py:90
  93.2 0.0 copy-done.1
  93.2 0.0 copy-done.3
  93.2 3.9 %collective-permute-start = (f32[2,4,256]{2,1,0:T(4,128)S(1)}, f32[2,4,256]{2,1,0:T(4,128)S(1)}, u32[]{:S(2)}, u32[]{:S(2)}) collective-permute-start(f32[2,4,256]{2,1,0:T(4,128)S(1)} %get-tuple-element.53), channel_id=1, source_target_pairs={{0,4},{4,8},{8,12},{12,16},{16,20},{20,24},{24,28},{28,32},{32,36}... | collective-permute-start | bytes 24584 | tf_op jit(solution)/shard_map/ppermute | solution.py:32
  97.1 3.6 %collective-permute-start.1 = (f32[2,4,256]{2,1,0:T(4,128)S(1)}, f32[2,4,256]{2,1,0:T(4,128)S(1)}, u32[]{:S(2)}, u32[]{:S(2)}) collective-permute-start(f32[2,4,256]{2,1,0:T(4,128)S(1)} %get-tuple-element.54), channel_id=1, source_target_pairs={{4,0},{8,4},{12,8},{16,12},{20,16},{24,20},{28,24},{32,28},{36,32}... | collective-permute-start | bytes 24584 | tf_op jit(solution)/shard_map/ppermute | solution.py:33
  100.7 0.0 collective-permute-done
  100.7 1.9 %collective-permute-done.1 = f32[2,4,256]{2,1,0:T(4,128)S(1)} collective-permute-done((f32[2,4,256]{2,1,0:T(4,128)S(1)}, f32[2,4,256]{2,1,0:T(4,128)S(1)}, u32[]{:S(2)}, u32[]{:S(2)}) %collective-permute-start.1) | collective-permute-done | bytes 8224 | tf_op jit(solution)/shard_map/ppermute | solution.py:33
  102.6 0.1 compare_select_fusion
  102.7 0.0 copy-start.2
  102.9 22.9 %all-to-all-done.2 = bf16[512,8,128]{2,1,0:T(8,128)(2,1)S(1)} async-done(((bf16[512,8,128]{2,1,0:T(8,128)(2,1)}), bf16[512,8,128]{2,1,0:T(8,128)(2,1)S(1)}, u32[]{:S(2)}, u32[]{:S(2)}) %all-to-all-start.2) | async-done | bytes 1048608 | tf_op jit(solution)/shard_map/all_to_all | solution.py:90
  125.8 0.6 gather_fusion.3
  126.4 0.1 copy.50
  126.5 0.1 reshape.70
  126.6 2.8 %collective-permute-start.2 = (bf16[8,4,256]{2,1,0:T(4,128)(2,1)S(1)}, bf16[8,4,256]{2,1,0:T(4,128)(2,1)S(1)}, u32[]{:S(2)}, u32[]{:S(2)}) collective-permute-start(bf16[8,4,256]{2,1,0:T(4,128)(2,1)S(1)} %get-tuple-element.47), channel_id=1, source_target_pairs={{0,4},{4,8},{8,12},{12,16},{16,20},{20,24},{24,28},{28,32},{32,36}... | collective-permute-start | bytes 49160 | tf_op jit(solution)/shard_map/ppermute | solution.py:32
  129.4 1.9 %collective-permute-start.3 = (bf16[8,4,256]{2,1,0:T(4,128)(2,1)S(1)}, bf16[8,4,256]{2,1,0:T(4,128)(2,1)S(1)}, u32[]{:S(2)}, u32[]{:S(2)}) collective-permute-start(bf16[8,4,256]{2,1,0:T(4,128)(2,1)S(1)} %get-tuple-element.48), channel_id=1, source_target_pairs={{4,0},{8,4},{12,8},{16,12},{20,16},{24,20},{28,24},{32,28},{36,32}... | collective-permute-start | bytes 49160 | tf_op jit(solution)/shard_map/ppermute | solution.py:33
  131.3 0.2 broadcast_multiply_fusion.2
  131.5 0.0 copy-done.2
  131.5 0.2 broadcast_multiply_fusion.1
  131.8 0.0 slice-start
  131.8 0.2 broadcast_multiply_fusion
  132.0 0.2 pad_slice_fusion.3
  132.2 0.3 slice-done
  132.5 0.1 fusion.24
  132.6 0.0 collective-permute-done.2
  132.6 1.8 %collective-permute-done.3 = bf16[8,4,256]{2,1,0:T(4,128)(2,1)S(1)} collective-permute-done((bf16[8,4,256]{2,1,0:T(4,128)(2,1)S(1)}, bf16[8,4,256]{2,1,0:T(4,128)(2,1)S(1)}, u32[]{:S(2)}, u32[]{:S(2)}) %collective-permute-start.3) | collective-permute-done | bytes 16416 | tf_op jit(solution)/shard_map/ppermute | solution.py:33
  134.5 0.2 broadcast_multiply_fusion.8
  134.7 0.1 broadcast_multiply_fusion.7
  134.9 0.1 broadcast_multiply_fusion.4
  135.0 0.2 broadcast_multiply_fusion.3
  135.2 0.1 pad_slice_fusion.19
  135.4 0.1 pad_slice_fusion.35
  135.5 0.1 fusion.62
  135.6 0.7 pad_maximum_fusion
  (27 shorter events, 0.4 us)
Async XLA Ops:
  1.7 29.9 %all-to-all-start = ((s32[128,1,128]{2,1,0:T(1,128)}), s32[128,1,128]{2,1,0:T(1,128)S(1)}, u32[]{:S(2)}, u32[]{:S(2)}) async-start(s32[128,1,128]{2,1,0:T(1,128)} %broadcast_in_dim.55), calls=%async_computation | async-start | bytes 131072 | tf_op jit(solution)/shard_map/all_to_all | solution.py:68
  33.4 11.6 %copy-start = (bf16[16,2,99,128]{3,1,2,0:T(2,128)(2,1)S(1)}, bf16[16,2,99,128]{3,1,2,0:T(2,128)(2,1)}, u32[]{:S(2)}) copy-start(bf16[16,2,99,128]{3,1,2,0:T(2,128)(2,1)} %param.8) | copy-start | bytes 2433028
  33.5 42.3 %all-to-all-start.1 = ((bf16[512,8,128]{2,1,0:T(8,128)(2,1)}), bf16[512,8,128]{2,1,0:T(8,128)(2,1)}, u32[]{:S(2)}, u32[]{:S(2)}) async-start(bf16[512,8,128]{2,1,0:T(8,128)(2,1)} %bitcast.11), calls=%async_computation.1 | async-start | bytes 2097152 | tf_op jit(solution)/shard_map/all_to_all | solution.py:82
  46.4 0.7 copy-start.4
  83.9 9.3 %copy-start.1 = (f32[32,256]{1,0:T(8,128)S(1)}, f32[32,256]{1,0:T(8,128)}, u32[]{:S(2)}) copy-start(f32[32,256]{1,0:T(8,128)} %param.11) | copy-start | bytes 98308
  83.9 9.3 %copy-start.3 = (s32[32,256]{1,0:T(8,128)S(1)}, s32[32,256]{1,0:T(8,128)}, u32[]{:S(2)}) copy-start(s32[32,256]{1,0:T(8,128)} %param.10) | copy-start | bytes 98308
  83.9 42.0 %all-to-all-start.2 = ((bf16[512,8,128]{2,1,0:T(8,128)(2,1)}), bf16[512,8,128]{2,1,0:T(8,128)(2,1)S(1)}, u32[]{:S(2)}, u32[]{:S(2)}) async-start(bf16[512,8,128]{2,1,0:T(8,128)(2,1)} %bitcast.16), calls=%async_computation.2 | async-start | bytes 2097152 | tf_op jit(solution)/shard_map/all_to_all | solution.py:90
  93.2 7.5 %collective-permute-start = (f32[2,4,256]{2,1,0:T(4,128)S(1)}, f32[2,4,256]{2,1,0:T(4,128)S(1)}, u32[]{:S(2)}, u32[]{:S(2)}) collective-permute-start(f32[2,4,256]{2,1,0:T(4,128)S(1)} %get-tuple-element.53), channel_id=1, source_target_pairs={{0,4},{4,8},{8,12},{12,16},{16,20},{20,24},{24,28},{28,32},{32,36}... | collective-permute-start | bytes 24584 | tf_op jit(solution)/shard_map/ppermute | solution.py:32
  97.1 5.5 %collective-permute-start.1 = (f32[2,4,256]{2,1,0:T(4,128)S(1)}, f32[2,4,256]{2,1,0:T(4,128)S(1)}, u32[]{:S(2)}, u32[]{:S(2)}) collective-permute-start(f32[2,4,256]{2,1,0:T(4,128)S(1)} %get-tuple-element.54), channel_id=1, source_target_pairs={{4,0},{8,4},{12,8},{16,12},{20,16},{24,20},{28,24},{32,28},{36,32}... | collective-permute-start | bytes 24584 | tf_op jit(solution)/shard_map/ppermute | solution.py:33
  102.7 28.8 %copy-start.2 = (f32[40,256]{1,0:T(8,128)}, f32[40,256]{1,0:T(8,128)S(1)}, u32[]{:S(2)}) copy-start(f32[40,256]{1,0:T(8,128)S(1)} %compare_select_fusion) | copy-start | bytes 122884
  126.6 6.0 %collective-permute-start.2 = (bf16[8,4,256]{2,1,0:T(4,128)(2,1)S(1)}, bf16[8,4,256]{2,1,0:T(4,128)(2,1)S(1)}, u32[]{:S(2)}, u32[]{:S(2)}) collective-permute-start(bf16[8,4,256]{2,1,0:T(4,128)(2,1)S(1)} %get-tuple-element.47), channel_id=1, source_target_pairs={{0,4},{4,8},{8,12},{12,16},{16,20},{20,24},{24,28},{28,32},{32,36}... | collective-permute-start | bytes 49160 | tf_op jit(solution)/shard_map/ppermute | solution.py:32
  129.4 5.1 %collective-permute-start.3 = (bf16[8,4,256]{2,1,0:T(4,128)(2,1)S(1)}, bf16[8,4,256]{2,1,0:T(4,128)(2,1)S(1)}, u32[]{:S(2)}, u32[]{:S(2)}) collective-permute-start(bf16[8,4,256]{2,1,0:T(4,128)(2,1)S(1)} %get-tuple-element.48), channel_id=1, source_target_pairs={{4,0},{8,4},{12,8},{16,12},{20,16},{24,20},{28,24},{32,28},{36,32}... | collective-permute-start | bytes 49160 | tf_op jit(solution)/shard_map/ppermute | solution.py:33
  131.8 0.7 slice-start

commit v4 on v3

--- a/solution.py
+++ b/solution.py
@@ -23,6 +23,10 @@
         padded = jnp.pad(field * weights[None], ((0, 0), (1, 1), (1, 1)))
         field = (center[None] * field + neighbour_sum(padded)) / denom[None]
     return field
+
+
+def select_rows(pick, rows):
+    return jnp.dot(pick, rows, preferred_element_type=jnp.float32).astype(jnp.bfloat16)
 
 
 def with_halo(cells, width):
@@ -62,7 +66,6 @@
     match = target[None, :] == tile_ids[:, None]
     has = jnp.any(match, axis=1)
     slot_table = jnp.where(has, jnp.sum(jnp.where(match, place_slot[None, :], 0), axis=1), owned)
-    local_of = jnp.sum(jnp.where(match, jnp.arange(served, dtype=jnp.int32)[None, :], 0), axis=1)
 
     lanes = 128
     recv_rows = lax.all_to_all(
@@ -70,22 +73,23 @@
         "tiles", 0, 0, tiled=True,
     )
 
-    picked = jnp.minimum(recv_rows[:, 0], owned - 1)
     slot_ids = jnp.arange(owned, dtype=jnp.int32)
     holder = jnp.sum(
         jnp.where(recv_rows[:, :owned] == slot_ids[None, :], tile_ids[:, None], 0), axis=0
     )
 
-    local = observed.reshape(day_count, owned, ndays, quarter)
-    outgoing = jnp.take(local, picked, axis=1, mode="clip")
-    outgoing = outgoing.transpose(1, 2, 0, 3).reshape(ntiles * ndays, day_count, quarter)
+    send_pick = (recv_rows[:, :owned] == slot_ids[None, :]).astype(jnp.bfloat16)
+    local = observed.reshape(day_count, owned, ndays, quarter).transpose(1, 2, 0, 3)
+    outgoing = select_rows(send_pick, local.reshape(owned, -1))
+    outgoing = outgoing.reshape(ntiles * ndays, day_count, quarter)
     arrived = lax.all_to_all(outgoing, ("tiles", "days"), 0, 0, tiled=True)
-    arrived = arrived.reshape(ntiles, ndays * day_count, quarter)
-    own_rows = jnp.take(arrived, target, axis=0, mode="clip")
+    arrived = arrived.reshape(ntiles, ndays * day_count * quarter)
+    own_pick = match.T.astype(jnp.bfloat16)
+    own_rows = select_rows(own_pick, arrived).reshape(served, ndays * day_count, quarter)
 
     mapped_part = quantile_map(own_rows, knot_base, knot_steps)
 
-    packed = jnp.take(mapped_part, local_of, axis=0, mode="clip")
+    packed = select_rows(match.astype(jnp.bfloat16), mapped_part.reshape(served, -1))
     packed = packed.reshape(ntiles * ndays, day_count, quarter)
     returned = lax.all_to_all(packed, ("tiles", "days"), 0, 0, tiled=True)
     returned = returned.reshape(ntiles, ndays, day_count, quarter)

time: 137 us -> 137 us (level)
  starting transfers between devices: 51.5 us -> 48.8 us
    gather x3 -> x0, local copies, waits for them, and re-layouts: 5.17 us -> none  [the longest x1 1.8 us: body(): own_rows = jnp.take(arrived, target, axis=0, mode='clip')]
    reshape x2 -> x5, local copies, waits for them, and re-layouts: 1.03 us -> 4.14 us  [the longest x1 1.32 us: body(): outgoing = outgoing.reshape(ntiles * ndays, day_count, quarter)]
    all_to_all x1, starting transfers between devices: 11.6 us -> 8.93 us  [body(): arrived = lax.all_to_all(outgoing, ('tiles', 'days'), 0, 0, tiled=True)]
  transfers between devices with their start and end apart: 7 -> 7, of which waited for: 5 -> 5; matrix products, arithmetic and copies ran while one was open for 3% -> 5% of each run, Pallas kernels for 0% -> 0%
where the time goes in v4:
time: 137 us
  waiting for transfers between devices  65 us (47%)
  starting transfers between devices  48.8 us (36%)
  local copies, waits for them, and re-layouts  11.8 us (9%)
  other arithmetic  9.55 us (7%)
    all_to_all x1, waiting for transfers between devices, body(): arrived = lax.all_to_all(outgoing, ('tiles', 'days'), 0, 0, tiled=True)  27.9 us
    all_to_all x1, waiting for transfers between devices, body(): returned = lax.all_to_all(packed, ('tiles', 'days'), 0, 0, tiled=True)  22.9 us
    all_to_all x1, starting transfers between devices, body(): lax.all_to_all(jnp.broadcast_to(slot_table.astype(jnp.int32)[:, None], (n...  18.4 us
    all_to_all x1, waiting for transfers between devices, body(): lax.all_to_all(jnp.broadcast_to(slot_table.astype(jnp.int32)[:, None], (n...  10.4 us
    all_to_all x1, starting transfers between devices, body(): returned = lax.all_to_all(packed, ('tiles', 'days'), 0, 0, tiled=True)  9.29 us
    all_to_all x1, starting transfers between devices, body(): arrived = lax.all_to_all(outgoing, ('tiles', 'days'), 0, 0, tiled=True)  8.93 us
    ppermute x2, starting transfers between devices, with_halo(): lax.ppermute(tail, 'tiles', [(i, i + 1) for i in range(count - 1)])  6.7 us
    reduce_sum x1, other arithmetic, quantile_map(): total = jnp.sum(slopes[:, None] * clamped, axis=2)  5.55 us
  transfers between devices with their start and end apart: 7, of which 5 were waited for; matrix products, arithmetic and copies ran while one was open for 5% of the time, Pallas kernels for 0%

profile of v4, /device:TPU:1, one launch (start us, length us, event | category | flops | bytes accessed | tf_op | source)
XLA Modules:
  0.0 136.7 jit_solution(12505822429845828670)
XLA Ops:
  0.0 0.7 and_select_fusion
  0.7 0.1 fusion.61
  0.8 0.1 select_reduce_fusion.1
  0.9 0.8 broadcast_in_dim.37
  1.7 18.4 %all-to-all-start = ((s32[128,1,128]{2,1,0:T(1,128)}), s32[128,1,128]{2,1,0:T(1,128)S(1)}, u32[]{:S(2)}, u32[]{:S(2)}) async-start(s32[128,1,128]{2,1,0:T(1,128)} %broadcast_in_dim.37), calls=%async_computation | async-start | bytes 131072 | tf_op jit(solution)/shard_map/all_to_all | solution.py:71
  20.2 0.9 reshape.78
  21.1 0.1 copy.35
  21.2 10.4 %all-to-all-done = s32[128,1,128]{2,1,0:T(1,128)S(1)} async-done(((s32[128,1,128]{2,1,0:T(1,128)}), s32[128,1,128]{2,1,0:T(1,128)S(1)}, u32[]{:S(2)}, u32[]{:S(2)}) %all-to-all-start) | async-done | bytes 65568 | tf_op jit(solution)/shard_map/all_to_all | solution.py:71
  31.7 0.4 convolution_convert_fusion.1
  32.1 1.3 reshape.80
  33.4 8.9 %all-to-all-start.1 = ((bf16[512,8,128]{2,1,0:T(8,128)(2,1)}), bf16[512,8,128]{2,1,0:T(8,128)(2,1)S(1)}, u32[]{:S(2)}, u32[]{:S(2)}) async-start(bf16[512,8,128]{2,1,0:T(8,128)(2,1)} %reshape.80), calls=%async_computation.1 | async-start | bytes 2097152 | tf_op jit(solution)/shard_map/all_to_all | solution.py:85
  42.3 0.0 copy-done.2
  42.3 1.1 fusion.83
  43.5 0.2 fusion.6
  43.6 0.0 copy-start.6
  43.7 0.3 copy.34
  43.9 0.4 copy-done.6
  44.4 0.2 fusion.8
  44.6 0.1 fusion.9
  44.7 1.2 copy.36
  45.9 1.2 copy.37
  47.1 27.9 %all-to-all-done.1 = bf16[512,8,128]{2,1,0:T(8,128)(2,1)S(1)} async-done(((bf16[512,8,128]{2,1,0:T(8,128)(2,1)}), bf16[512,8,128]{2,1,0:T(8,128)(2,1)S(1)}, u32[]{:S(2)}, u32[]{:S(2)}) %all-to-all-start.1) | async-done | bytes 1048608 | tf_op jit(solution)/shard_map/all_to_all | solution.py:85
  75.0 0.5 reshape.81
  75.5 0.0 copy-start
  75.5 0.0 copy-start.1
  75.5 0.3 fusion.4
  75.8 0.1 copy.42
  75.9 0.8 copy-done
  76.6 0.3 copy-done.1
  76.9 5.6 %multiply_reduce_fusion = f32[16,32,128]{2,1,0:T(8,128)S(1)} fusion(f32[16,99,128]{2,1,0:T(8,128)S(1)} %copy-done.1, f32[16,99,128]{2,1,0:T(8,128)S(1)} %copy-done, f32[16,32,128]{2,1,0:T(8,128)S(1)} %bitcast.78, f32[16,99,128]{2,1,0:T(8,128)S(1)} %copy.34), kind=kLoop, calls=%fused_computation.1 | loop fusion | flops 25886720 | bytes 2957312 | tf_op jit(solution)/shard_map/reduce_sum | solution.py:51
  82.5 0.4 convolution_convert_fusion
  82.9 1.3 reshape.82
  84.2 9.3 %all-to-all-start.2 = ((bf16[512,8,128]{2,1,0:T(8,128)(2,1)}), bf16[512,8,128]{2,1,0:T(8,128)(2,1)S(1)}, u32[]{:S(2)}, u32[]{:S(2)}) async-start(bf16[512,8,128]{2,1,0:T(8,128)(2,1)} %reshape.82), calls=%async_computation.2 | async-start | bytes 2097152 | tf_op jit(solution)/shard_map/all_to_all | solution.py:94
  93.5 0.0 copy-done.3
  93.5 0.0 copy-done.5
  93.6 3.9 %collective-permute-start = (f32[2,4,256]{2,1,0:T(4,128)S(1)}, f32[2,4,256]{2,1,0:T(4,128)S(1)}, u32[]{:S(2)}, u32[]{:S(2)}) collective-permute-start(f32[2,4,256]{2,1,0:T(4,128)S(1)} %get-tuple-element.53), channel_id=1, source_target_pairs={{0,4},{4,8},{8,12},{12,16},{16,20},{20,24},{24,28},{28,32},{32,36}... | collective-permute-start | bytes 24584 | tf_op jit(solution)/shard_map/ppermute | solution.py:36
  97.5 3.6 %collective-permute-start.1 = (f32[2,4,256]{2,1,0:T(4,128)S(1)}, f32[2,4,256]{2,1,0:T(4,128)S(1)}, u32[]{:S(2)}, u32[]{:S(2)}) collective-permute-start(f32[2,4,256]{2,1,0:T(4,128)S(1)} %get-tuple-element.54), channel_id=1, source_target_pairs={{4,0},{8,4},{12,8},{16,12},{20,16},{24,20},{28,24},{32,28},{36,32}... | collective-permute-start | bytes 24584 | tf_op jit(solution)/shard_map/ppermute | solution.py:37
  101.1 0.0 collective-permute-done
  101.1 1.9 %collective-permute-done.1 = f32[2,4,256]{2,1,0:T(4,128)S(1)} collective-permute-done((f32[2,4,256]{2,1,0:T(4,128)S(1)}, f32[2,4,256]{2,1,0:T(4,128)S(1)}, u32[]{:S(2)}, u32[]{:S(2)}) %collective-permute-start.1) | collective-permute-done | bytes 8224 | tf_op jit(solution)/shard_map/ppermute | solution.py:37
  103.0 0.1 compare_select_fusion
  103.1 0.0 copy-start.4
  103.3 22.9 %all-to-all-done.2 = bf16[512,8,128]{2,1,0:T(8,128)(2,1)S(1)} async-done(((bf16[512,8,128]{2,1,0:T(8,128)(2,1)}), bf16[512,8,128]{2,1,0:T(8,128)(2,1)S(1)}, u32[]{:S(2)}, u32[]{:S(2)}) %all-to-all-start.2) | async-done | bytes 1048608 | tf_op jit(solution)/shard_map/all_to_all | solution.py:94
  126.2 0.6 gather_fusion
  126.8 0.1 copy.38
  126.8 0.1 reshape.84
  127.0 2.8 %collective-permute-start.2 = (bf16[8,4,256]{2,1,0:T(4,128)(2,1)S(1)}, bf16[8,4,256]{2,1,0:T(4,128)(2,1)S(1)}, u32[]{:S(2)}, u32[]{:S(2)}) collective-permute-start(bf16[8,4,256]{2,1,0:T(4,128)(2,1)S(1)} %get-tuple-element.47), channel_id=1, source_target_pairs={{0,4},{4,8},{8,12},{12,16},{16,20},{20,24},{24,28},{28,32},{32,36}... | collective-permute-start | bytes 49160 | tf_op jit(solution)/shard_map/ppermute | solution.py:36
  129.8 1.9 %collective-permute-start.3 = (bf16[8,4,256]{2,1,0:T(4,128)(2,1)S(1)}, bf16[8,4,256]{2,1,0:T(4,128)(2,1)S(1)}, u32[]{:S(2)}, u32[]{:S(2)}) collective-permute-start(bf16[8,4,256]{2,1,0:T(4,128)(2,1)S(1)} %get-tuple-element.48), channel_id=1, source_target_pairs={{4,0},{8,4},{12,8},{16,12},{20,16},{24,20},{28,24},{32,28},{36,32}... | collective-permute-start | bytes 49160 | tf_op jit(solution)/shard_map/ppermute | solution.py:37
  131.7 0.2 broadcast_multiply_fusion.2
  131.9 0.2 broadcast_multiply_fusion.1
  132.1 0.0 slice-start
  132.1 0.2 broadcast_multiply_fusion
  132.4 0.2 pad_slice_fusion.3
  132.6 0.3 slice-done
  132.9 0.1 fusion.26
  133.0 0.0 collective-permute-done.2
  133.0 1.8 %collective-permute-done.3 = bf16[8,4,256]{2,1,0:T(4,128)(2,1)S(1)} collective-permute-done((bf16[8,4,256]{2,1,0:T(4,128)(2,1)S(1)}, bf16[8,4,256]{2,1,0:T(4,128)(2,1)S(1)}, u32[]{:S(2)}, u32[]{:S(2)}) %collective-permute-start.3) | collective-permute-done | bytes 16416 | tf_op jit(solution)/shard_map/ppermute | solution.py:37
  134.9 0.2 broadcast_multiply_fusion.8
  135.1 0.1 broadcast_multiply_fusion.7
  135.2 0.1 broadcast_multiply_fusion.4
  135.4 0.2 broadcast_multiply_fusion.3
  135.6 0.1 pad_slice_fusion.19
  135.7 0.1 pad_slice_fusion.35
  135.9 0.1 fusion.67
  136.0 0.7 pad_maximum_fusion
  (27 shorter events, 0.3 us)
Async XLA Ops:
  1.7 29.9 %all-to-all-start = ((s32[128,1,128]{2,1,0:T(1,128)}), s32[128,1,128]{2,1,0:T(1,128)S(1)}, u32[]{:S(2)}, u32[]{:S(2)}) async-start(s32[128,1,128]{2,1,0:T(1,128)} %broadcast_in_dim.37), calls=%async_computation | async-start | bytes 131072 | tf_op jit(solution)/shard_map/all_to_all | solution.py:71
  33.4 8.9 %copy-start.2 = (bf16[16,2,99,128]{3,1,2,0:T(2,128)(2,1)S(1)}, bf16[16,2,99,128]{3,1,2,0:T(2,128)(2,1)}, u32[]{:S(2)}) copy-start(bf16[16,2,99,128]{3,1,2,0:T(2,128)(2,1)} %param.8) | copy-start | bytes 2433028
  33.4 41.6 %all-to-all-start.1 = ((bf16[512,8,128]{2,1,0:T(8,128)(2,1)}), bf16[512,8,128]{2,1,0:T(8,128)(2,1)S(1)}, u32[]{:S(2)}, u32[]{:S(2)}) async-start(bf16[512,8,128]{2,1,0:T(8,128)(2,1)} %reshape.80), calls=%async_computation.1 | async-start | bytes 2097152 | tf_op jit(solution)/shard_map/all_to_all | solution.py:85
  43.6 0.7 copy-start.6
  75.5 1.2 copy-start
  75.5 1.4 %copy-start.1 = (f32[16,99,128]{2,1,0:T(8,128)S(1)}, f32[16,99,128]{2,1,0:T(8,128)}, u32[]{:S(2)}) copy-start(f32[16,99,128]{2,1,0:T(8,128)} %copy.37) | copy-start | bytes 2433028
  84.2 9.3 %copy-start.3 = (f32[32,256]{1,0:T(8,128)S(1)}, f32[32,256]{1,0:T(8,128)}, u32[]{:S(2)}) copy-start(f32[32,256]{1,0:T(8,128)} %param.11) | copy-start | bytes 98308
  84.2 9.3 %copy-start.5 = (s32[32,256]{1,0:T(8,128)S(1)}, s32[32,256]{1,0:T(8,128)}, u32[]{:S(2)}) copy-start(s32[32,256]{1,0:T(8,128)} %param.10) | copy-start | bytes 98308
  84.2 42.0 %all-to-all-start.2 = ((bf16[512,8,128]{2,1,0:T(8,128)(2,1)}), bf16[512,8,128]{2,1,0:T(8,128)(2,1)S(1)}, u32[]{:S(2)}, u32[]{:S(2)}) async-start(bf16[512,8,128]{2,1,0:T(8,128)(2,1)} %reshape.82), calls=%async_computation.2 | async-start | bytes 2097152 | tf_op jit(solution)/shard_map/all_to_all | solution.py:94
  93.6 7.5 %collective-permute-start = (f32[2,4,256]{2,1,0:T(4,128)S(1)}, f32[2,4,256]{2,1,0:T(4,128)S(1)}, u32[]{:S(2)}, u32[]{:S(2)}) collective-permute-start(f32[2,4,256]{2,1,0:T(4,128)S(1)} %get-tuple-element.53), channel_id=1, source_target_pairs={{0,4},{4,8},{8,12},{12,16},{16,20},{20,24},{24,28},{28,32},{32,36}... | collective-permute-start | bytes 24584 | tf_op jit(solution)/shard_map/ppermute | solution.py:36
  97.5 5.5 %collective-permute-start.1 = (f32[2,4,256]{2,1,0:T(4,128)S(1)}, f32[2,4,256]{2,1,0:T(4,128)S(1)}, u32[]{:S(2)}, u32[]{:S(2)}) collective-permute-start(f32[2,4,256]{2,1,0:T(4,128)S(1)} %get-tuple-element.54), channel_id=1, source_target_pairs={{4,0},{8,4},{12,8},{16,12},{20,16},{24,20},{28,24},{32,28},{36,32}... | collective-permute-start | bytes 24584 | tf_op jit(solution)/shard_map/ppermute | solution.py:37
  103.1 28.8 %copy-start.4 = (f32[40,256]{1,0:T(8,128)}, f32[40,256]{1,0:T(8,128)S(1)}, u32[]{:S(2)}) copy-start(f32[40,256]{1,0:T(8,128)S(1)} %compare_select_fusion) | copy-start | bytes 122884
  127.0 6.0 %collective-permute-start.2 = (bf16[8,4,256]{2,1,0:T(4,128)(2,1)S(1)}, bf16[8,4,256]{2,1,0:T(4,128)(2,1)S(1)}, u32[]{:S(2)}, u32[]{:S(2)}) collective-permute-start(bf16[8,4,256]{2,1,0:T(4,128)(2,1)S(1)} %get-tuple-element.47), channel_id=1, source_target_pairs={{0,4},{4,8},{8,12},{12,16},{16,20},{20,24},{24,28},{28,32},{32,36}... | collective-permute-start | bytes 49160 | tf_op jit(solution)/shard_map/ppermute | solution.py:36
  129.8 5.1 %collective-permute-start.3 = (bf16[8,4,256]{2,1,0:T(4,128)(2,1)S(1)}, bf16[8,4,256]{2,1,0:T(4,128)(2,1)S(1)}, u32[]{:S(2)}, u32[]{:S(2)}) collective-permute-start(bf16[8,4,256]{2,1,0:T(4,128)(2,1)S(1)} %get-tuple-element.48), channel_id=1, source_target_pairs={{4,0},{8,4},{12,8},{16,12},{20,16},{24,20},{28,24},{32,28},{36,32}... | collective-permute-start | bytes 49160 | tf_op jit(solution)/shard_map/ppermute | solution.py:37
  132.1 0.7 slice-start

commit v5 on v3

--- a/solution.py
+++ b/solution.py
@@ -37,14 +37,14 @@
 def quantile_map(values, anchor, increments):
     step_x = increments[:, 0].astype(jnp.float32)
     step_y = increments[:, 1].astype(jnp.float32)
-    position = anchor[:, 0][:, None, :].astype(jnp.float32) + jnp.cumsum(step_x, axis=1) - step_x
-    upper = position + step_x
+    ends = anchor[:, 0][:, None, :].astype(jnp.float32) + jnp.cumsum(step_x, axis=1)
+    position = jnp.concatenate([anchor[:, 0][:, None, :].astype(jnp.float32), ends], axis=1)
     slopes = step_y / step_x
-    offset = anchor[:, 1].astype(jnp.float32) - jnp.sum(slopes * position, axis=1)
-    clamped = jnp.minimum(
-        jnp.maximum(values.astype(jnp.float32)[:, :, None, :], position[:, None]), upper[:, None]
-    )
-    total = jnp.sum(slopes[:, None] * clamped, axis=2)
+    zero = jnp.zeros_like(slopes[:, :1])
+    bends = jnp.concatenate([slopes, zero], axis=1) - jnp.concatenate([zero, slopes], axis=1)
+    offset = anchor[:, 1].astype(jnp.float32) - jnp.sum(bends * position, axis=1)
+    above = jnp.maximum(values.astype(jnp.float32)[:, :, None, :], position[:, None])
+    total = jnp.sum(bends[:, None] * above, axis=2)
     return (offset[:, None, :] + total).astype(jnp.bfloat16)
 
 
@@ -113,9 +113,9 @@
     bottom = smoothed(
         wide_field[:, low:], wide_weights[low:], wide_center[low:], wide_denom[low:]
     )
-    return jnp.concatenate(
-        [top[:, depth : 2 * depth], inner[:, depth : row_count - depth], bottom[:, depth : 2 * depth]],
-        axis=1,
+    inner = lax.dynamic_update_slice_in_dim(inner, top[:, depth : 2 * depth], 0, axis=1)
+    return lax.dynamic_update_slice_in_dim(
+        inner, bottom[:, depth : 2 * depth], row_count - depth, axis=1
     )
 
 

time: 137 us -> 134 us (0.978)
  waiting for transfers between devices: 64.7 us -> 67.8 us
  starting transfers between devices: 51.5 us -> 48.8 us
  local copies, waits for them, and re-layouts: 11 us -> 9.19 us
  other arithmetic: 8.73 us -> 7.08 us
    all_to_all x1, starting transfers between devices: 11.6 us -> 8.89 us  [body(): arrived = lax.all_to_all(outgoing, ('tiles', 'days'), 0, 0, tiled=True)]
    all_to_all x1, waiting for transfers between devices: 27.7 us -> 30.3 us  [body(): arrived = lax.all_to_all(outgoing, ('tiles', 'days'), 0, 0, tiled=True)]
    reduce_sum x1 -> x2, other arithmetic: 4.57 us -> 3.13 us  [the longest x1 2.88 us: quantile_map(): total = jnp.sum(bends[:, None] * above, axis=2)]
where the time goes in v5:
time: 134 us; the launch traced here: 133 us
  waiting for transfers between devices  67.8 us (51%)
  starting transfers between devices  48.8 us (36%)
  local copies, waits for them, and re-layouts  9.19 us (7%)
  other arithmetic  7.08 us (5%)
    all_to_all x1, waiting for transfers between devices, body(): arrived = lax.all_to_all(outgoing, ('tiles', 'days'), 0, 0, tiled=True)  30.3 us
    all_to_all x1, waiting for transfers between devices, body(): returned = lax.all_to_all(packed, ('tiles', 'days'), 0, 0, tiled=True)  22.9 us
    all_to_all x1, starting transfers between devices, body(): lax.all_to_all(jnp.broadcast_to(slot_table.astype(jnp.int32)[:, None], (n...  18.4 us
    all_to_all x1, waiting for transfers between devices, body(): lax.all_to_all(jnp.broadcast_to(slot_table.astype(jnp.int32)[:, None], (n...  10.4 us
    all_to_all x1, starting transfers between devices, body(): returned = lax.all_to_all(packed, ('tiles', 'days'), 0, 0, tiled=True)  9.29 us
    all_to_all x1, starting transfers between devices, body(): arrived = lax.all_to_all(outgoing, ('tiles', 'days'), 0, 0, tiled=True)  8.89 us
    ppermute x2, starting transfers between devices, with_halo(): lax.ppermute(tail, 'tiles', [(i, i + 1) for i in range(count - 1)])  6.7 us
    ppermute x2, starting transfers between devices, with_halo(): lax.ppermute(head, 'tiles', [(i + 1, i) for i in range(count - 1)])  5.49 us
  transfers between devices with their start and end apart: 7, of which 5 were waited for; matrix products, arithmetic and copies ran while one was open for 3% of the time, Pallas kernels for 0%

profile of v5, /device:TPU:1, one launch (start us, length us, event | category | flops | bytes accessed | tf_op | source)
XLA Modules:
  0.0 133.3 jit_solution(15215068366372621412)
XLA Ops:
  0.0 0.7 and_select_fusion
  0.7 0.1 fusion.55
  0.8 0.1 select_reduce_fusion.1
  0.9 0.8 broadcast_in_dim.55
  1.7 18.4 %all-to-all-start = ((s32[128,1,128]{2,1,0:T(1,128)}), s32[128,1,128]{2,1,0:T(1,128)S(1)}, u32[]{:S(2)}, u32[]{:S(2)}) async-start(s32[128,1,128]{2,1,0:T(1,128)} %broadcast_in_dim.55), calls=%async_computation | async-start | bytes 131072 | tf_op jit(solution)/shard_map/all_to_all | solution.py:68
  20.2 0.9 reshape.59
  21.1 0.1 copy.48
  21.2 10.4 %all-to-all-done = s32[128,1,128]{2,1,0:T(1,128)S(1)} async-done(((s32[128,1,128]{2,1,0:T(1,128)}), s32[128,1,128]{2,1,0:T(1,128)S(1)}, u32[]{:S(2)}, u32[]{:S(2)}) %all-to-all-start) | async-done | bytes 65568 | tf_op jit(solution)/shard_map/all_to_all | solution.py:68
  31.6 0.1 fusion.54
  31.7 1.7 %gather_fusion = bf16[128,8,4,128]{3,1,2,0:T(8,128)(2,1)} fusion(bf16[8,16,4,128]{3,0,2,1:T(8,128)(2,1)S(1)} %copy.48, s32[1024]{0:T(1024)S(1)} %pad_clamp_fusion.3), kind=kCustom, calls=%fused_computation | custom fusion | bytes 2097664 | tf_op jit(solution)/shard_map/jit(_take)/gather | solution.py:80
  33.4 0.0 copy-start.4
  33.4 0.0 copy-start
  33.4 8.9 %all-to-all-start.1 = ((bf16[512,8,128]{2,1,0:T(8,128)(2,1)}), bf16[512,8,128]{2,1,0:T(8,128)(2,1)S(1)}, u32[]{:S(2)}, u32[]{:S(2)}) async-start(bf16[512,8,128]{2,1,0:T(8,128)(2,1)} %bitcast.11), calls=%async_computation.1 | async-start | bytes 2097152 | tf_op jit(solution)/shard_map/all_to_all | solution.py:82
  42.3 0.0 copy-done.4
  42.3 0.0 copy-done
  42.4 1.1 fusion.74
  43.5 0.2 convert_divide_fusion
  43.7 0.1 broadcast_add_fusion
  43.8 0.2 multiply_reduce_fusion.1
  44.1 0.3 copy.47
  44.3 0.3 copy.49
  44.7 30.3 %all-to-all-done.1 = bf16[512,8,128]{2,1,0:T(8,128)(2,1)S(1)} async-done(((bf16[512,8,128]{2,1,0:T(8,128)(2,1)}), bf16[512,8,128]{2,1,0:T(8,128)(2,1)S(1)}, u32[]{:S(2)}, u32[]{:S(2)}) %all-to-all-start.1) | async-done | bytes 1048608 | tf_op jit(solution)/shard_map/all_to_all | solution.py:82
  75.0 0.6 gather_fusion.1
  75.6 2.9 %multiply_reduce_fusion = f32[16,32,128]{2,1,0:T(8,128)S(1)} fusion(f32[16,100,128]{2,1,0:T(8,128)S(1)} %copy.49, f32[16,32,128]{2,1,0:T(8,128)S(1)} %convert_element_type.62, f32[16,100,128]{2,1,0:T(8,128)S(1)} %copy.47), kind=kLoop, calls=%fused_computation.4 | loop fusion | flops 19595264 | bytes 2162688 | tf_op jit(solution)/shard_map/reduce_sum | solution.py:47
  78.5 1.7 %gather_fusion.2 = bf16[128,32,128]{2,1,0:T(8,128)(2,1)} fusion(bf16[16,32,128]{2,1,0:T(8,128)(2,1)S(1)} %add_convert_fusion, s32[1024]{0:T(1024)S(1)} %pad_clamp_fusion.1), kind=kCustom, calls=%fused_computation.2 | custom fusion | bytes 2097664 | tf_op jit(solution)/shard_map/jit(_take)/gather | solution.py:88
  80.2 0.0 copy-start.1
  80.2 0.0 copy-start.3
  80.2 9.3 %all-to-all-start.2 = ((bf16[512,8,128]{2,1,0:T(8,128)(2,1)}), bf16[512,8,128]{2,1,0:T(8,128)(2,1)S(1)}, u32[]{:S(2)}, u32[]{:S(2)}) async-start(bf16[512,8,128]{2,1,0:T(8,128)(2,1)} %bitcast.13), calls=%async_computation.2 | async-start | bytes 2097152 | tf_op jit(solution)/shard_map/all_to_all | solution.py:90
  89.5 0.0 copy-done.1
  89.5 0.0 copy-done.3
  89.5 3.9 %collective-permute-start = (f32[2,4,256]{2,1,0:T(4,128)S(1)}, f32[2,4,256]{2,1,0:T(4,128)S(1)}, u32[]{:S(2)}, u32[]{:S(2)}) collective-permute-start(f32[2,4,256]{2,1,0:T(4,128)S(1)} %get-tuple-element.45), channel_id=1, source_target_pairs={{0,4},{4,8},{8,12},{12,16},{16,20},{20,24},{24,28},{28,32},{32,36}... | collective-permute-start | bytes 24584 | tf_op jit(solution)/shard_map/ppermute | solution.py:32
  93.5 3.6 %collective-permute-start.1 = (f32[2,4,256]{2,1,0:T(4,128)S(1)}, f32[2,4,256]{2,1,0:T(4,128)S(1)}, u32[]{:S(2)}, u32[]{:S(2)}) collective-permute-start(f32[2,4,256]{2,1,0:T(4,128)S(1)} %get-tuple-element.46), channel_id=1, source_target_pairs={{4,0},{8,4},{12,8},{16,12},{20,16},{24,20},{28,24},{32,28},{36,32}... | collective-permute-start | bytes 24584 | tf_op jit(solution)/shard_map/ppermute | solution.py:33
  97.1 0.0 collective-permute-done
  97.1 1.9 %collective-permute-done.1 = f32[2,4,256]{2,1,0:T(4,128)S(1)} collective-permute-done((f32[2,4,256]{2,1,0:T(4,128)S(1)}, f32[2,4,256]{2,1,0:T(4,128)S(1)}, u32[]{:S(2)}, u32[]{:S(2)}) %collective-permute-start.1) | collective-permute-done | bytes 8224 | tf_op jit(solution)/shard_map/ppermute | solution.py:33
  99.0 0.1 compare_select_fusion
  99.2 22.9 %all-to-all-done.2 = bf16[512,8,128]{2,1,0:T(8,128)(2,1)S(1)} async-done(((bf16[512,8,128]{2,1,0:T(8,128)(2,1)}), bf16[512,8,128]{2,1,0:T(8,128)(2,1)S(1)}, u32[]{:S(2)}, u32[]{:S(2)}) %all-to-all-start.2) | async-done | bytes 1048608 | tf_op jit(solution)/shard_map/all_to_all | solution.py:90
  122.2 0.6 gather_fusion.3
  122.7 0.1 copy.50
  122.8 0.1 reshape.64
  123.0 2.8 %collective-permute-start.2 = (bf16[8,4,256]{2,1,0:T(4,128)(2,1)S(1)}, bf16[8,4,256]{2,1,0:T(4,128)(2,1)S(1)}, u32[]{:S(2)}, u32[]{:S(2)}) collective-permute-start(bf16[8,4,256]{2,1,0:T(4,128)(2,1)S(1)} %get-tuple-element.39), channel_id=1, source_target_pairs={{0,4},{4,8},{8,12},{12,16},{16,20},{20,24},{24,28},{28,32},{32,36}... | collective-permute-start | bytes 49160 | tf_op jit(solution)/shard_map/ppermute | solution.py:32
  125.7 1.9 %collective-permute-start.3 = (bf16[8,4,256]{2,1,0:T(4,128)(2,1)S(1)}, bf16[8,4,256]{2,1,0:T(4,128)(2,1)S(1)}, u32[]{:S(2)}, u32[]{:S(2)}) collective-permute-start(bf16[8,4,256]{2,1,0:T(4,128)(2,1)S(1)} %get-tuple-element.40), channel_id=1, source_target_pairs={{4,0},{8,4},{12,8},{16,12},{20,16},{24,20},{28,24},{32,28},{36,32}... | collective-permute-start | bytes 49160 | tf_op jit(solution)/shard_map/ppermute | solution.py:33
  127.7 0.2 broadcast_multiply_fusion.2
  127.9 0.2 broadcast_multiply_fusion.1
  128.1 0.2 broadcast_multiply_fusion
  128.3 0.2 fusion.21
  128.5 0.0 collective-permute-done.2
  128.5 2.3 %collective-permute-done.3 = bf16[8,4,256]{2,1,0:T(4,128)(2,1)S(1)} collective-permute-done((bf16[8,4,256]{2,1,0:T(4,128)(2,1)S(1)}, bf16[8,4,256]{2,1,0:T(4,128)(2,1)S(1)}, u32[]{:S(2)}, u32[]{:S(2)}) %collective-permute-start.3) | collective-permute-done | bytes 16416 | tf_op jit(solution)/shard_map/ppermute | solution.py:33
  130.8 0.1 broadcast_multiply_fusion.5
  131.0 0.1 broadcast_multiply_fusion.8
  131.1 0.1 broadcast_multiply_fusion.7
  131.2 0.1 broadcast_multiply_fusion.4
  131.4 0.2 broadcast_multiply_fusion.3
  131.6 0.1 pad_slice_fusion.35
  131.8 0.1 pad_slice_fusion.19
  131.9 0.1 divide_dynamic-update-slice_fusion.1
  132.0 0.0 copy-start.2
  132.0 0.7 copy-done.2
  132.7 0.7 divide_dynamic-update-slice_fusion
  (25 shorter events, 0.3 us)
Async XLA Ops:
  1.7 29.9 %all-to-all-start = ((s32[128,1,128]{2,1,0:T(1,128)}), s32[128,1,128]{2,1,0:T(1,128)S(1)}, u32[]{:S(2)}, u32[]{:S(2)}) async-start(s32[128,1,128]{2,1,0:T(1,128)} %broadcast_in_dim.55), calls=%async_computation | async-start | bytes 131072 | tf_op jit(solution)/shard_map/all_to_all | solution.py:68
  33.4 8.9 %copy-start.4 = (bf16[16,2,128]{2,1,0:T(2,128)(2,1)S(1)}, bf16[16,2,128]{2,1,0:T(2,128)(2,1)}, u32[]{:S(2)}) copy-start(bf16[16,2,128]{2,1,0:T(2,128)(2,1)} %param.7) | copy-start | bytes 24580
  33.4 8.9 %copy-start = (bf16[16,2,99,128]{3,1,2,0:T(2,128)(2,1)S(1)}, bf16[16,2,99,128]{3,1,2,0:T(2,128)(2,1)}, u32[]{:S(2)}) copy-start(bf16[16,2,99,128]{3,1,2,0:T(2,128)(2,1)} %param.8) | copy-start | bytes 2433028
  33.4 41.6 %all-to-all-start.1 = ((bf16[512,8,128]{2,1,0:T(8,128)(2,1)}), bf16[512,8,128]{2,1,0:T(8,128)(2,1)S(1)}, u32[]{:S(2)}, u32[]{:S(2)}) async-start(bf16[512,8,128]{2,1,0:T(8,128)(2,1)} %bitcast.11), calls=%async_computation.1 | async-start | bytes 2097152 | tf_op jit(solution)/shard_map/all_to_all | solution.py:82
  80.2 9.3 %copy-start.1 = (f32[32,256]{1,0:T(8,128)S(1)}, f32[32,256]{1,0:T(8,128)}, u32[]{:S(2)}) copy-start(f32[32,256]{1,0:T(8,128)} %param.11) | copy-start | bytes 98308
  80.2 9.3 %copy-start.3 = (s32[32,256]{1,0:T(8,128)S(1)}, s32[32,256]{1,0:T(8,128)}, u32[]{:S(2)}) copy-start(s32[32,256]{1,0:T(8,128)} %param.10) | copy-start | bytes 98308
  80.2 42.0 %all-to-all-start.2 = ((bf16[512,8,128]{2,1,0:T(8,128)(2,1)}), bf16[512,8,128]{2,1,0:T(8,128)(2,1)S(1)}, u32[]{:S(2)}, u32[]{:S(2)}) async-start(bf16[512,8,128]{2,1,0:T(8,128)(2,1)} %bitcast.13), calls=%async_computation.2 | async-start | bytes 2097152 | tf_op jit(solution)/shard_map/all_to_all | solution.py:90
  89.5 7.5 %collective-permute-start = (f32[2,4,256]{2,1,0:T(4,128)S(1)}, f32[2,4,256]{2,1,0:T(4,128)S(1)}, u32[]{:S(2)}, u32[]{:S(2)}) collective-permute-start(f32[2,4,256]{2,1,0:T(4,128)S(1)} %get-tuple-element.45), channel_id=1, source_target_pairs={{0,4},{4,8},{8,12},{12,16},{16,20},{20,24},{24,28},{28,32},{32,36}... | collective-permute-start | bytes 24584 | tf_op jit(solution)/shard_map/ppermute | solution.py:32
  93.5 5.5 %collective-permute-start.1 = (f32[2,4,256]{2,1,0:T(4,128)S(1)}, f32[2,4,256]{2,1,0:T(4,128)S(1)}, u32[]{:S(2)}, u32[]{:S(2)}) collective-permute-start(f32[2,4,256]{2,1,0:T(4,128)S(1)} %get-tuple-element.46), channel_id=1, source_target_pairs={{4,0},{8,4},{12,8},{16,12},{20,16},{24,20},{28,24},{32,28},{36,32}... | collective-permute-start | bytes 24584 | tf_op jit(solution)/shard_map/ppermute | solution.py:33
  123.0 5.6 %collective-permute-start.2 = (bf16[8,4,256]{2,1,0:T(4,128)(2,1)S(1)}, bf16[8,4,256]{2,1,0:T(4,128)(2,1)S(1)}, u32[]{:S(2)}, u32[]{:S(2)}) collective-permute-start(bf16[8,4,256]{2,1,0:T(4,128)(2,1)S(1)} %get-tuple-element.39), channel_id=1, source_target_pairs={{0,4},{4,8},{8,12},{12,16},{16,20},{20,24},{24,28},{28,32},{32,36}... | collective-permute-start | bytes 49160 | tf_op jit(solution)/shard_map/ppermute | solution.py:32
  125.7 5.1 %collective-permute-start.3 = (bf16[8,4,256]{2,1,0:T(4,128)(2,1)S(1)}, bf16[8,4,256]{2,1,0:T(4,128)(2,1)S(1)}, u32[]{:S(2)}, u32[]{:S(2)}) collective-permute-start(bf16[8,4,256]{2,1,0:T(4,128)(2,1)S(1)} %get-tuple-element.40), channel_id=1, source_target_pairs={{4,0},{8,4},{12,8},{16,12},{20,16},{24,20},{28,24},{32,28},{36,32}... | collective-permute-start | bytes 49160 | tf_op jit(solution)/shard_map/ppermute | solution.py:33
  132.0 0.7 copy-start.2

commit v6 on v5

--- a/solution.py
+++ b/solution.py
@@ -25,10 +25,12 @@
     return field
 
 
-def with_halo(cells, width):
+def with_halo(cells, width, edge_rows=None):
     count = lax.axis_size("tiles")
-    head = cells[..., :width, :]
-    tail = cells[..., cells.shape[-2] - width :, :]
+    if edge_rows is None:
+        edge_rows = jnp.concatenate([cells[..., :width, :], cells[..., cells.shape[-2] - width :, :]], axis=-2)
+    head = edge_rows[..., :width, :]
+    tail = edge_rows[..., width:, :]
     from_above = lax.ppermute(tail, "tiles", [(i, i + 1) for i in range(count - 1)])
     from_below = lax.ppermute(head, "tiles", [(i + 1, i) for i in range(count - 1)])
     return jnp.concatenate([from_above, cells, from_below], axis=-2)
@@ -91,6 +93,10 @@
     returned = returned.reshape(ntiles, ndays, day_count, quarter)
     blocks = jnp.take(returned, holder, axis=0, mode="clip")
     mapped = blocks.transpose(2, 0, 1, 3).reshape(day_count, row_count, columns)
+    edge_count = PASSES // 2
+    edges = jnp.concatenate([holder[:edge_count], holder[owned - edge_count :]])
+    edge_rows = jnp.take(returned, edges, axis=0, mode="clip").transpose(2, 0, 1, 3)
+    edge_rows = edge_rows.reshape(day_count, 2 * PASSES, columns)
 
     depth = PASSES
     weights = terrain * land_mask.astype(jnp.float32)
@@ -104,7 +110,7 @@
     own_denom = wide_denom[depth : depth + row_count]
     field = mapped.astype(jnp.float32)
     inner = smoothed(field, own_weights, own_center, own_denom)
-    wide_field = with_halo(mapped, depth).astype(jnp.float32)
+    wide_field = with_halo(mapped, depth, edge_rows).astype(jnp.float32)
     strip = 3 * depth
     top = smoothed(
         wide_field[:, :strip], wide_weights[:strip], wide_center[:strip], wide_denom[:strip]
@@ -113,9 +119,9 @@
     bottom = smoothed(
         wide_field[:, low:], wide_weights[low:], wide_center[low:], wide_denom[low:]
     )
-    inner = lax.dynamic_update_slice_in_dim(inner, top[:, depth : 2 * depth], 0, axis=1)
-    return lax.dynamic_update_slice_in_dim(
-        inner, bottom[:, depth : 2 * depth], row_count - depth, axis=1
+    return jnp.concatenate(
+        [top[:, depth : 2 * depth], inner[:, depth : row_count - depth], bottom[:, depth : 2 * depth]],
+        axis=1,
     )
 
 

time: 134 us -> 133 us (level)
  waiting for transfers between devices: 67.8 us -> 66.3 us
    all_to_all x1, waiting for transfers between devices: 22.9 us -> 32.1 us  [body(): returned = lax.all_to_all(packed, ('tiles', 'days'), 0, 0, tiled=True)]
    all_to_all x1, waiting for transfers between devices: 30.3 us -> 22.7 us  [body(): arrived = lax.all_to_all(outgoing, ('tiles', 'days'), 0, 0, tiled=True)]
    ppermute x2, waiting for transfers between devices: 4.14 us -> 1.05 us  [with_halo(): lax.ppermute(head, 'tiles', [(i + 1, i) for i in range(count - 1)])]
  transfers between devices with their start and end apart: 7 -> 7, of which waited for: 5 -> 4; matrix products, arithmetic and copies ran while one was open for 3% -> 4% of each run, Pallas kernels for 0% -> 0%
where the time goes in v6:
time: 133 us
  waiting for transfers between devices  66.3 us (50%)
  starting transfers between devices  49 us (37%)
  local copies, waits for them, and re-layouts  9.73 us (7%)
  other arithmetic  7.14 us (5%)
    all_to_all x1, waiting for transfers between devices, body(): returned = lax.all_to_all(packed, ('tiles', 'days'), 0, 0, tiled=True)  32.1 us
    all_to_all x1, waiting for transfers between devices, body(): arrived = lax.all_to_all(outgoing, ('tiles', 'days'), 0, 0, tiled=True)  22.7 us
    all_to_all x1, starting transfers between devices, body(): lax.all_to_all(jnp.broadcast_to(slot_table.astype(jnp.int32)[:, None], (n...  18.4 us
    all_to_all x1, waiting for transfers between devices, body(): lax.all_to_all(jnp.broadcast_to(slot_table.astype(jnp.int32)[:, None], (n...  10.4 us
    all_to_all x1, starting transfers between devices, body(): returned = lax.all_to_all(packed, ('tiles', 'days'), 0, 0, tiled=True)  9.15 us
    all_to_all x1, starting transfers between devices, body(): arrived = lax.all_to_all(outgoing, ('tiles', 'days'), 0, 0, tiled=True)  8.93 us
    ppermute x2, starting transfers between devices, with_halo(): lax.ppermute(tail, 'tiles', [(i, i + 1) for i in range(count - 1)])  6.97 us
    ppermute x2, starting transfers between devices, with_halo(): lax.ppermute(head, 'tiles', [(i + 1, i) for i in range(count - 1)])  5.49 us
  transfers between devices with their start and end apart: 7, of which 4 were waited for; matrix products, arithmetic and copies ran while one was open for 4% of the time, Pallas kernels for 0%

profile of v6, /device:TPU:1, one launch (start us, length us, event | category | flops | bytes accessed | tf_op | source)
XLA Modules:
  0.0 132.6 jit_solution(15654698428448578716)
XLA Ops:
  0.0 0.7 and_select_fusion
  0.7 0.1 fusion.52
  0.8 0.1 select_reduce_fusion.1
  0.9 0.8 broadcast_in_dim.59
  1.7 18.4 %all-to-all-start = ((s32[128,1,128]{2,1,0:T(1,128)}), s32[128,1,128]{2,1,0:T(1,128)S(1)}, u32[]{:S(2)}, u32[]{:S(2)}) async-start(s32[128,1,128]{2,1,0:T(1,128)} %broadcast_in_dim.59), calls=%async_computation | async-start | bytes 131072 | tf_op jit(solution)/shard_map/all_to_all | solution.py:70
  20.2 0.9 reshape.62
  21.1 0.1 copy.52
  21.2 10.4 %all-to-all-done = s32[128,1,128]{2,1,0:T(1,128)S(1)} async-done(((s32[128,1,128]{2,1,0:T(1,128)}), s32[128,1,128]{2,1,0:T(1,128)S(1)}, u32[]{:S(2)}, u32[]{:S(2)}) %all-to-all-start) | async-done | bytes 65568 | tf_op jit(solution)/shard_map/all_to_all | solution.py:70
  31.6 0.1 fusion.51
  31.7 1.7 %gather_fusion = bf16[128,8,4,128]{3,1,2,0:T(8,128)(2,1)} fusion(bf16[8,16,4,128]{3,0,2,1:T(8,128)(2,1)S(1)} %copy.52, s32[1024]{0:T(1024)S(1)} %pad_clamp_fusion.4), kind=kCustom, calls=%fused_computation | custom fusion | bytes 2097664 | tf_op jit(solution)/shard_map/jit(_take)/gather | solution.py:82
  33.4 0.0 copy-start.1
  33.4 0.0 copy-start.3
  33.4 0.0 copy-start.4
  33.4 0.0 copy-start
  33.4 8.9 %all-to-all-start.1 = ((bf16[512,8,128]{2,1,0:T(8,128)(2,1)}), bf16[512,8,128]{2,1,0:T(8,128)(2,1)S(1)}, u32[]{:S(2)}, u32[]{:S(2)}) async-start(bf16[512,8,128]{2,1,0:T(8,128)(2,1)} %bitcast.11), calls=%async_computation.1 | async-start | bytes 2097152 | tf_op jit(solution)/shard_map/all_to_all | solution.py:84
  42.4 0.0 copy-done.1
  42.4 0.0 copy-done.3
  42.4 4.1 %collective-permute-start = (f32[2,4,256]{2,1,0:T(4,128)S(1)}, f32[2,4,256]{2,1,0:T(4,128)S(1)}, u32[]{:S(2)}, u32[]{:S(2)}) collective-permute-start(f32[2,4,256]{2,1,0:T(4,128)S(1)} %get-tuple-element.50), channel_id=1, source_target_pairs={{0,4},{4,8},{8,12},{12,16},{16,20},{20,24},{24,28},{28,32},{32,36}... | collective-permute-start | bytes 24584 | tf_op jit(solution)/shard_map/ppermute | solution.py:34
  46.5 3.6 %collective-permute-start.1 = (f32[2,4,256]{2,1,0:T(4,128)S(1)}, f32[2,4,256]{2,1,0:T(4,128)S(1)}, u32[]{:S(2)}, u32[]{:S(2)}) collective-permute-start(f32[2,4,256]{2,1,0:T(4,128)S(1)} %get-tuple-element.51), channel_id=1, source_target_pairs={{4,0},{8,4},{12,8},{16,12},{20,16},{24,20},{28,24},{32,28},{36,32}... | collective-permute-start | bytes 24584 | tf_op jit(solution)/shard_map/ppermute | solution.py:35
  50.1 0.0 copy-done.4
  50.1 0.0 copy-done
  50.1 1.1 fusion.73
  51.3 0.2 convert_divide_fusion
  51.5 0.1 broadcast_add_fusion
  51.6 0.2 multiply_reduce_fusion.1
  51.9 0.3 copy.51
  52.2 0.3 copy.53
  52.4 0.0 collective-permute-done
  52.4 0.0 collective-permute-done.1
  52.5 22.7 %all-to-all-done.1 = bf16[512,8,128]{2,1,0:T(8,128)(2,1)S(1)} async-done(((bf16[512,8,128]{2,1,0:T(8,128)(2,1)}), bf16[512,8,128]{2,1,0:T(8,128)(2,1)S(1)}, u32[]{:S(2)}, u32[]{:S(2)}) %all-to-all-start.1) | async-done | bytes 1048608 | tf_op jit(solution)/shard_map/all_to_all | solution.py:84
  75.2 0.6 gather_fusion.1
  75.8 2.9 %multiply_reduce_fusion = f32[16,32,128]{2,1,0:T(8,128)S(1)} fusion(f32[16,100,128]{2,1,0:T(8,128)S(1)} %copy.53, f32[16,32,128]{2,1,0:T(8,128)S(1)} %convert_element_type.62, f32[16,100,128]{2,1,0:T(8,128)S(1)} %copy.51), kind=kLoop, calls=%fused_computation.5 | loop fusion | flops 19595264 | bytes 2162688 | tf_op jit(solution)/shard_map/reduce_sum | solution.py:49
  78.7 1.7 %gather_fusion.2 = bf16[128,32,128]{2,1,0:T(8,128)(2,1)} fusion(bf16[16,32,128]{2,1,0:T(8,128)(2,1)S(1)} %add_convert_fusion, s32[1024]{0:T(1024)S(1)} %pad_clamp_fusion.2), kind=kCustom, calls=%fused_computation.2 | custom fusion | bytes 2097664 | tf_op jit(solution)/shard_map/jit(_take)/gather | solution.py:90
  80.4 9.2 %all-to-all-start.2 = ((bf16[512,8,128]{2,1,0:T(8,128)(2,1)}), bf16[512,8,128]{2,1,0:T(8,128)(2,1)S(1)}, u32[]{:S(2)}, u32[]{:S(2)}) async-start(bf16[512,8,128]{2,1,0:T(8,128)(2,1)} %bitcast.13), calls=%async_computation.2 | async-start | bytes 2097152 | tf_op jit(solution)/shard_map/all_to_all | solution.py:92
  89.6 0.1 compare_select_fusion
  89.7 0.0 copy-start.2
  89.8 0.1 fusion.77
  89.9 0.1 pad_add_fusion
  90.0 32.1 %all-to-all-done.2 = bf16[512,8,128]{2,1,0:T(8,128)(2,1)S(1)} async-done(((bf16[512,8,128]{2,1,0:T(8,128)(2,1)}), bf16[512,8,128]{2,1,0:T(8,128)(2,1)S(1)}, u32[]{:S(2)}, u32[]{:S(2)}) %all-to-all-start.2) | async-done | bytes 1048608 | tf_op jit(solution)/shard_map/all_to_all | solution.py:92
  122.1 0.6 gather_fusion.3
  122.7 2.9 %collective-permute-start.2 = (bf16[8,4,256]{2,1,0:T(4,128)(2,1)S(1)}, bf16[8,4,256]{2,1,0:T(4,128)(2,1)S(1)}, u32[]{:S(2)}, u32[]{:S(2)}) collective-permute-start(bf16[8,4,256]{2,1,0:T(4,128)(2,1)S(1)} %get-tuple-element.58), channel_id=1, source_target_pairs={{0,4},{4,8},{8,12},{12,16},{16,20},{20,24},{24,28},{28,32},{32,36}... | collective-permute-start | bytes 49160 | tf_op jit(solution)/shard_map/ppermute | solution.py:34
  125.6 1.9 %collective-permute-start.3 = (bf16[8,4,256]{2,1,0:T(4,128)(2,1)S(1)}, bf16[8,4,256]{2,1,0:T(4,128)(2,1)S(1)}, u32[]{:S(2)}, u32[]{:S(2)}) collective-permute-start(bf16[8,4,256]{2,1,0:T(4,128)(2,1)S(1)} %get-tuple-element.59), channel_id=1, source_target_pairs={{4,0},{8,4},{12,8},{16,12},{20,16},{24,20},{28,24},{32,28},{36,32}... | collective-permute-start | bytes 49160 | tf_op jit(solution)/shard_map/ppermute | solution.py:35
  127.6 0.6 gather_fusion.4
  128.2 0.1 copy.55
  128.2 0.1 reshape.68
  128.3 0.2 broadcast_multiply_fusion.2
  128.6 0.0 copy-done.2
  128.6 0.2 broadcast_multiply_fusion.1
  128.8 0.0 slice-start
  128.8 0.2 broadcast_multiply_fusion
  129.0 0.2 pad_slice_fusion.3
  129.2 0.3 slice-done
  129.5 0.1 fusion.18
  129.6 0.0 collective-permute-done.2
  129.7 1.0 collective-permute-done.3
  130.8 0.2 broadcast_multiply_fusion.8
  131.0 0.1 broadcast_multiply_fusion.7
  131.1 0.1 broadcast_multiply_fusion.4
  131.3 0.2 broadcast_multiply_fusion.3
  131.5 0.1 pad_slice_fusion.35
  131.6 0.1 pad_slice_fusion.19
  131.9 0.7 pad_maximum_fusion.1
  (31 shorter events, 0.4 us)
Async XLA Ops:
  1.7 29.9 %all-to-all-start = ((s32[128,1,128]{2,1,0:T(1,128)}), s32[128,1,128]{2,1,0:T(1,128)S(1)}, u32[]{:S(2)}, u32[]{:S(2)}) async-start(s32[128,1,128]{2,1,0:T(1,128)} %broadcast_in_dim.59), calls=%async_computation | async-start | bytes 131072 | tf_op jit(solution)/shard_map/all_to_all | solution.py:70
  33.4 9.0 %copy-start.1 = (f32[32,256]{1,0:T(8,128)S(1)}, f32[32,256]{1,0:T(8,128)}, u32[]{:S(2)}) copy-start(f32[32,256]{1,0:T(8,128)} %param.11) | copy-start | bytes 98308
  33.4 9.0 %copy-start.3 = (s32[32,256]{1,0:T(8,128)S(1)}, s32[32,256]{1,0:T(8,128)}, u32[]{:S(2)}) copy-start(s32[32,256]{1,0:T(8,128)} %param.10) | copy-start | bytes 98308
  33.4 16.7 %copy-start.4 = (bf16[16,2,128]{2,1,0:T(2,128)(2,1)S(1)}, bf16[16,2,128]{2,1,0:T(2,128)(2,1)}, u32[]{:S(2)}) copy-start(bf16[16,2,128]{2,1,0:T(2,128)(2,1)} %param.7) | copy-start | bytes 24580
  33.4 16.7 %copy-start = (bf16[16,2,99,128]{3,1,2,0:T(2,128)(2,1)S(1)}, bf16[16,2,99,128]{3,1,2,0:T(2,128)(2,1)}, u32[]{:S(2)}) copy-start(bf16[16,2,99,128]{3,1,2,0:T(2,128)(2,1)} %param.8) | copy-start | bytes 2433028
  33.4 41.8 %all-to-all-start.1 = ((bf16[512,8,128]{2,1,0:T(8,128)(2,1)}), bf16[512,8,128]{2,1,0:T(8,128)(2,1)S(1)}, u32[]{:S(2)}, u32[]{:S(2)}) async-start(bf16[512,8,128]{2,1,0:T(8,128)(2,1)} %bitcast.11), calls=%async_computation.1 | async-start | bytes 2097152 | tf_op jit(solution)/shard_map/all_to_all | solution.py:84
  42.4 10.0 %collective-permute-start = (f32[2,4,256]{2,1,0:T(4,128)S(1)}, f32[2,4,256]{2,1,0:T(4,128)S(1)}, u32[]{:S(2)}, u32[]{:S(2)}) collective-permute-start(f32[2,4,256]{2,1,0:T(4,128)S(1)} %get-tuple-element.50), channel_id=1, source_target_pairs={{0,4},{4,8},{8,12},{12,16},{16,20},{20,24},{24,28},{28,32},{32,36}... | collective-permute-start | bytes 24584 | tf_op jit(solution)/shard_map/ppermute | solution.py:34
  46.5 5.9 %collective-permute-start.1 = (f32[2,4,256]{2,1,0:T(4,128)S(1)}, f32[2,4,256]{2,1,0:T(4,128)S(1)}, u32[]{:S(2)}, u32[]{:S(2)}) collective-permute-start(f32[2,4,256]{2,1,0:T(4,128)S(1)} %get-tuple-element.51), channel_id=1, source_target_pairs={{4,0},{8,4},{12,8},{16,12},{20,16},{24,20},{28,24},{32,28},{36,32}... | collective-permute-start | bytes 24584 | tf_op jit(solution)/shard_map/ppermute | solution.py:35
  80.4 41.7 %all-to-all-start.2 = ((bf16[512,8,128]{2,1,0:T(8,128)(2,1)}), bf16[512,8,128]{2,1,0:T(8,128)(2,1)S(1)}, u32[]{:S(2)}, u32[]{:S(2)}) async-start(bf16[512,8,128]{2,1,0:T(8,128)(2,1)} %bitcast.13), calls=%async_computation.2 | async-start | bytes 2097152 | tf_op jit(solution)/shard_map/all_to_all | solution.py:92
  89.7 38.9 %copy-start.2 = (f32[40,256]{1,0:T(8,128)}, f32[40,256]{1,0:T(8,128)S(1)}, u32[]{:S(2)}) copy-start(f32[40,256]{1,0:T(8,128)S(1)} %compare_select_fusion) | copy-start | bytes 122884
  122.7 6.9 %collective-permute-start.2 = (bf16[8,4,256]{2,1,0:T(4,128)(2,1)S(1)}, bf16[8,4,256]{2,1,0:T(4,128)(2,1)S(1)}, u32[]{:S(2)}, u32[]{:S(2)}) collective-permute-start(bf16[8,4,256]{2,1,0:T(4,128)(2,1)S(1)} %get-tuple-element.58), channel_id=1, source_target_pairs={{0,4},{4,8},{8,12},{12,16},{16,20},{20,24},{24,28},{28,32},{32,36}... | collective-permute-start | bytes 49160 | tf_op jit(solution)/shard_map/ppermute | solution.py:34
  125.6 5.1 %collective-permute-start.3 = (bf16[8,4,256]{2,1,0:T(4,128)(2,1)S(1)}, bf16[8,4,256]{2,1,0:T(4,128)(2,1)S(1)}, u32[]{:S(2)}, u32[]{:S(2)}) collective-permute-start(bf16[8,4,256]{2,1,0:T(4,128)(2,1)S(1)} %get-tuple-element.59), channel_id=1, source_target_pairs={{4,0},{8,4},{12,8},{16,12},{20,16},{24,20},{28,24},{32,28},{36,32}... | collective-permute-start | bytes 49160 | tf_op jit(solution)/shard_map/ppermute | solution.py:35
  128.8 0.7 slice-start

commit v7 on v6

--- a/solution.py
+++ b/solution.py
@@ -64,7 +64,6 @@
     match = target[None, :] == tile_ids[:, None]
     has = jnp.any(match, axis=1)
     slot_table = jnp.where(has, jnp.sum(jnp.where(match, place_slot[None, :], 0), axis=1), owned)
-    local_of = jnp.sum(jnp.where(match, jnp.arange(served, dtype=jnp.int32)[None, :], 0), axis=1)
 
     lanes = 128
     recv_rows = lax.all_to_all(
@@ -87,7 +86,7 @@
 
     mapped_part = quantile_map(own_rows, knot_base, knot_steps)
 
-    packed = jnp.take(mapped_part, local_of, axis=0, mode="clip")
+    packed = arrived.at[target].set(mapped_part, unique_indices=True, mode="promise_in_bounds")
     packed = packed.reshape(ntiles * ndays, day_count, quarter)
     returned = lax.all_to_all(packed, ("tiles", "days"), 0, 0, tiled=True)
     returned = returned.reshape(ntiles, ndays, day_count, quarter)

time: 133 us -> 137 us (1.030); the launches traced: 133 us -> 135 us
  starting transfers between devices: 49 us -> 52.4 us
  waiting for transfers between devices: 66.3 us -> 63.2 us
  local copies, waits for them, and re-layouts: 9.73 us -> 11.5 us
    all_to_all x1, waiting for transfers between devices: 22.7 us -> 19.2 us  [body(): arrived = lax.all_to_all(outgoing, ('tiles', 'days'), 0, 0, tiled=True)]
    all_to_all x1, starting transfers between devices: 8.93 us -> 11.6 us  [body(): arrived = lax.all_to_all(outgoing, ('tiles', 'days'), 0, 0, tiled=True)]
    scatter x0 -> x1, local copies, waits for them, and re-layouts: none -> 2.21 us  [body(): arrived.at[target]]
    gather x1 -> x0, local copies, waits for them, and re-layouts: 1.67 us -> none  [body(): packed = jnp.take(mapped_part, local_of, axis=0, mode='clip')]
where the time goes in v7:
time: 137 us; the launch traced here: 135 us
  waiting for transfers between devices  63.2 us (46%)
  starting transfers between devices  52.4 us (38%)
  local copies, waits for them, and re-layouts  11.5 us (8%)
  other arithmetic  7.13 us (5%)
    all_to_all x1, waiting for transfers between devices, body(): returned = lax.all_to_all(packed, ('tiles', 'days'), 0, 0, tiled=True)  32.1 us
    all_to_all x1, waiting for transfers between devices, body(): arrived = lax.all_to_all(outgoing, ('tiles', 'days'), 0, 0, tiled=True)  19.2 us
    all_to_all x1, starting transfers between devices, body(): lax.all_to_all(jnp.broadcast_to(slot_table.astype(jnp.int32)[:, None], (n...  18.4 us
    all_to_all x1, starting transfers between devices, body(): arrived = lax.all_to_all(outgoing, ('tiles', 'days'), 0, 0, tiled=True)  11.6 us
    all_to_all x1, waiting for transfers between devices, body(): lax.all_to_all(jnp.broadcast_to(slot_table.astype(jnp.int32)[:, None], (n...  10.4 us
    all_to_all x1, starting transfers between devices, body(): returned = lax.all_to_all(packed, ('tiles', 'days'), 0, 0, tiled=True)  9.15 us
    ppermute x2, starting transfers between devices, with_halo(): lax.ppermute(tail, 'tiles', [(i, i + 1) for i in range(count - 1)])  7.49 us
    ppermute x2, starting transfers between devices, with_halo(): lax.ppermute(head, 'tiles', [(i + 1, i) for i in range(count - 1)])  5.78 us
  transfers between devices with their start and end apart: 7, of which 4 were waited for; matrix products, arithmetic and copies ran while one was open for 4% of the time, Pallas kernels for 0%

profile of v7, /device:TPU:1, one launch (start us, length us, event | category | flops | bytes accessed | tf_op | source)
XLA Modules:
  0.0 134.8 jit_solution(5901951482186022778)
XLA Ops:
  0.0 0.7 compare_select_fusion.1
  0.7 0.1 fusion.52
  0.8 0.1 select_reduce_fusion.1
  0.9 0.8 broadcast_in_dim.49
  1.7 18.4 %all-to-all-start = ((s32[128,1,128]{2,1,0:T(1,128)}), s32[128,1,128]{2,1,0:T(1,128)S(1)}, u32[]{:S(2)}, u32[]{:S(2)}) async-start(s32[128,1,128]{2,1,0:T(1,128)} %broadcast_in_dim.49), calls=%async_computation | async-start | bytes 131072 | tf_op jit(solution)/shard_map/all_to_all | solution.py:69
  20.2 0.9 reshape.62
  21.1 0.1 copy.48
  21.2 10.4 %all-to-all-done = s32[128,1,128]{2,1,0:T(1,128)S(1)} async-done(((s32[128,1,128]{2,1,0:T(1,128)}), s32[128,1,128]{2,1,0:T(1,128)S(1)}, u32[]{:S(2)}, u32[]{:S(2)}) %all-to-all-start) | async-done | bytes 65568 | tf_op jit(solution)/shard_map/all_to_all | solution.py:69
  31.6 0.1 fusion.51
  31.7 1.7 %gather_fusion = bf16[128,8,4,128]{3,1,2,0:T(8,128)(2,1)} fusion(bf16[8,16,4,128]{3,0,2,1:T(8,128)(2,1)S(1)} %copy.48, s32[1024]{0:T(1024)S(1)} %pad_clamp_fusion.3), kind=kCustom, calls=%fused_computation | custom fusion | bytes 2097664 | tf_op jit(solution)/shard_map/jit(_take)/gather | solution.py:81
  33.4 0.0 copy-start.1
  33.5 0.0 copy-start.3
  33.5 0.0 copy-start.4
  33.5 0.0 copy-start
  33.5 11.6 %all-to-all-start.1 = ((bf16[512,8,128]{2,1,0:T(8,128)(2,1)}), bf16[512,8,128]{2,1,0:T(8,128)(2,1)}, u32[]{:S(2)}, u32[]{:S(2)}) async-start(bf16[512,8,128]{2,1,0:T(8,128)(2,1)} %bitcast.5), calls=%async_computation.1 | async-start | bytes 2097152 | tf_op jit(solution)/shard_map/all_to_all | solution.py:83
  45.1 0.0 copy-done.1
  45.1 0.0 copy-done.3
  45.1 4.1 %collective-permute-start = (f32[2,4,256]{2,1,0:T(4,128)S(1)}, f32[2,4,256]{2,1,0:T(4,128)S(1)}, u32[]{:S(2)}, u32[]{:S(2)}) collective-permute-start(f32[2,4,256]{2,1,0:T(4,128)S(1)} %get-tuple-element.50), channel_id=1, source_target_pairs={{0,4},{4,8},{8,12},{12,16},{16,20},{20,24},{24,28},{28,32},{32,36}... | collective-permute-start | bytes 24584 | tf_op jit(solution)/shard_map/ppermute | solution.py:34
  49.2 3.6 %collective-permute-start.1 = (f32[2,4,256]{2,1,0:T(4,128)S(1)}, f32[2,4,256]{2,1,0:T(4,128)S(1)}, u32[]{:S(2)}, u32[]{:S(2)}) collective-permute-start(f32[2,4,256]{2,1,0:T(4,128)S(1)} %get-tuple-element.51), channel_id=1, source_target_pairs={{4,0},{8,4},{12,8},{16,12},{20,16},{24,20},{28,24},{32,28},{36,32}... | collective-permute-start | bytes 24584 | tf_op jit(solution)/shard_map/ppermute | solution.py:35
  52.8 0.0 copy-done.4
  52.9 0.0 copy-done
  52.9 1.1 fusion.73
  54.0 0.2 convert_divide_fusion
  54.2 0.1 broadcast_add_fusion
  54.3 0.2 multiply_reduce_fusion.1
  54.6 0.3 copy.53
  54.9 0.3 copy.52
  55.2 0.0 collective-permute-done
  55.2 1.5 %collective-permute-done.1 = f32[2,4,256]{2,1,0:T(4,128)S(1)} collective-permute-done((f32[2,4,256]{2,1,0:T(4,128)S(1)}, f32[2,4,256]{2,1,0:T(4,128)S(1)}, u32[]{:S(2)}, u32[]{:S(2)}) %collective-permute-start.1) | collective-permute-done | bytes 8224 | tf_op jit(solution)/shard_map/ppermute | solution.py:35
  56.7 19.2 %all-to-all-done.1 = bf16[512,8,128]{2,1,0:T(8,128)(2,1)} async-done(((bf16[512,8,128]{2,1,0:T(8,128)(2,1)}), bf16[512,8,128]{2,1,0:T(8,128)(2,1)}, u32[]{:S(2)}, u32[]{:S(2)}) %all-to-all-start.1) | async-done | bytes 1048608 | tf_op jit(solution)/shard_map/all_to_all | solution.py:83
  75.9 1.8 %gather_fusion.1 = bf16[16,32,128]{2,1,0:T(8,128)(2,1)S(1)} fusion(bf16[128,32,128]{2,1,0:T(8,128)(2,1)} %bitcast.6, s32[1024]{0:T(1024)S(1)} %pad_clamp_fusion.2), kind=kCustom, calls=%fused_computation.1 | custom fusion | bytes 262208 | tf_op jit(solution)/shard_map/jit(_take)/gather | solution.py:85
  77.7 2.9 %multiply_reduce_fusion = f32[16,32,128]{2,1,0:T(8,128)S(1)} fusion(f32[16,100,128]{2,1,0:T(8,128)S(1)} %copy.53, f32[16,32,128]{2,1,0:T(8,128)S(1)} %convert_element_type.62, f32[16,100,128]{2,1,0:T(8,128)S(1)} %copy.52), kind=kLoop, calls=%fused_computation.5 | loop fusion | flops 19595264 | bytes 2162688 | tf_op jit(solution)/shard_map/reduce_sum | solution.py:49
  80.7 2.2 %scatter_fusion = bf16[128,32,128]{2,1,0:T(8,128)(2,1)} fusion(bf16[128,32,128]{2,1,0:T(8,128)(2,1)} %bitcast.6, s32[16]{0:T(128)S(1)} %get-tuple-element.23, bf16[16,32,128]{2,1,0:T(8,128)(2,1)S(1)} %add_convert_fusion), kind=kCustom, calls=%fused_computation.4 | custom fusion | bytes 393280 | tf_op jit(solution)/shard_map/scatter | solution.py:89
  82.9 9.1 %all-to-all-start.2 = ((bf16[512,8,128]{2,1,0:T(8,128)(2,1)}), bf16[512,8,128]{2,1,0:T(8,128)(2,1)S(1)}, u32[]{:S(2)}, u32[]{:S(2)}) async-start(bf16[512,8,128]{2,1,0:T(8,128)(2,1)} %bitcast.13), calls=%async_computation.2 | async-start | bytes 2097152 | tf_op jit(solution)/shard_map/all_to_all | solution.py:91
  92.0 0.1 compare_select_fusion
  92.1 0.0 copy-start.2
  92.3 0.1 fusion.77
  92.4 0.1 pad_add_fusion
  92.5 32.1 %all-to-all-done.2 = bf16[512,8,128]{2,1,0:T(8,128)(2,1)S(1)} async-done(((bf16[512,8,128]{2,1,0:T(8,128)(2,1)}), bf16[512,8,128]{2,1,0:T(8,128)(2,1)S(1)}, u32[]{:S(2)}, u32[]{:S(2)}) %all-to-all-start.2) | async-done | bytes 1048608 | tf_op jit(solution)/shard_map/all_to_all | solution.py:91
  124.6 0.6 gather_fusion.2
  125.2 2.1 %collective-permute-start.3 = (bf16[8,4,256]{2,1,0:T(4,128)(2,1)S(1)}, bf16[8,4,256]{2,1,0:T(4,128)(2,1)S(1)}, u32[]{:S(2)}, u32[]{:S(2)}) collective-permute-start(bf16[8,4,256]{2,1,0:T(4,128)(2,1)S(1)} %get-tuple-element.59), channel_id=1, source_target_pairs={{4,0},{8,4},{12,8},{16,12},{20,16},{24,20},{28,24},{32,28},{36,32}... | collective-permute-start | bytes 49160 | tf_op jit(solution)/shard_map/ppermute | solution.py:35
  127.4 0.6 gather_fusion.3
  127.9 0.1 copy.55
  128.0 0.1 reshape.68
  128.1 3.4 %collective-permute-start.2 = (bf16[8,4,256]{2,1,0:T(4,128)(2,1)S(1)}, bf16[8,4,256]{2,1,0:T(4,128)(2,1)S(1)}, u32[]{:S(2)}, u32[]{:S(2)}) collective-permute-start(bf16[8,4,256]{2,1,0:T(4,128)(2,1)S(1)} %get-tuple-element.58), channel_id=1, source_target_pairs={{0,4},{4,8},{8,12},{12,16},{16,20},{20,24},{24,28},{28,32},{32,36}... | collective-permute-start | bytes 49160 | tf_op jit(solution)/shard_map/ppermute | solution.py:34
  131.5 0.2 broadcast_multiply_fusion.2
  131.8 0.0 copy-done.2
  131.8 0.2 broadcast_multiply_fusion.1
  132.0 0.0 slice-start
  132.0 0.2 broadcast_multiply_fusion
  132.2 0.2 pad_slice_fusion.3
  132.4 0.3 slice-done
  132.7 0.1 fusion.18
  132.9 0.0 collective-permute-done.3
  132.9 0.0 collective-permute-done.2
  132.9 0.2 broadcast_multiply_fusion.8
  133.1 0.1 broadcast_multiply_fusion.4
  133.3 0.1 broadcast_multiply_fusion.7
  133.4 0.2 broadcast_multiply_fusion.3
  133.7 0.1 pad_slice_fusion.19
  133.8 0.1 pad_slice_fusion.35
  134.0 0.7 pad_maximum_fusion.1
  (30 shorter events, 0.4 us)
Async XLA Ops:
  1.7 29.9 %all-to-all-start = ((s32[128,1,128]{2,1,0:T(1,128)}), s32[128,1,128]{2,1,0:T(1,128)S(1)}, u32[]{:S(2)}, u32[]{:S(2)}) async-start(s32[128,1,128]{2,1,0:T(1,128)} %broadcast_in_dim.49), calls=%async_computation | async-start | bytes 131072 | tf_op jit(solution)/shard_map/all_to_all | solution.py:69
  33.4 11.6 %copy-start.1 = (f32[32,256]{1,0:T(8,128)S(1)}, f32[32,256]{1,0:T(8,128)}, u32[]{:S(2)}) copy-start(f32[32,256]{1,0:T(8,128)} %param.11) | copy-start | bytes 98308
  33.5 11.6 %copy-start.3 = (s32[32,256]{1,0:T(8,128)S(1)}, s32[32,256]{1,0:T(8,128)}, u32[]{:S(2)}) copy-start(s32[32,256]{1,0:T(8,128)} %param.10) | copy-start | bytes 98308
  33.5 19.4 %copy-start.4 = (bf16[16,2,128]{2,1,0:T(2,128)(2,1)S(1)}, bf16[16,2,128]{2,1,0:T(2,128)(2,1)}, u32[]{:S(2)}) copy-start(bf16[16,2,128]{2,1,0:T(2,128)(2,1)} %param.7) | copy-start | bytes 24580
  33.5 19.4 %copy-start = (bf16[16,2,99,128]{3,1,2,0:T(2,128)(2,1)S(1)}, bf16[16,2,99,128]{3,1,2,0:T(2,128)(2,1)}, u32[]{:S(2)}) copy-start(bf16[16,2,99,128]{3,1,2,0:T(2,128)(2,1)} %param.8) | copy-start | bytes 2433028
  33.5 42.4 %all-to-all-start.1 = ((bf16[512,8,128]{2,1,0:T(8,128)(2,1)}), bf16[512,8,128]{2,1,0:T(8,128)(2,1)}, u32[]{:S(2)}, u32[]{:S(2)}) async-start(bf16[512,8,128]{2,1,0:T(8,128)(2,1)} %bitcast.5), calls=%async_computation.1 | async-start | bytes 2097152 | tf_op jit(solution)/shard_map/all_to_all | solution.py:83
  45.1 10.1 %collective-permute-start = (f32[2,4,256]{2,1,0:T(4,128)S(1)}, f32[2,4,256]{2,1,0:T(4,128)S(1)}, u32[]{:S(2)}, u32[]{:S(2)}) collective-permute-start(f32[2,4,256]{2,1,0:T(4,128)S(1)} %get-tuple-element.50), channel_id=1, source_target_pairs={{0,4},{4,8},{8,12},{12,16},{16,20},{20,24},{24,28},{28,32},{32,36}... | collective-permute-start | bytes 24584 | tf_op jit(solution)/shard_map/ppermute | solution.py:34
  49.2 7.5 %collective-permute-start.1 = (f32[2,4,256]{2,1,0:T(4,128)S(1)}, f32[2,4,256]{2,1,0:T(4,128)S(1)}, u32[]{:S(2)}, u32[]{:S(2)}) collective-permute-start(f32[2,4,256]{2,1,0:T(4,128)S(1)} %get-tuple-element.51), channel_id=1, source_target_pairs={{4,0},{8,4},{12,8},{16,12},{20,16},{24,20},{28,24},{32,28},{36,32}... | collective-permute-start | bytes 24584 | tf_op jit(solution)/shard_map/ppermute | solution.py:35
  82.9 41.7 %all-to-all-start.2 = ((bf16[512,8,128]{2,1,0:T(8,128)(2,1)}), bf16[512,8,128]{2,1,0:T(8,128)(2,1)S(1)}, u32[]{:S(2)}, u32[]{:S(2)}) async-start(bf16[512,8,128]{2,1,0:T(8,128)(2,1)} %bitcast.13), calls=%async_computation.2 | async-start | bytes 2097152 | tf_op jit(solution)/shard_map/all_to_all | solution.py:91
  92.1 39.6 %copy-start.2 = (f32[40,256]{1,0:T(8,128)}, f32[40,256]{1,0:T(8,128)S(1)}, u32[]{:S(2)}) copy-start(f32[40,256]{1,0:T(8,128)S(1)} %compare_select_fusion) | copy-start | bytes 122884
  125.2 7.7 %collective-permute-start.3 = (bf16[8,4,256]{2,1,0:T(4,128)(2,1)S(1)}, bf16[8,4,256]{2,1,0:T(4,128)(2,1)S(1)}, u32[]{:S(2)}, u32[]{:S(2)}) collective-permute-start(bf16[8,4,256]{2,1,0:T(4,128)(2,1)S(1)} %get-tuple-element.59), channel_id=1, source_target_pairs={{4,0},{8,4},{12,8},{16,12},{20,16},{24,20},{28,24},{32,28},{36,32}... | collective-permute-start | bytes 49160 | tf_op jit(solution)/shard_map/ppermute | solution.py:35
  128.1 4.8 %collective-permute-start.2 = (bf16[8,4,256]{2,1,0:T(4,128)(2,1)S(1)}, bf16[8,4,256]{2,1,0:T(4,128)(2,1)S(1)}, u32[]{:S(2)}, u32[]{:S(2)}) collective-permute-start(bf16[8,4,256]{2,1,0:T(4,128)(2,1)S(1)} %get-tuple-element.58), channel_id=1, source_target_pairs={{0,4},{4,8},{8,12},{12,16},{16,20},{20,24},{24,28},{28,32},{32,36}... | collective-permute-start | bytes 49160 | tf_op jit(solution)/shard_map/ppermute | solution.py:34
  132.0 0.7 slice-start

commit v8 on v7

--- a/solution.py
+++ b/solution.py
@@ -1,6 +1,8 @@
 import jax
 import jax.numpy as jnp
 from jax import lax
+from jax.experimental import pallas as pl
+from jax.experimental.pallas import tpu as pltpu
 from jax.sharding import PartitionSpec as P
 
 PASSES = 4
@@ -36,19 +38,64 @@
     return jnp.concatenate([from_above, cells, from_below], axis=-2)
 
 
-def quantile_map(values, anchor, increments):
-    step_x = increments[:, 0].astype(jnp.float32)
-    step_y = increments[:, 1].astype(jnp.float32)
-    ends = anchor[:, 0][:, None, :].astype(jnp.float32) + jnp.cumsum(step_x, axis=1)
-    position = jnp.concatenate([anchor[:, 0][:, None, :].astype(jnp.float32), ends], axis=1)
-    slopes = step_y / step_x
-    zero = jnp.zeros_like(slopes[:, :1])
-    bends = jnp.concatenate([slopes, zero], axis=1) - jnp.concatenate([zero, slopes], axis=1)
-    offset = anchor[:, 1].astype(jnp.float32) - jnp.sum(bends * position, axis=1)
-    above = jnp.maximum(values.astype(jnp.float32)[:, :, None, :], position[:, None])
-    total = jnp.sum(bends[:, None] * above, axis=2)
-    return (offset[:, None, :] + total).astype(jnp.bfloat16)
+def _qmap_kernel(tgt_ref, arrived_hbm, base_ref, steps_ref, out_hbm, vin, vout, sem_in, sem_out):
+    served = vin.shape[0]
+    knots = steps_ref.shape[2]
+    for k in range(served):
+        pltpu.make_async_copy(arrived_hbm.at[tgt_ref[k]], vin.at[k], sem_in.at[k]).start()
+    for k in range(served):
+        pltpu.make_async_copy(arrived_hbm.at[tgt_ref[k]], vin.at[k], sem_in.at[k]).wait()
 
+    def block(k, carry):
+        x = vin[k].astype(jnp.float32)
+        step_x = steps_ref[k, 0].astype(jnp.float32)
+        step_y = steps_ref[k, 1].astype(jnp.float32)
+        slopes = step_y / step_x
+        p = base_ref[k, 0:1, :].astype(jnp.float32)
+        offset = base_ref[k, 1:2, :].astype(jnp.float32)
+        acc = jnp.zeros_like(x)
+        before = jnp.zeros_like(p)
+        for j in range(knots + 1):
+            now = slopes[j : j + 1] if j < knots else jnp.zeros_like(p)
+            bend = now - before
+            acc = acc + bend * jnp.maximum(x, p)
+            offset = offset - bend * p
+            if j < knots:
+                p = p + step_x[j : j + 1]
+            before = now
+        vout[k] = (offset + acc).astype(vout.dtype)
+        return carry
+
+    lax.fori_loop(0, served, block, 0)
+    for k in range(served):
+        pltpu.make_async_copy(vout.at[k], out_hbm.at[tgt_ref[k]], sem_out.at[k]).start()
+    for k in range(served):
+        pltpu.make_async_copy(vout.at[k], out_hbm.at[tgt_ref[k]], sem_out.at[k]).wait()
+
+
+def mapped_rows(target, arrived, anchor, increments):
+    served = anchor.shape[0]
+    rows = arrived.shape[1:]
+    return pl.pallas_call(
+        _qmap_kernel,
+        grid_spec=pltpu.PrefetchScalarGridSpec(
+            num_scalar_prefetch=1,
+            grid=(1,),
+            in_specs=[
+                pl.BlockSpec(memory_space=pl.ANY),
+                pl.BlockSpec(anchor.shape, lambda i, t: (0, 0, 0)),
+                pl.BlockSpec(increments.shape, lambda i, t: (0, 0, 0, 0)),
+            ],
+            out_specs=pl.BlockSpec(memory_space=pl.ANY),
+            scratch_shapes=[
+                pltpu.VMEM((served,) + rows, arrived.dtype),
+                pltpu.VMEM((served,) + rows, jnp.bfloat16),
+                pltpu.SemaphoreType.DMA((served,)),
+                pltpu.SemaphoreType.DMA((served,)),
+            ],
+        ),
+        out_shape=jax.ShapeDtypeStruct(arrived.shape, jnp.bfloat16),
+    )(target, arrived, anchor, increments)
 
 def body(observed, knot_base, knot_steps, block_route, land_mask, terrain):
     day_count, row_count, columns = observed.shape
@@ -82,11 +129,7 @@
     outgoing = outgoing.transpose(1, 2, 0, 3).reshape(ntiles * ndays, day_count, quarter)
     arrived = lax.all_to_all(outgoing, ("tiles", "days"), 0, 0, tiled=True)
     arrived = arrived.reshape(ntiles, ndays * day_count, quarter)
-    own_rows = jnp.take(arrived, target, axis=0, mode="clip")
-
-    mapped_part = quantile_map(own_rows, knot_base, knot_steps)
-
-    packed = arrived.at[target].set(mapped_part, unique_indices=True, mode="promise_in_bounds")
+    packed = mapped_rows(target, arrived, knot_base, knot_steps)
     packed = packed.reshape(ntiles * ndays, day_count, quarter)
     returned = lax.all_to_all(packed, ("tiles", "days"), 0, 0, tiled=True)
     returned = returned.reshape(ntiles, ndays, day_count, quarter)

time: 137 us -> 139 us (1.015); the launches traced: 135 us -> 139 us
  Pallas kernels: 0 us -> 8.4 us
  waiting for transfers between devices: 63.2 us -> 67.9 us
  other arithmetic: 7.13 us -> 3.63 us
  starting transfers between devices: 52.4 us -> 49 us
  local copies, waits for them, and re-layouts: 11.5 us -> 9.35 us
    pallas_call x0 -> x1, Pallas kernels: none -> 8.4 us  [mapped_rows(): pl.pallas_call(_qmap_kernel, grid_spec=pltpu.PrefetchScalarGridSpec(num_s...]
    all_to_all x1, waiting for transfers between devices: 19.2 us -> 23.2 us  [body(): arrived = lax.all_to_all(outgoing, ('tiles', 'days'), 0, 0, tiled=True)]
    reduce_sum x2 -> x0, other arithmetic: 3.13 us -> none  [the longest x1 2.88 us: quantile_map(): total = jnp.sum(bends[:, None] * above, axis=2)]
    unnamed x10 -> x15, local copies, waits for them, and re-layouts: 0.02 us -> 2.95 us
    all_to_all x1, starting transfers between devices: 11.6 us -> 8.91 us  [body(): arrived = lax.all_to_all(outgoing, ('tiles', 'days'), 0, 0, tiled=True)]
    scatter x1 -> x0, local copies, waits for them, and re-layouts: 2.21 us -> none  [body(): arrived.at[target]]
    gather x1 -> x0, local copies, waits for them, and re-layouts: 1.8 us -> none  [body(): own_rows = jnp.take(arrived, target, axis=0, mode='clip')]
  transfers between devices with their start and end apart: 7 -> 7, of which waited for: 4 -> 5; matrix products, arithmetic and copies ran while one was open for 4% -> 2% of each run, Pallas kernels for 0% -> 0%
where the time goes in v8:
time: 139 us
  waiting for transfers between devices  67.9 us (49%)
  starting transfers between devices  49 us (35%)
  local copies, waits for them, and re-layouts  9.35 us (7%)
  Pallas kernels  8.4 us (6%)
  other arithmetic  3.63 us (3%)
    all_to_all x1, waiting for transfers between devices, body(): returned = lax.all_to_all(packed, ('tiles', 'days'), 0, 0, tiled=True)  31.6 us
    all_to_all x1, waiting for transfers between devices, body(): arrived = lax.all_to_all(outgoing, ('tiles', 'days'), 0, 0, tiled=True)  23.2 us
    all_to_all x1, starting transfers between devices, body(): lax.all_to_all(jnp.broadcast_to(slot_table.astype(jnp.int32)[:, None], (n...  18.4 us
    all_to_all x1, waiting for transfers between devices, body(): lax.all_to_all(jnp.broadcast_to(slot_table.astype(jnp.int32)[:, None], (n...  11.4 us
    all_to_all x1, starting transfers between devices, body(): returned = lax.all_to_all(packed, ('tiles', 'days'), 0, 0, tiled=True)  9.18 us
    all_to_all x1, starting transfers between devices, body(): arrived = lax.all_to_all(outgoing, ('tiles', 'days'), 0, 0, tiled=True)  8.91 us
    pallas_call x1, Pallas kernels, mapped_rows(): pl.pallas_call(_qmap_kernel, grid_spec=pltpu.PrefetchScalarGridSpec(num_s...  8.4 us
    ppermute x2, starting transfers between devices, with_halo(): lax.ppermute(tail, 'tiles', [(i, i + 1) for i in range(count - 1)])  6.97 us
  transfers between devices with their start and end apart: 7, of which 5 were waited for; matrix products, arithmetic and copies ran while one was open for 2% of the time, Pallas kernels for 0%

profile of v8, /device:TPU:1, one launch (start us, length us, event | category | flops | bytes accessed | tf_op | source)
XLA Modules:
  0.0 138.7 jit_solution(16760791429720959668)
XLA Ops:
  0.0 0.0 copy-start.4
  0.0 0.7 and_select_fusion
  0.7 0.0 copy-start.6
  0.7 0.1 fusion.48
  0.8 0.4 copy-done.6
  1.2 0.1 select_reduce_fusion.1
  1.3 0.8 broadcast_in_dim.43
  2.2 18.4 %all-to-all-start = ((s32[128,1,128]{2,1,0:T(1,128)}), s32[128,1,128]{2,1,0:T(1,128)S(1)}, u32[]{:S(2)}, u32[]{:S(2)}) async-start(s32[128,1,128]{2,1,0:T(1,128)} %broadcast_in_dim.43), calls=%async_computation | async-start | bytes 131072 | tf_op jit(solution)/shard_map/all_to_all | solution.py:116
  20.6 0.0 copy-done.4
  20.6 11.4 %all-to-all-done = s32[128,1,128]{2,1,0:T(1,128)S(1)} async-done(((s32[128,1,128]{2,1,0:T(1,128)}), s32[128,1,128]{2,1,0:T(1,128)S(1)}, u32[]{:S(2)}, u32[]{:S(2)}) %all-to-all-start) | async-done | bytes 65568 | tf_op jit(solution)/shard_map/all_to_all | solution.py:116
  32.1 0.1 fusion.47
  32.2 1.9 %gather_fusion = bf16[128,8,4,128]{3,2,1,0:T(4,128)(2,1)S(1)} fusion(bf16[8,16,4,128]{3,2,1,0:T(4,128)(2,1)S(1)} %reshape.52, s32[1024]{0:T(1024)S(1)} %pad_clamp_fusion.2), kind=kCustom, calls=%fused_computation | custom fusion | bytes 2097664 | tf_op jit(solution)/shard_map/jit(_take)/gather | solution.py:128
  34.1 1.2 copy.19
  35.3 0.0 copy-start.2
  35.3 0.0 copy-start.5
  35.3 0.0 copy-start.1
  35.3 8.9 %all-to-all-start.1 = ((bf16[512,8,128]{2,1,0:T(8,128)(2,1)}), bf16[512,8,128]{2,1,0:T(8,128)(2,1)S(1)}, u32[]{:S(2)}, u32[]{:S(2)}) async-start(bf16[512,8,128]{2,1,0:T(8,128)(2,1)} %bitcast.5), calls=%async_computation.1 | async-start | bytes 2097152 | tf_op jit(solution)/shard_map/all_to_all | solution.py:130
  44.2 0.0 copy-done.2
  44.2 0.0 copy-done.5
  44.2 4.1 %collective-permute-start = (f32[2,4,256]{2,1,0:T(4,128)S(1)}, f32[2,4,256]{2,1,0:T(4,128)S(1)}, u32[]{:S(2)}, u32[]{:S(2)}) collective-permute-start(f32[2,4,256]{2,1,0:T(4,128)S(1)} %get-tuple-element.43), channel_id=1, source_target_pairs={{0,4},{4,8},{8,12},{12,16},{16,20},{20,24},{24,28},{28,32},{32,36}... | collective-permute-start | bytes 24584 | tf_op jit(solution)/shard_map/ppermute | solution.py:36
  48.3 3.6 %collective-permute-start.1 = (f32[2,4,256]{2,1,0:T(4,128)S(1)}, f32[2,4,256]{2,1,0:T(4,128)S(1)}, u32[]{:S(2)}, u32[]{:S(2)}) collective-permute-start(f32[2,4,256]{2,1,0:T(4,128)S(1)} %get-tuple-element.44), channel_id=1, source_target_pairs={{4,0},{8,4},{12,8},{16,12},{20,16},{24,20},{28,24},{32,28},{36,32}... | collective-permute-start | bytes 24584 | tf_op jit(solution)/shard_map/ppermute | solution.py:37
  51.9 0.0 copy-done.1
  51.9 1.0 copy.20.steps_ref
  52.9 0.0 collective-permute-done
  52.9 0.8 collective-permute-done.1
  53.8 23.2 %all-to-all-done.1 = bf16[512,8,128]{2,1,0:T(8,128)(2,1)S(1)} async-done(((bf16[512,8,128]{2,1,0:T(8,128)(2,1)}), bf16[512,8,128]{2,1,0:T(8,128)(2,1)S(1)}, u32[]{:S(2)}, u32[]{:S(2)}) %all-to-all-start.1) | async-done | bytes 1048608 | tf_op jit(solution)/shard_map/all_to_all | solution.py:130
  77.0 0.0 copy-start
  77.0 1.0 copy-done
  78.0 8.4 %shard_map.64 = bf16[128,32,128]{2,1,0:T(8,128)(2,1)} custom-call(s32[16]{0:T(128)} %copy-done.6, bf16[128,32,128]{2,1,0:T(8,128)(2,1)} %bitcast.25, bf16[16,2,128]{2,1,0:T(2,128)(2,1)} %base_ref.1, bf16[16,2,99,128]{3,2,1,0:T(8,128)(2,1)} %copy.20.steps_ref), custom_call_target="tpu_custom_call" | custom-call | tf_op jit(solution)/shard_map/pallas_call | solution.py:79
  86.4 9.2 %all-to-all-start.2 = ((bf16[512,8,128]{2,1,0:T(8,128)(2,1)}), bf16[512,8,128]{2,1,0:T(8,128)(2,1)S(1)}, u32[]{:S(2)}, u32[]{:S(2)}) async-start(bf16[512,8,128]{2,1,0:T(8,128)(2,1)} %bitcast.24), calls=%async_computation.2 | async-start | bytes 2097152 | tf_op jit(solution)/shard_map/all_to_all | solution.py:134
  95.6 0.1 compare_select_fusion
  95.7 0.0 copy-start.3
  95.8 0.5 copy-done.3
  96.4 0.1 fusion.71
  96.5 0.1 pad_add_fusion
  96.6 31.6 %all-to-all-done.2 = bf16[512,8,128]{2,1,0:T(8,128)(2,1)S(1)} async-done(((bf16[512,8,128]{2,1,0:T(8,128)(2,1)}), bf16[512,8,128]{2,1,0:T(8,128)(2,1)S(1)}, u32[]{:S(2)}, u32[]{:S(2)}) %all-to-all-start.2) | async-done | bytes 1048608 | tf_op jit(solution)/shard_map/all_to_all | solution.py:134
  128.1 0.6 gather_fusion.1
  128.8 2.9 %collective-permute-start.2 = (bf16[8,4,256]{2,1,0:T(4,128)(2,1)S(1)}, bf16[8,4,256]{2,1,0:T(4,128)(2,1)S(1)}, u32[]{:S(2)}, u32[]{:S(2)}) collective-permute-start(bf16[8,4,256]{2,1,0:T(4,128)(2,1)S(1)} %get-tuple-element.51), channel_id=1, source_target_pairs={{0,4},{4,8},{8,12},{12,16},{16,20},{20,24},{24,28},{28,32},{32,36}... | collective-permute-start | bytes 49160 | tf_op jit(solution)/shard_map/ppermute | solution.py:36
  131.7 1.9 %collective-permute-start.3 = (bf16[8,4,256]{2,1,0:T(4,128)(2,1)S(1)}, bf16[8,4,256]{2,1,0:T(4,128)(2,1)S(1)}, u32[]{:S(2)}, u32[]{:S(2)}) collective-permute-start(bf16[8,4,256]{2,1,0:T(4,128)(2,1)S(1)} %get-tuple-element.52), channel_id=1, source_target_pairs={{4,0},{8,4},{12,8},{16,12},{20,16},{24,20},{28,24},{32,28},{36,32}... | collective-permute-start | bytes 49160 | tf_op jit(solution)/shard_map/ppermute | solution.py:37
  133.6 0.6 gather_fusion.2
  134.2 0.1 copy.22
  134.3 0.1 reshape.58
  134.4 0.2 broadcast_multiply_fusion.2
  134.6 0.2 broadcast_multiply_fusion.1
  134.8 0.2 broadcast_multiply_fusion
  135.0 0.0 slice-start
  135.0 0.2 pad_slice_fusion.3
  135.3 0.5 slice-done
  135.8 0.1 fusion.16
  135.9 0.0 collective-permute-done.2
  135.9 0.8 collective-permute-done.3
  136.8 0.2 broadcast_multiply_fusion.8
  137.0 0.1 broadcast_multiply_fusion.7
  137.2 0.1 broadcast_multiply_fusion.4
  137.3 0.2 broadcast_multiply_fusion.3
  137.5 0.1 pad_slice_fusion.35
  137.7 0.1 pad_slice_fusion.19
  137.8 0.1 fusion.56
  137.9 0.7 pad_maximum_fusion
  (25 shorter events, 0.3 us)
Async XLA Ops:
  0.0 20.6 %copy-start.4 = (bf16[8,32,256]{2,1,0:T(8,128)(2,1)S(1)}, bf16[8,32,256]{2,1,0:T(8,128)(2,1)}, u32[]{:S(2)}) copy-start(bf16[8,32,256]{2,1,0:T(8,128)(2,1)} %param.6) | copy-start | bytes 393220
  0.7 0.5 copy-start.6
  2.2 29.9 %all-to-all-start = ((s32[128,1,128]{2,1,0:T(1,128)}), s32[128,1,128]{2,1,0:T(1,128)S(1)}, u32[]{:S(2)}, u32[]{:S(2)}) async-start(s32[128,1,128]{2,1,0:T(1,128)} %broadcast_in_dim.43), calls=%async_computation | async-start | bytes 131072 | tf_op jit(solution)/shard_map/all_to_all | solution.py:116
  35.3 8.9 %copy-start.2 = (f32[32,256]{1,0:T(8,128)S(1)}, f32[32,256]{1,0:T(8,128)}, u32[]{:S(2)}) copy-start(f32[32,256]{1,0:T(8,128)} %param.11) | copy-start | bytes 98308
  35.3 8.9 %copy-start.5 = (s32[32,256]{1,0:T(8,128)S(1)}, s32[32,256]{1,0:T(8,128)}, u32[]{:S(2)}) copy-start(s32[32,256]{1,0:T(8,128)} %param.10) | copy-start | bytes 98308
  35.3 16.6 %copy-start.1 = (bf16[16,2,99,128]{3,1,2,0:T(2,128)(2,1)S(1)}, bf16[16,2,99,128]{3,1,2,0:T(2,128)(2,1)}, u32[]{:S(2)}) copy-start(bf16[16,2,99,128]{3,1,2,0:T(2,128)(2,1)} %param.8) | copy-start | bytes 2433028
  35.3 41.7 %all-to-all-start.1 = ((bf16[512,8,128]{2,1,0:T(8,128)(2,1)}), bf16[512,8,128]{2,1,0:T(8,128)(2,1)S(1)}, u32[]{:S(2)}, u32[]{:S(2)}) async-start(bf16[512,8,128]{2,1,0:T(8,128)(2,1)} %bitcast.5), calls=%async_computation.1 | async-start | bytes 2097152 | tf_op jit(solution)/shard_map/all_to_all | solution.py:130
  44.2 8.7 %collective-permute-start = (f32[2,4,256]{2,1,0:T(4,128)S(1)}, f32[2,4,256]{2,1,0:T(4,128)S(1)}, u32[]{:S(2)}, u32[]{:S(2)}) collective-permute-start(f32[2,4,256]{2,1,0:T(4,128)S(1)} %get-tuple-element.43), channel_id=1, source_target_pairs={{0,4},{4,8},{8,12},{12,16},{16,20},{20,24},{24,28},{28,32},{32,36}... | collective-permute-start | bytes 24584 | tf_op jit(solution)/shard_map/ppermute | solution.py:36
  48.3 5.5 %collective-permute-start.1 = (f32[2,4,256]{2,1,0:T(4,128)S(1)}, f32[2,4,256]{2,1,0:T(4,128)S(1)}, u32[]{:S(2)}, u32[]{:S(2)}) collective-permute-start(f32[2,4,256]{2,1,0:T(4,128)S(1)} %get-tuple-element.44), channel_id=1, source_target_pairs={{4,0},{8,4},{12,8},{16,12},{20,16},{24,20},{28,24},{32,28},{36,32}... | collective-permute-start | bytes 24584 | tf_op jit(solution)/shard_map/ppermute | solution.py:37
  77.0 1.0 copy-start
  86.4 41.7 %all-to-all-start.2 = ((bf16[512,8,128]{2,1,0:T(8,128)(2,1)}), bf16[512,8,128]{2,1,0:T(8,128)(2,1)S(1)}, u32[]{:S(2)}, u32[]{:S(2)}) async-start(bf16[512,8,128]{2,1,0:T(8,128)(2,1)} %bitcast.24), calls=%async_computation.2 | async-start | bytes 2097152 | tf_op jit(solution)/shard_map/all_to_all | solution.py:134
  95.7 0.6 copy-start.3
  128.8 7.1 %collective-permute-start.2 = (bf16[8,4,256]{2,1,0:T(4,128)(2,1)S(1)}, bf16[8,4,256]{2,1,0:T(4,128)(2,1)S(1)}, u32[]{:S(2)}, u32[]{:S(2)}) collective-permute-start(bf16[8,4,256]{2,1,0:T(4,128)(2,1)S(1)} %get-tuple-element.51), channel_id=1, source_target_pairs={{0,4},{4,8},{8,12},{12,16},{16,20},{20,24},{24,28},{28,32},{32,36}... | collective-permute-start | bytes 49160 | tf_op jit(solution)/shard_map/ppermute | solution.py:36
  131.7 5.1 %collective-permute-start.3 = (bf16[8,4,256]{2,1,0:T(4,128)(2,1)S(1)}, bf16[8,4,256]{2,1,0:T(4,128)(2,1)S(1)}, u32[]{:S(2)}, u32[]{:S(2)}) collective-permute-start(bf16[8,4,256]{2,1,0:T(4,128)(2,1)S(1)} %get-tuple-element.52), channel_id=1, source_target_pairs={{4,0},{8,4},{12,8},{16,12},{20,16},{24,20},{28,24},{32,28},{36,32}... | collective-permute-start | bytes 49160 | tf_op jit(solution)/shard_map/ppermute | solution.py:37
  135.0 0.7 slice-start

commit v9 on v6

--- a/solution.py
+++ b/solution.py
@@ -72,30 +72,40 @@
         "tiles", 0, 0, tiled=True,
     )
 
+    knots = jnp.concatenate([knot_base[:, :, None, :], knot_steps], axis=2)
+    knots = lax.all_to_all(
+        jnp.broadcast_to(knots[None], (ndays,) + knots.shape), "days", 0, 0, tiled=True
+    )
+    anchors = knots[:, :, :, 0, :]
+    quarters = knots[:, :, :, 1:, :]
+
     picked = jnp.minimum(recv_rows[:, 0], owned - 1)
     slot_ids = jnp.arange(owned, dtype=jnp.int32)
     holder = jnp.sum(
         jnp.where(recv_rows[:, :owned] == slot_ids[None, :], tile_ids[:, None], 0), axis=0
     )
 
-    local = observed.reshape(day_count, owned, ndays, quarter)
-    outgoing = jnp.take(local, picked, axis=1, mode="clip")
-    outgoing = outgoing.transpose(1, 2, 0, 3).reshape(ntiles * ndays, day_count, quarter)
-    arrived = lax.all_to_all(outgoing, ("tiles", "days"), 0, 0, tiled=True)
-    arrived = arrived.reshape(ntiles, ndays * day_count, quarter)
+    local = observed.reshape(day_count, owned, 2 * columns)
+    outgoing = jnp.take(local, picked, axis=1, mode="clip").transpose(1, 0, 2)
+    arrived = lax.all_to_all(outgoing, "tiles", 0, 0, tiled=True)
     own_rows = jnp.take(arrived, target, axis=0, mode="clip")
+    own_rows = own_rows.reshape(served, day_count, ndays, quarter).transpose(2, 0, 1, 3)
 
-    mapped_part = quantile_map(own_rows, knot_base, knot_steps)
+    mapped_part = quantile_map(
+        own_rows.reshape(ndays * served, day_count, quarter),
+        anchors.reshape(ndays * served, 2, quarter),
+        quarters.reshape((ndays * served,) + knot_steps.shape[1:]),
+    )
+    mapped_part = mapped_part.reshape(ndays, served, day_count, quarter).transpose(1, 2, 0, 3)
+    mapped_part = mapped_part.reshape(served, day_count, 2 * columns)
 
     packed = jnp.take(mapped_part, local_of, axis=0, mode="clip")
-    packed = packed.reshape(ntiles * ndays, day_count, quarter)
-    returned = lax.all_to_all(packed, ("tiles", "days"), 0, 0, tiled=True)
-    returned = returned.reshape(ntiles, ndays, day_count, quarter)
+    returned = lax.all_to_all(packed, "tiles", 0, 0, tiled=True)
     blocks = jnp.take(returned, holder, axis=0, mode="clip")
-    mapped = blocks.transpose(2, 0, 1, 3).reshape(day_count, row_count, columns)
+    mapped = blocks.transpose(1, 0, 2).reshape(day_count, row_count, columns)
     edge_count = PASSES // 2
     edges = jnp.concatenate([holder[:edge_count], holder[owned - edge_count :]])
-    edge_rows = jnp.take(returned, edges, axis=0, mode="clip").transpose(2, 0, 1, 3)
+    edge_rows = jnp.take(returned, edges, axis=0, mode="clip").transpose(1, 0, 2)
     edge_rows = edge_rows.reshape(day_count, 2 * PASSES, columns)
 
     depth = PASSES

time: 133 us -> 179 us (1.35)
  waiting for transfers between devices: 66.3 us -> 97.4 us
  local copies, waits for them, and re-layouts: 9.73 us -> 17.3 us
  other arithmetic: 7.14 us -> 13.7 us
    all_to_all x2 -> x3, waiting for transfers between devices: 54.8 us -> 83.6 us  [the longest x1 30 us: body(): returned = lax.all_to_all(packed, 'tiles', 0, 0, tiled=True)]
    ppermute x2, waiting for transfers between devices: 1.05 us -> 3.39 us  [with_halo(): lax.ppermute(head, 'tiles', [(i + 1, i) for i in range(count - 1)])]
    broadcast_in_dim x0 -> x1, local copies, waits for them, and re-layouts: none -> 2.09 us  [body(): jnp.broadcast_to(knots[None], (ndays,) + knots.shape)]
    all_to_all x2 -> x3, starting transfers between devices: 18.1 us -> 19.2 us  [the longest x1 9.37 us: body(): returned = lax.all_to_all(packed, 'tiles', 0, 0, tiled=True)]
  transfers between devices with their start and end apart: 7 -> 8, of which waited for: 4 -> 6; matrix products, arithmetic and copies ran while one was open for 4% -> 5% of each run, Pallas kernels for 0% -> 0%
where the time goes in v9:
time: 179 us; the launch traced here: 178 us
  waiting for transfers between devices  97.4 us (54%)
  starting transfers between devices  49.5 us (28%)
  local copies, waits for them, and re-layouts  17.3 us (10%)
  other arithmetic  13.7 us (8%)
    all_to_all x1, waiting for transfers between devices, body(): returned = lax.all_to_all(packed, 'tiles', 0, 0, tiled=True)  30 us
    all_to_all x1, waiting for transfers between devices, body(): arrived = lax.all_to_all(outgoing, 'tiles', 0, 0, tiled=True)  29.2 us
    all_to_all x1, waiting for transfers between devices, body(): lax.all_to_all(jnp.broadcast_to(knots[None], (ndays,) + knots.shape), 'da...  24.5 us
    all_to_all x1, starting transfers between devices, body(): lax.all_to_all(jnp.broadcast_to(slot_table.astype(jnp.int32)[:, None], (n...  18.4 us
    all_to_all x1, waiting for transfers between devices, body(): lax.all_to_all(jnp.broadcast_to(slot_table.astype(jnp.int32)[:, None], (n...  10.4 us
    all_to_all x1, starting transfers between devices, body(): returned = lax.all_to_all(packed, 'tiles', 0, 0, tiled=True)  9.37 us
    ppermute x2, starting transfers between devices, with_halo(): lax.ppermute(tail, 'tiles', [(i, i + 1) for i in range(count - 1)])  7.77 us
    all_to_all x1, starting transfers between devices, body(): arrived = lax.all_to_all(outgoing, 'tiles', 0, 0, tiled=True)  5.73 us
  transfers between devices with their start and end apart: 8, of which 6 were waited for; matrix products, arithmetic and copies ran while one was open for 5% of the time, Pallas kernels for 0%

profile of v9, /device:TPU:1, one launch (start us, length us, event | category | flops | bytes accessed | tf_op | source)
XLA Modules:
  0.0 178.4 jit_solution(13680692099481957104)
XLA Ops:
  0.0 0.7 and_select_fusion
  0.7 0.1 fusion.53
  0.9 0.1 select_reduce_fusion.1
  1.0 0.8 broadcast_in_dim.64
  1.8 18.4 %all-to-all-start.1 = ((s32[128,1,128]{2,1,0:T(1,128)}), s32[128,1,128]{2,1,0:T(1,128)S(1)}, u32[]{:S(2)}, u32[]{:S(2)}) async-start(s32[128,1,128]{2,1,0:T(1,128)} %broadcast_in_dim.64), calls=%async_computation.1 | async-start | bytes 131072 | tf_op jit(solution)/shard_map/all_to_all | solution.py:70
  20.3 1.0 reshape.70
  21.2 0.1 copy.47
  21.3 10.4 %all-to-all-done.1 = s32[128,1,128]{2,1,0:T(1,128)S(1)} async-done(((s32[128,1,128]{2,1,0:T(1,128)}), s32[128,1,128]{2,1,0:T(1,128)S(1)}, u32[]{:S(2)}, u32[]{:S(2)}) %all-to-all-start.1) | async-done | bytes 65568 | tf_op jit(solution)/shard_map/all_to_all | solution.py:70
  31.7 0.1 fusion.52
  31.8 1.6 gather_fusion
  33.5 5.7 %all-to-all-start.2 = ((bf16[128,8,512]{2,1,0:T(8,128)(2,1)}), bf16[128,8,512]{2,1,0:T(8,128)(2,1)S(1)}, u32[]{:S(2)}, u32[]{:S(2)}) async-start(bf16[128,8,512]{2,1,0:T(8,128)(2,1)} %gather_fusion), calls=%async_computation.2 | async-start | bytes 2097152 | tf_op jit(solution)/shard_map/all_to_all | solution.py:90
  39.2 0.0 copy-done.6
  39.2 0.0 copy-done.2
  39.2 1.1 pad_maximum_fusion.1
  40.3 0.1 copy.43
  40.4 29.2 %all-to-all-done.2 = bf16[128,8,512]{2,1,0:T(8,128)(2,1)S(1)} async-done(((bf16[128,8,512]{2,1,0:T(8,128)(2,1)}), bf16[128,8,512]{2,1,0:T(8,128)(2,1)S(1)}, u32[]{:S(2)}, u32[]{:S(2)}) %all-to-all-start.2) | async-done | bytes 1048608 | tf_op jit(solution)/shard_map/all_to_all | solution.py:90
  69.6 2.1 %broadcast_in_dim.60 = bf16[4,16,2,100,128]{4,1,3,2,0:T(8,128)(2,1)} broadcast(bf16[16,2,100,128]{3,0,2,1:T(8,128)(2,1)S(1)} %copy.43), dimensions={1,2,3,4} | broadcast | bytes 4096000 | tf_op jit(solution)/shard_map/broadcast_in_dim | solution.py:77
  71.7 4.1 %all-to-all-start = ((bf16[4,16,2,100,128]{4,1,3,2,0:T(8,128)(2,1)}), bf16[4,16,2,100,128]{4,1,3,2,0:T(8,128)(2,1)S(1)}, u32[]{:S(2)}, u32[]{:S(2)}) async-start(bf16[4,16,2,100,128]{4,1,3,2,0:T(8,128)(2,1)} %broadcast_in_dim.60), calls=%async_computation | async-start | bytes 6553600 | tf_op jit(solution)/shard_map/all_to_all | solution.py:76
  75.8 0.0 copy-done.3
  75.9 4.0 %collective-permute-start = (f32[2,4,256]{2,1,0:T(4,128)S(1)}, f32[2,4,256]{2,1,0:T(4,128)S(1)}, u32[]{:S(2)}, u32[]{:S(2)}) collective-permute-start(f32[2,4,256]{2,1,0:T(4,128)S(1)} %get-tuple-element.48), channel_id=1, source_target_pairs={{0,4},{4,8},{8,12},{12,16},{16,20},{20,24},{24,28},{28,32},{32,36}... | collective-permute-start | bytes 24584 | tf_op jit(solution)/shard_map/ppermute | solution.py:34
  79.8 2.1 %collective-permute-start.1 = (f32[2,4,256]{2,1,0:T(4,128)S(1)}, f32[2,4,256]{2,1,0:T(4,128)S(1)}, u32[]{:S(2)}, u32[]{:S(2)}) collective-permute-start(f32[2,4,256]{2,1,0:T(4,128)S(1)} %get-tuple-element.49), channel_id=1, source_target_pairs={{4,0},{8,4},{12,8},{16,12},{20,16},{24,20},{28,24},{32,28},{36,32}... | collective-permute-start | bytes 24584 | tf_op jit(solution)/shard_map/ppermute | solution.py:35
  81.9 0.6 pad_clamp_fusion.3
  82.5 0.6 pad_clamp_fusion.2
  83.1 0.0 collective-permute-done
  83.1 2.0 %collective-permute-done.1 = f32[2,4,256]{2,1,0:T(4,128)S(1)} collective-permute-done((f32[2,4,256]{2,1,0:T(4,128)S(1)}, f32[2,4,256]{2,1,0:T(4,128)S(1)}, u32[]{:S(2)}, u32[]{:S(2)}) %collective-permute-start.1) | collective-permute-done | bytes 8224 | tf_op jit(solution)/shard_map/ppermute | solution.py:35
  85.1 0.6 pad_maximum_fusion.3
  85.8 1.9 %gather_fusion.1 = bf16[16,8,512]{2,1,0:T(8,128)(2,1)S(1)} fusion(bf16[128,8,512]{2,1,0:T(8,128)(2,1)} %copy-done, s32[1024]{0:T(1024)} %pad_clamp_fusion.3), kind=kCustom, calls=%fused_computation.1 | custom fusion | bytes 262208 | tf_op jit(solution)/shard_map/jit(_take)/gather | solution.py:91
  87.7 0.7 copy.48
  88.4 24.5 %all-to-all-done = bf16[4,16,2,100,128]{4,1,3,2,0:T(8,128)(2,1)S(1)} async-done(((bf16[4,16,2,100,128]{4,1,3,2,0:T(8,128)(2,1)}), bf16[4,16,2,100,128]{4,1,3,2,0:T(8,128)(2,1)S(1)}, u32[]{:S(2)}, u32[]{:S(2)}) %all-to-all-start) | async-done | bytes 3276832 | tf_op jit(solution)/shard_map/all_to_all | solution.py:76
  112.9 0.6 slice.361
  113.5 1.0 copy.45
  114.4 0.6 convert_divide_fusion
  115.1 0.4 broadcast_add_fusion
  115.5 1.5 multiply_reduce_fusion.1
  117.0 1.9 %copy.46 = f32[64,100,128]{2,1,0:T(8,128)S(1)} copy(f32[64,100,128]{2,0,1:T(8,128)S(1)} %get-tuple-element.27) | data formatting | bytes 6553600 | tf_op jit(solution)/shard_map/sub | solution.py:46
  118.9 0.0 copy-start.1
  118.9 1.9 %copy.49 = f32[64,100,128]{2,1,0:T(8,128)S(1)} copy(f32[64,100,128]{2,0,1:T(8,128)S(1)} %get-tuple-element.26) | data formatting | bytes 6553600 | tf_op jit(solution)/shard_map/concatenate | solution.py:43
  120.9 4.5 %multiply_reduce_fusion = f32[64,8,128]{2,1,0:T(8,128)S(1)} fusion(f32[64,100,128]{2,1,0:T(8,128)S(1)} %copy.49, f32[64,8,128]{2,1,0:T(8,128)S(1)} %bitcast.59, f32[64,100,128]{2,1,0:T(8,128)S(1)} %copy.46), kind=kLoop, calls=%fused_computation.5 | loop fusion | flops 19595264 | bytes 7077888 | tf_op jit(solution)/shard_map/reduce_sum | solution.py:49
  125.4 1.7 gather_fusion.2
  127.2 9.4 %all-to-all-start.3 = ((bf16[128,8,512]{2,1,0:T(8,128)(2,1)}), bf16[128,8,512]{2,1,0:T(8,128)(2,1)S(1)}, u32[]{:S(2)}, u32[]{:S(2)}) async-start(bf16[128,8,512]{2,1,0:T(8,128)(2,1)} %gather_fusion.2), calls=%async_computation.3 | async-start | bytes 2097152 | tf_op jit(solution)/shard_map/all_to_all | solution.py:103
  136.5 0.0 copy-done.4
  136.6 0.1 compare_select_fusion
  136.8 0.1 fusion.77
  136.9 0.1 pad_add_fusion
  137.0 30.0 %all-to-all-done.3 = bf16[128,8,512]{2,1,0:T(8,128)(2,1)S(1)} async-done(((bf16[128,8,512]{2,1,0:T(8,128)(2,1)}), bf16[128,8,512]{2,1,0:T(8,128)(2,1)S(1)}, u32[]{:S(2)}, u32[]{:S(2)}) %all-to-all-start.3) | async-done | bytes 1048608 | tf_op jit(solution)/shard_map/all_to_all | solution.py:103
  167.0 0.5 gather_fusion.3
  167.6 3.8 %collective-permute-start.2 = (bf16[8,4,256]{2,1,0:T(4,128)(2,1)S(1)}, bf16[8,4,256]{2,1,0:T(4,128)(2,1)S(1)}, u32[]{:S(2)}, u32[]{:S(2)}) collective-permute-start(bf16[8,4,256]{2,1,0:T(4,128)(2,1)S(1)} %get-tuple-element.56), channel_id=1, source_target_pairs={{0,4},{4,8},{8,12},{12,16},{16,20},{20,24},{24,28},{28,32},{32,36}... | collective-permute-start | bytes 49160 | tf_op jit(solution)/shard_map/ppermute | solution.py:34
  171.4 1.9 %collective-permute-start.3 = (bf16[8,4,256]{2,1,0:T(4,128)(2,1)S(1)}, bf16[8,4,256]{2,1,0:T(4,128)(2,1)S(1)}, u32[]{:S(2)}, u32[]{:S(2)}) collective-permute-start(bf16[8,4,256]{2,1,0:T(4,128)(2,1)S(1)} %get-tuple-element.57), channel_id=1, source_target_pairs={{4,0},{8,4},{12,8},{16,12},{20,16},{24,20},{28,24},{32,28},{36,32}... | collective-permute-start | bytes 49160 | tf_op jit(solution)/shard_map/ppermute | solution.py:35
  173.3 0.6 gather_fusion.4
  174.0 0.2 broadcast_multiply_fusion.2
  174.3 0.2 broadcast_multiply_fusion.1
  174.5 0.2 broadcast_multiply_fusion
  174.7 0.2 pad_slice_fusion.3
  174.9 0.1 fusion.20
  175.0 0.0 collective-permute-done.2
  175.0 1.4 collective-permute-done.3
  176.5 0.2 broadcast_multiply_fusion.8
  176.7 0.1 broadcast_multiply_fusion.7
  176.9 0.1 broadcast_multiply_fusion.4
  177.0 0.2 broadcast_multiply_fusion.3
  177.3 0.1 pad_slice_fusion.35
  177.4 0.1 pad_slice_fusion.19
  177.5 0.1 fusion.61
  177.6 0.7 pad_maximum_fusion.2
  (41 shorter events, 0.5 us)
Async XLA Ops:
  0.0 39.2 %copy-start.6 = (bf16[16,2,128]{2,1,0:T(2,128)(2,1)S(1)}, bf16[16,2,128]{2,1,0:T(2,128)(2,1)}, u32[]{:S(2)}) copy-start(bf16[16,2,128]{2,1,0:T(2,128)(2,1)} %param.7) | copy-start | bytes 24580
  0.0 39.2 %copy-start.2 = (bf16[16,2,99,128]{3,1,2,0:T(2,128)(2,1)S(1)}, bf16[16,2,99,128]{3,1,2,0:T(2,128)(2,1)}, u32[]{:S(2)}) copy-start(bf16[16,2,99,128]{3,1,2,0:T(2,128)(2,1)} %param.8) | copy-start | bytes 2433028
  1.8 29.9 %all-to-all-start.1 = ((s32[128,1,128]{2,1,0:T(1,128)}), s32[128,1,128]{2,1,0:T(1,128)S(1)}, u32[]{:S(2)}, u32[]{:S(2)}) async-start(s32[128,1,128]{2,1,0:T(1,128)} %broadcast_in_dim.64), calls=%async_computation.1 | async-start | bytes 131072 | tf_op jit(solution)/shard_map/all_to_all | solution.py:70
  33.5 36.1 %all-to-all-start.2 = ((bf16[128,8,512]{2,1,0:T(8,128)(2,1)}), bf16[128,8,512]{2,1,0:T(8,128)(2,1)S(1)}, u32[]{:S(2)}, u32[]{:S(2)}) async-start(bf16[128,8,512]{2,1,0:T(8,128)(2,1)} %gather_fusion), calls=%async_computation.2 | async-start | bytes 2097152 | tf_op jit(solution)/shard_map/all_to_all | solution.py:90
  69.6 2.1 %copy-start = (bf16[128,8,512]{2,1,0:T(8,128)(2,1)}, bf16[128,8,512]{2,1,0:T(8,128)(2,1)S(1)}, u32[]{:S(2)}) copy-start(bf16[128,8,512]{2,1,0:T(8,128)(2,1)S(1)} %all-to-all-done.2) | copy-start | bytes 3145732
  71.7 4.2 %copy-start.3 = (f32[32,256]{1,0:T(8,128)S(1)}, f32[32,256]{1,0:T(8,128)}, u32[]{:S(2)}) copy-start(f32[32,256]{1,0:T(8,128)} %param.11) | copy-start | bytes 98308
  71.7 4.2 %copy-start.5 = (s32[32,256]{1,0:T(8,128)S(1)}, s32[32,256]{1,0:T(8,128)}, u32[]{:S(2)}) copy-start(s32[32,256]{1,0:T(8,128)} %param.10) | copy-start | bytes 98308
  71.7 41.2 %all-to-all-start = ((bf16[4,16,2,100,128]{4,1,3,2,0:T(8,128)(2,1)}), bf16[4,16,2,100,128]{4,1,3,2,0:T(8,128)(2,1)S(1)}, u32[]{:S(2)}, u32[]{:S(2)}) async-start(bf16[4,16,2,100,128]{4,1,3,2,0:T(8,128)(2,1)} %broadcast_in_dim.60), calls=%async_computation | async-start | bytes 6553600 | tf_op jit(solution)/shard_map/all_to_all | solution.py:76
  75.9 7.3 %collective-permute-start = (f32[2,4,256]{2,1,0:T(4,128)S(1)}, f32[2,4,256]{2,1,0:T(4,128)S(1)}, u32[]{:S(2)}, u32[]{:S(2)}) collective-permute-start(f32[2,4,256]{2,1,0:T(4,128)S(1)} %get-tuple-element.48), channel_id=1, source_target_pairs={{0,4},{4,8},{8,12},{12,16},{16,20},{20,24},{24,28},{28,32},{32,36}... | collective-permute-start | bytes 24584 | tf_op jit(solution)/shard_map/ppermute | solution.py:34
  79.8 5.3 %collective-permute-start.1 = (f32[2,4,256]{2,1,0:T(4,128)S(1)}, f32[2,4,256]{2,1,0:T(4,128)S(1)}, u32[]{:S(2)}, u32[]{:S(2)}) collective-permute-start(f32[2,4,256]{2,1,0:T(4,128)S(1)} %get-tuple-element.49), channel_id=1, source_target_pairs={{4,0},{8,4},{12,8},{16,12},{20,16},{24,20},{28,24},{32,28},{36,32}... | collective-permute-start | bytes 24584 | tf_op jit(solution)/shard_map/ppermute | solution.py:35
  118.9 1.9 %copy-start.1 = (f32[16,8,4,128]{3,1,0,2:T(8,128)S(1)}, f32[16,8,4,128]{3,1,0,2:T(8,128)}, u32[]{:S(2)}) copy-start(f32[16,8,4,128]{3,1,0,2:T(8,128)} %copy.48) | copy-start | bytes 786436
  125.4 11.2 %copy-start.4 = (f32[2,40,256]{2,1,0:T(8,128)S(1)}, f32[2,40,256]{2,1,0:T(8,128)}, u32[]{:S(2)}) copy-start(f32[2,40,256]{2,1,0:T(8,128)} %pad_maximum_fusion.3) | copy-start | bytes 245764
  127.2 39.8 %all-to-all-start.3 = ((bf16[128,8,512]{2,1,0:T(8,128)(2,1)}), bf16[128,8,512]{2,1,0:T(8,128)(2,1)S(1)}, u32[]{:S(2)}, u32[]{:S(2)}) async-start(bf16[128,8,512]{2,1,0:T(8,128)(2,1)} %gather_fusion.2), calls=%async_computation.3 | async-start | bytes 2097152 | tf_op jit(solution)/shard_map/all_to_all | solution.py:103
  167.6 7.4 %collective-permute-start.2 = (bf16[8,4,256]{2,1,0:T(4,128)(2,1)S(1)}, bf16[8,4,256]{2,1,0:T(4,128)(2,1)S(1)}, u32[]{:S(2)}, u32[]{:S(2)}) collective-permute-start(bf16[8,4,256]{2,1,0:T(4,128)(2,1)S(1)} %get-tuple-element.56), channel_id=1, source_target_pairs={{0,4},{4,8},{8,12},{12,16},{16,20},{20,24},{24,28},{28,32},{32,36}... | collective-permute-start | bytes 49160 | tf_op jit(solution)/shard_map/ppermute | solution.py:34
  171.4 5.1 %collective-permute-start.3 = (bf16[8,4,256]{2,1,0:T(4,128)(2,1)S(1)}, bf16[8,4,256]{2,1,0:T(4,128)(2,1)S(1)}, u32[]{:S(2)}, u32[]{:S(2)}) collective-permute-start(bf16[8,4,256]{2,1,0:T(4,128)(2,1)S(1)} %get-tuple-element.57), channel_id=1, source_target_pairs={{4,0},{8,4},{12,8},{16,12},{20,16},{24,20},{28,24},{32,28},{36,32}... | collective-permute-start | bytes 49160 | tf_op jit(solution)/shard_map/ppermute | solution.py:35

commit v10 on v6

--- a/solution.py
+++ b/solution.py
@@ -68,19 +68,21 @@
 
     lanes = 128
     recv_rows = lax.all_to_all(
-        jnp.broadcast_to(slot_table.astype(jnp.int32)[:, None], (ntiles, lanes)),
+        jnp.broadcast_to(slot_table.astype(jnp.bfloat16)[:, None], (ntiles, lanes)),
         "tiles", 0, 0, tiled=True,
     )
 
+    recv_rows = recv_rows.astype(jnp.int32)
     picked = jnp.minimum(recv_rows[:, 0], owned - 1)
     slot_ids = jnp.arange(owned, dtype=jnp.int32)
     holder = jnp.sum(
         jnp.where(recv_rows[:, :owned] == slot_ids[None, :], tile_ids[:, None], 0), axis=0
     )
 
-    local = observed.reshape(day_count, owned, ndays, quarter)
-    outgoing = jnp.take(local, picked, axis=1, mode="clip")
-    outgoing = outgoing.transpose(1, 2, 0, 3).reshape(ntiles * ndays, day_count, quarter)
+    local = observed.reshape(day_count, owned, ndays, quarter).transpose(1, 2, 0, 3)
+    local = lax.optimization_barrier(local)
+    outgoing = jnp.take(local, picked, axis=0, mode="clip")
+    outgoing = outgoing.reshape(ntiles * ndays, day_count, quarter)
     arrived = lax.all_to_all(outgoing, ("tiles", "days"), 0, 0, tiled=True)
     arrived = arrived.reshape(ntiles, ndays * day_count, quarter)
     own_rows = jnp.take(arrived, target, axis=0, mode="clip")

time: 133 us -> 133 us (level)
  no operation moved by 1% of the time
where the time goes in v10:
time: 133 us
  waiting for transfers between devices  66.3 us (50%)
  starting transfers between devices  49 us (37%)
  local copies, waits for them, and re-layouts  9.72 us (7%)
  other arithmetic  7.21 us (5%)
    all_to_all x1, waiting for transfers between devices, body(): returned = lax.all_to_all(packed, ('tiles', 'days'), 0, 0, tiled=True)  32.1 us
    all_to_all x1, waiting for transfers between devices, body(): arrived = lax.all_to_all(outgoing, ('tiles', 'days'), 0, 0, tiled=True)  22.7 us
    all_to_all x1, starting transfers between devices, body(): lax.all_to_all(jnp.broadcast_to(slot_table.astype(jnp.bfloat16)[:, None],...  18.4 us
    all_to_all x1, waiting for transfers between devices, body(): lax.all_to_all(jnp.broadcast_to(slot_table.astype(jnp.bfloat16)[:, None],...  10.4 us
    all_to_all x1, starting transfers between devices, body(): returned = lax.all_to_all(packed, ('tiles', 'days'), 0, 0, tiled=True)  9.16 us
    all_to_all x1, starting transfers between devices, body(): arrived = lax.all_to_all(outgoing, ('tiles', 'days'), 0, 0, tiled=True)  8.94 us
    ppermute x2, starting transfers between devices, with_halo(): lax.ppermute(tail, 'tiles', [(i, i + 1) for i in range(count - 1)])  6.97 us
    ppermute x2, starting transfers between devices, with_halo(): lax.ppermute(head, 'tiles', [(i + 1, i) for i in range(count - 1)])  5.49 us
  transfers between devices with their start and end apart: 7, of which 4 were waited for; matrix products, arithmetic and copies ran while one was open for 4% of the time, Pallas kernels for 0%

profile of v10, /device:TPU:1, one launch (start us, length us, event | category | flops | bytes accessed | tf_op | source)
XLA Modules:
  0.0 132.7 jit_solution(10996771428656673951)
XLA Ops:
  0.0 0.7 and_select_fusion
  0.7 0.1 fusion.52
  0.8 0.1 select_reduce_fusion.1
  0.9 0.8 broadcast_in_dim.59
  1.7 18.4 %all-to-all-start = ((bf16[128,1,128]{2,1,0:T(2,128)(2,1)}), bf16[128,1,128]{2,1,0:T(2,128)(2,1)S(1)}, u32[]{:S(2)}, u32[]{:S(2)}) async-start(bf16[128,1,128]{2,1,0:T(2,128)(2,1)} %broadcast_in_dim.59), calls=%async_computation | async-start | bytes 131072 | tf_op jit(solution)/shard_map/all_to_all | solution.py:70
  20.2 0.9 reshape.65
  21.1 0.1 copy.74
  21.2 10.4 %all-to-all-done = bf16[128,1,128]{2,1,0:T(2,128)(2,1)S(1)} async-done(((bf16[128,1,128]{2,1,0:T(2,128)(2,1)}), bf16[128,1,128]{2,1,0:T(2,128)(2,1)S(1)}, u32[]{:S(2)}, u32[]{:S(2)}) %all-to-all-start) | async-done | bytes 32800 | tf_op jit(solution)/shard_map/all_to_all | solution.py:70
  31.6 0.1 convert_element_type.84
  31.7 0.1 fusion.51
  31.8 1.7 %gather_fusion = bf16[128,4,8,128]{3,2,1,0:T(8,128)(2,1)} fusion(bf16[16,4,8,128]{3,2,1,0:T(8,128)(2,1)S(1)} %bitcast.46, s32[1024]{0:T(1024)S(1)} %pad_clamp_fusion.4), kind=kCustom, calls=%fused_computation | custom fusion | bytes 2097664 | tf_op jit(solution)/shard_map/jit(_take)/gather | solution.py:84
  33.5 0.0 copy-start.1
  33.5 0.0 copy-start.3
  33.5 0.0 copy-start.4
  33.5 0.0 copy-start
  33.5 8.9 %all-to-all-start.1 = ((bf16[512,8,128]{2,1,0:T(8,128)(2,1)}), bf16[512,8,128]{2,1,0:T(8,128)(2,1)S(1)}, u32[]{:S(2)}, u32[]{:S(2)}) async-start(bf16[512,8,128]{2,1,0:T(8,128)(2,1)} %bitcast.11), calls=%async_computation.1 | async-start | bytes 2097152 | tf_op jit(solution)/shard_map/all_to_all | solution.py:86
  42.5 0.0 copy-done.1
  42.5 0.0 copy-done.3
  42.5 4.1 %collective-permute-start = (f32[2,4,256]{2,1,0:T(4,128)S(1)}, f32[2,4,256]{2,1,0:T(4,128)S(1)}, u32[]{:S(2)}, u32[]{:S(2)}) collective-permute-start(f32[2,4,256]{2,1,0:T(4,128)S(1)} %get-tuple-element.50), channel_id=1, source_target_pairs={{0,4},{4,8},{8,12},{12,16},{16,20},{20,24},{24,28},{28,32},{32,36}... | collective-permute-start | bytes 24584 | tf_op jit(solution)/shard_map/ppermute | solution.py:34
  46.6 3.6 %collective-permute-start.1 = (f32[2,4,256]{2,1,0:T(4,128)S(1)}, f32[2,4,256]{2,1,0:T(4,128)S(1)}, u32[]{:S(2)}, u32[]{:S(2)}) collective-permute-start(f32[2,4,256]{2,1,0:T(4,128)S(1)} %get-tuple-element.51), channel_id=1, source_target_pairs={{4,0},{8,4},{12,8},{16,12},{20,16},{24,20},{28,24},{32,28},{36,32}... | collective-permute-start | bytes 24584 | tf_op jit(solution)/shard_map/ppermute | solution.py:35
  50.2 0.0 copy-done.4
  50.2 0.0 copy-done
  50.2 1.1 fusion.73
  51.3 0.2 convert_divide_fusion
  51.6 0.1 broadcast_add_fusion
  51.7 0.2 multiply_reduce_fusion.1
  52.0 0.3 copy.51
  52.2 0.3 copy.53
  52.5 0.0 collective-permute-done
  52.5 0.0 collective-permute-done.1
  52.6 22.7 %all-to-all-done.1 = bf16[512,8,128]{2,1,0:T(8,128)(2,1)S(1)} async-done(((bf16[512,8,128]{2,1,0:T(8,128)(2,1)}), bf16[512,8,128]{2,1,0:T(8,128)(2,1)S(1)}, u32[]{:S(2)}, u32[]{:S(2)}) %all-to-all-start.1) | async-done | bytes 1048608 | tf_op jit(solution)/shard_map/all_to_all | solution.py:86
  75.3 0.6 gather_fusion.1
  75.9 2.9 %multiply_reduce_fusion = f32[16,32,128]{2,1,0:T(8,128)S(1)} fusion(f32[16,100,128]{2,1,0:T(8,128)S(1)} %copy.53, f32[16,32,128]{2,1,0:T(8,128)S(1)} %convert_element_type.78, f32[16,100,128]{2,1,0:T(8,128)S(1)} %copy.51), kind=kLoop, calls=%fused_computation.5 | loop fusion | flops 19595264 | bytes 2162688 | tf_op jit(solution)/shard_map/reduce_sum | solution.py:49
  78.8 1.7 %gather_fusion.2 = bf16[128,32,128]{2,1,0:T(8,128)(2,1)} fusion(bf16[16,32,128]{2,1,0:T(8,128)(2,1)S(1)} %add_convert_fusion, s32[1024]{0:T(1024)S(1)} %pad_clamp_fusion.2), kind=kCustom, calls=%fused_computation.2 | custom fusion | bytes 2097664 | tf_op jit(solution)/shard_map/jit(_take)/gather | solution.py:92
  80.5 9.2 %all-to-all-start.2 = ((bf16[512,8,128]{2,1,0:T(8,128)(2,1)}), bf16[512,8,128]{2,1,0:T(8,128)(2,1)S(1)}, u32[]{:S(2)}, u32[]{:S(2)}) async-start(bf16[512,8,128]{2,1,0:T(8,128)(2,1)} %bitcast.13), calls=%async_computation.2 | async-start | bytes 2097152 | tf_op jit(solution)/shard_map/all_to_all | solution.py:94
  89.7 0.1 compare_select_fusion
  89.8 0.0 copy-start.2
  89.9 0.1 fusion.77
  90.0 0.1 pad_add_fusion
  90.1 32.1 %all-to-all-done.2 = bf16[512,8,128]{2,1,0:T(8,128)(2,1)S(1)} async-done(((bf16[512,8,128]{2,1,0:T(8,128)(2,1)}), bf16[512,8,128]{2,1,0:T(8,128)(2,1)S(1)}, u32[]{:S(2)}, u32[]{:S(2)}) %all-to-all-start.2) | async-done | bytes 1048608 | tf_op jit(solution)/shard_map/all_to_all | solution.py:94
  122.2 0.6 gather_fusion.3
  122.8 2.9 %collective-permute-start.2 = (bf16[8,4,256]{2,1,0:T(4,128)(2,1)S(1)}, bf16[8,4,256]{2,1,0:T(4,128)(2,1)S(1)}, u32[]{:S(2)}, u32[]{:S(2)}) collective-permute-start(bf16[8,4,256]{2,1,0:T(4,128)(2,1)S(1)} %get-tuple-element.58), channel_id=1, source_target_pairs={{0,4},{4,8},{8,12},{12,16},{16,20},{20,24},{24,28},{28,32},{32,36}... | collective-permute-start | bytes 49160 | tf_op jit(solution)/shard_map/ppermute | solution.py:34
  125.7 1.9 %collective-permute-start.3 = (bf16[8,4,256]{2,1,0:T(4,128)(2,1)S(1)}, bf16[8,4,256]{2,1,0:T(4,128)(2,1)S(1)}, u32[]{:S(2)}, u32[]{:S(2)}) collective-permute-start(bf16[8,4,256]{2,1,0:T(4,128)(2,1)S(1)} %get-tuple-element.59), channel_id=1, source_target_pairs={{4,0},{8,4},{12,8},{16,12},{20,16},{24,20},{28,24},{32,28},{36,32}... | collective-permute-start | bytes 49160 | tf_op jit(solution)/shard_map/ppermute | solution.py:35
  127.7 0.6 gather_fusion.4
  128.2 0.1 copy.55
  128.3 0.1 reshape.71
  128.4 0.2 broadcast_multiply_fusion.2
  128.6 0.0 copy-done.2
  128.6 0.2 broadcast_multiply_fusion.1
  128.9 0.0 slice-start
  128.9 0.2 broadcast_multiply_fusion
  129.1 0.2 pad_slice_fusion.3
  129.3 0.3 slice-done
  129.6 0.1 fusion.18
  129.7 0.0 collective-permute-done.2
  129.7 1.0 collective-permute-done.3
  130.8 0.2 broadcast_multiply_fusion.8
  131.1 0.1 broadcast_multiply_fusion.7
  131.2 0.1 broadcast_multiply_fusion.4
  131.3 0.2 broadcast_multiply_fusion.3
  131.6 0.1 pad_slice_fusion.35
  131.7 0.1 pad_slice_fusion.19
  131.9 0.7 pad_maximum_fusion.1
  (31 shorter events, 0.4 us)
Async XLA Ops:
  1.7 29.9 %all-to-all-start = ((bf16[128,1,128]{2,1,0:T(2,128)(2,1)}), bf16[128,1,128]{2,1,0:T(2,128)(2,1)S(1)}, u32[]{:S(2)}, u32[]{:S(2)}) async-start(bf16[128,1,128]{2,1,0:T(2,128)(2,1)} %broadcast_in_dim.59), calls=%async_computation | async-start | bytes 131072 | tf_op jit(solution)/shard_map/all_to_all | solution.py:70
  33.5 9.0 %copy-start.1 = (f32[32,256]{1,0:T(8,128)S(1)}, f32[32,256]{1,0:T(8,128)}, u32[]{:S(2)}) copy-start(f32[32,256]{1,0:T(8,128)} %param.11) | copy-start | bytes 98308
  33.5 9.0 %copy-start.3 = (s32[32,256]{1,0:T(8,128)S(1)}, s32[32,256]{1,0:T(8,128)}, u32[]{:S(2)}) copy-start(s32[32,256]{1,0:T(8,128)} %param.10) | copy-start | bytes 98308
  33.5 16.7 %copy-start.4 = (bf16[16,2,128]{2,1,0:T(2,128)(2,1)S(1)}, bf16[16,2,128]{2,1,0:T(2,128)(2,1)}, u32[]{:S(2)}) copy-start(bf16[16,2,128]{2,1,0:T(2,128)(2,1)} %param.7) | copy-start | bytes 24580
  33.5 16.7 %copy-start = (bf16[16,2,99,128]{3,1,2,0:T(2,128)(2,1)S(1)}, bf16[16,2,99,128]{3,1,2,0:T(2,128)(2,1)}, u32[]{:S(2)}) copy-start(bf16[16,2,99,128]{3,1,2,0:T(2,128)(2,1)} %param.8) | copy-start | bytes 2433028
  33.5 41.8 %all-to-all-start.1 = ((bf16[512,8,128]{2,1,0:T(8,128)(2,1)}), bf16[512,8,128]{2,1,0:T(8,128)(2,1)S(1)}, u32[]{:S(2)}, u32[]{:S(2)}) async-start(bf16[512,8,128]{2,1,0:T(8,128)(2,1)} %bitcast.11), calls=%async_computation.1 | async-start | bytes 2097152 | tf_op jit(solution)/shard_map/all_to_all | solution.py:86
  42.5 10.0 %collective-permute-start = (f32[2,4,256]{2,1,0:T(4,128)S(1)}, f32[2,4,256]{2,1,0:T(4,128)S(1)}, u32[]{:S(2)}, u32[]{:S(2)}) collective-permute-start(f32[2,4,256]{2,1,0:T(4,128)S(1)} %get-tuple-element.50), channel_id=1, source_target_pairs={{0,4},{4,8},{8,12},{12,16},{16,20},{20,24},{24,28},{28,32},{32,36}... | collective-permute-start | bytes 24584 | tf_op jit(solution)/shard_map/ppermute | solution.py:34
  46.6 5.9 %collective-permute-start.1 = (f32[2,4,256]{2,1,0:T(4,128)S(1)}, f32[2,4,256]{2,1,0:T(4,128)S(1)}, u32[]{:S(2)}, u32[]{:S(2)}) collective-permute-start(f32[2,4,256]{2,1,0:T(4,128)S(1)} %get-tuple-element.51), channel_id=1, source_target_pairs={{4,0},{8,4},{12,8},{16,12},{20,16},{24,20},{28,24},{32,28},{36,32}... | collective-permute-start | bytes 24584 | tf_op jit(solution)/shard_map/ppermute | solution.py:35
  80.5 41.7 %all-to-all-start.2 = ((bf16[512,8,128]{2,1,0:T(8,128)(2,1)}), bf16[512,8,128]{2,1,0:T(8,128)(2,1)S(1)}, u32[]{:S(2)}, u32[]{:S(2)}) async-start(bf16[512,8,128]{2,1,0:T(8,128)(2,1)} %bitcast.13), calls=%async_computation.2 | async-start | bytes 2097152 | tf_op jit(solution)/shard_map/all_to_all | solution.py:94
  89.8 38.9 %copy-start.2 = (f32[40,256]{1,0:T(8,128)}, f32[40,256]{1,0:T(8,128)S(1)}, u32[]{:S(2)}) copy-start(f32[40,256]{1,0:T(8,128)S(1)} %compare_select_fusion) | copy-start | bytes 122884
  122.8 6.9 %collective-permute-start.2 = (bf16[8,4,256]{2,1,0:T(4,128)(2,1)S(1)}, bf16[8,4,256]{2,1,0:T(4,128)(2,1)S(1)}, u32[]{:S(2)}, u32[]{:S(2)}) collective-permute-start(bf16[8,4,256]{2,1,0:T(4,128)(2,1)S(1)} %get-tuple-element.58), channel_id=1, source_target_pairs={{0,4},{4,8},{8,12},{12,16},{16,20},{20,24},{24,28},{28,32},{32,36}... | collective-permute-start | bytes 49160 | tf_op jit(solution)/shard_map/ppermute | solution.py:34
  125.7 5.1 %collective-permute-start.3 = (bf16[8,4,256]{2,1,0:T(4,128)(2,1)S(1)}, bf16[8,4,256]{2,1,0:T(4,128)(2,1)S(1)}, u32[]{:S(2)}, u32[]{:S(2)}) collective-permute-start(bf16[8,4,256]{2,1,0:T(4,128)(2,1)S(1)} %get-tuple-element.59), channel_id=1, source_target_pairs={{4,0},{8,4},{12,8},{16,12},{20,16},{24,20},{28,24},{32,28},{36,32}... | collective-permute-start | bytes 49160 | tf_op jit(solution)/shard_map/ppermute | solution.py:35
  128.9 0.7 slice-start

commit v11 on v10

--- a/solution.py
+++ b/solution.py
@@ -1,6 +1,8 @@
 import jax
 import jax.numpy as jnp
 from jax import lax
+from jax.experimental import pallas as pl
+from jax.experimental.pallas import tpu as pltpu
 from jax.sharding import PartitionSpec as P
 
 PASSES = 4
@@ -24,6 +26,27 @@
         field = (center[None] * field + neighbour_sum(padded)) / denom[None]
     return field
 
+
+def _place_kernel(dst_ref, src_hbm, out_hbm, sems):
+    count = src_hbm.shape[0]
+    for j in range(count):
+        pltpu.make_async_copy(src_hbm.at[j], out_hbm.at[dst_ref[j]], sems.at[j]).start()
+    for j in range(count):
+        pltpu.make_async_copy(src_hbm.at[j], out_hbm.at[dst_ref[j]], sems.at[j]).wait()
+
+
+def place_rows(dst, src, total):
+    return pl.pallas_call(
+        _place_kernel,
+        grid_spec=pltpu.PrefetchScalarGridSpec(
+            num_scalar_prefetch=1,
+            grid=(1,),
+            in_specs=[pl.BlockSpec(memory_space=pl.ANY)],
+            out_specs=pl.BlockSpec(memory_space=pl.ANY),
+            scratch_shapes=[pltpu.SemaphoreType.DMA((src.shape[0],))],
+        ),
+        out_shape=jax.ShapeDtypeStruct((total,) + src.shape[1:], src.dtype),
+    )(dst, src)
 
 def with_halo(cells, width, edge_rows=None):
     count = lax.axis_size("tiles")
@@ -64,7 +87,6 @@
     match = target[None, :] == tile_ids[:, None]
     has = jnp.any(match, axis=1)
     slot_table = jnp.where(has, jnp.sum(jnp.where(match, place_slot[None, :], 0), axis=1), owned)
-    local_of = jnp.sum(jnp.where(match, jnp.arange(served, dtype=jnp.int32)[None, :], 0), axis=1)
 
     lanes = 128
     recv_rows = lax.all_to_all(
@@ -73,7 +95,6 @@
     )
 
     recv_rows = recv_rows.astype(jnp.int32)
-    picked = jnp.minimum(recv_rows[:, 0], owned - 1)
     slot_ids = jnp.arange(owned, dtype=jnp.int32)
     holder = jnp.sum(
         jnp.where(recv_rows[:, :owned] == slot_ids[None, :], tile_ids[:, None], 0), axis=0
@@ -81,7 +102,7 @@
 
     local = observed.reshape(day_count, owned, ndays, quarter).transpose(1, 2, 0, 3)
     local = lax.optimization_barrier(local)
-    outgoing = jnp.take(local, picked, axis=0, mode="clip")
+    outgoing = place_rows(holder, local.reshape(owned, ndays * day_count, quarter), ntiles)
     outgoing = outgoing.reshape(ntiles * ndays, day_count, quarter)
     arrived = lax.all_to_all(outgoing, ("tiles", "days"), 0, 0, tiled=True)
     arrived = arrived.reshape(ntiles, ndays * day_count, quarter)
@@ -89,7 +110,7 @@
 
     mapped_part = quantile_map(own_rows, knot_base, knot_steps)
 
-    packed = jnp.take(mapped_part, local_of, axis=0, mode="clip")
+    packed = place_rows(target, mapped_part, ntiles)
     packed = packed.reshape(ntiles * ndays, day_count, quarter)
     returned = lax.all_to_all(packed, ("tiles", "days"), 0, 0, tiled=True)
     returned = returned.reshape(ntiles, ndays, day_count, quarter)

time: 133 us -> 143 us (1.075)
  Pallas kernels: 0 us -> 11.8 us
  local copies, waits for them, and re-layouts: 9.72 us -> 7.03 us
    pallas_call x0 -> x2, Pallas kernels: none -> 11.8 us  [place_rows(): pl.pallas_call(_place_kernel, grid_spec=pltpu.PrefetchScalarGridSpec(num_...]
    gather x2 -> x0, local copies, waits for them, and re-layouts: 3.36 us -> none  [the longest x1 1.69 us: body(): outgoing = jnp.take(local, picked, axis=0, mode='clip')]
  transfers between devices with their start and end apart: 7 -> 7, of which waited for: 4 -> 4; matrix products, arithmetic and copies ran while one was open for 4% -> 7% of each run, Pallas kernels for 0% -> 4%
where the time goes in v11:
time: 143 us; the launch traced here: 142 us
  waiting for transfers between devices  65.7 us (46%)
  starting transfers between devices  49 us (34%)
  Pallas kernels  11.8 us (8%)
  other arithmetic  8.21 us (6%)
  local copies, waits for them, and re-layouts  7.03 us (5%)
    all_to_all x1, waiting for transfers between devices, body(): returned = lax.all_to_all(packed, ('tiles', 'days'), 0, 0, tiled=True)  32.1 us
    all_to_all x1, waiting for transfers between devices, body(): arrived = lax.all_to_all(outgoing, ('tiles', 'days'), 0, 0, tiled=True)  22.8 us
    all_to_all x1, starting transfers between devices, body(): lax.all_to_all(jnp.broadcast_to(slot_table.astype(jnp.bfloat16)[:, None],...  18.4 us
    pallas_call x2, Pallas kernels, place_rows(): pl.pallas_call(_place_kernel, grid_spec=pltpu.PrefetchScalarGridSpec(num_...  11.8 us
    all_to_all x1, waiting for transfers between devices, body(): lax.all_to_all(jnp.broadcast_to(slot_table.astype(jnp.bfloat16)[:, None],...  9.75 us
    all_to_all x1, starting transfers between devices, body(): returned = lax.all_to_all(packed, ('tiles', 'days'), 0, 0, tiled=True)  9.16 us
    all_to_all x1, starting transfers between devices, body(): arrived = lax.all_to_all(outgoing, ('tiles', 'days'), 0, 0, tiled=True)  8.93 us
    ppermute x2, starting transfers between devices, with_halo(): lax.ppermute(tail, 'tiles', [(i, i + 1) for i in range(count - 1)])  6.97 us
  transfers between devices with their start and end apart: 7, of which 4 were waited for; matrix products, arithmetic and copies ran while one was open for 7% of the time, Pallas kernels for 4%

profile of v11, /device:TPU:1, one launch (start us, length us, event | category | flops | bytes accessed | tf_op | source)
XLA Modules:
  0.0 142.2 jit_solution(5732566828910618475)
XLA Ops:
  0.0 0.7 and_select_fusion
  0.7 0.1 fusion.51
  0.8 0.1 select_reduce_fusion.1
  0.9 0.8 broadcast_in_dim.45
  1.7 18.4 %all-to-all-start = ((bf16[128,1,128]{2,1,0:T(2,128)(2,1)}), bf16[128,1,128]{2,1,0:T(2,128)(2,1)S(1)}, u32[]{:S(2)}, u32[]{:S(2)}) async-start(bf16[128,1,128]{2,1,0:T(2,128)(2,1)} %broadcast_in_dim.45), calls=%async_computation | async-start | bytes 131072 | tf_op jit(solution)/shard_map/all_to_all | solution.py:92
  20.2 0.9 reshape.68
  21.1 0.7 copy.71
  21.9 9.8 %all-to-all-done = bf16[128,1,128]{2,1,0:T(2,128)(2,1)S(1)} async-done(((bf16[128,1,128]{2,1,0:T(2,128)(2,1)}), bf16[128,1,128]{2,1,0:T(2,128)(2,1)S(1)}, u32[]{:S(2)}, u32[]{:S(2)}) %all-to-all-start) | async-done | bytes 32800 | tf_op jit(solution)/shard_map/all_to_all | solution.py:92
  31.6 0.6 select_reduce_fusion.dst_ref
  32.2 5.9 %shard_map.64 = bf16[128,32,128]{2,1,0:T(8,128)(2,1)} custom-call(s32[16]{0:T(128)} %select_reduce_fusion.dst_ref, bf16[16,32,128]{2,1,0:T(8,128)(2,1)} %bitcast.60), custom_call_target="tpu_custom_call" | custom-call | tf_op jit(solution)/shard_map/pallas_call | solution.py:39
  38.1 0.0 copy-start.1
  38.1 0.0 copy-start.3
  38.1 0.0 copy-start.4
  38.1 0.0 copy-start
  38.1 8.9 %all-to-all-start.1 = ((bf16[512,8,128]{2,1,0:T(8,128)(2,1)}), bf16[512,8,128]{2,1,0:T(8,128)(2,1)S(1)}, u32[]{:S(2)}, u32[]{:S(2)}) async-start(bf16[512,8,128]{2,1,0:T(8,128)(2,1)} %bitcast.50), calls=%async_computation.1 | async-start | bytes 2097152 | tf_op jit(solution)/shard_map/all_to_all | solution.py:107
  47.1 0.0 copy-done.1
  47.1 0.0 copy-done.3
  47.1 4.1 %collective-permute-start = (f32[2,4,256]{2,1,0:T(4,128)S(1)}, f32[2,4,256]{2,1,0:T(4,128)S(1)}, u32[]{:S(2)}, u32[]{:S(2)}) collective-permute-start(f32[2,4,256]{2,1,0:T(4,128)S(1)} %get-tuple-element.48), channel_id=1, source_target_pairs={{0,4},{4,8},{8,12},{12,16},{16,20},{20,24},{24,28},{28,32},{32,36}... | collective-permute-start | bytes 24584 | tf_op jit(solution)/shard_map/ppermute | solution.py:57
  51.2 3.6 %collective-permute-start.1 = (f32[2,4,256]{2,1,0:T(4,128)S(1)}, f32[2,4,256]{2,1,0:T(4,128)S(1)}, u32[]{:S(2)}, u32[]{:S(2)}) collective-permute-start(f32[2,4,256]{2,1,0:T(4,128)S(1)} %get-tuple-element.49), channel_id=1, source_target_pairs={{4,0},{8,4},{12,8},{16,12},{20,16},{24,20},{28,24},{32,28},{36,32}... | collective-permute-start | bytes 24584 | tf_op jit(solution)/shard_map/ppermute | solution.py:58
  54.8 0.0 copy-done.4
  54.8 0.0 copy-done
  54.8 1.1 fusion.72
  55.9 0.2 convert_divide_fusion
  56.1 0.1 broadcast_add_fusion
  56.3 0.2 multiply_reduce_fusion.1
  56.5 0.3 copy.46
  56.8 0.3 copy.48
  57.1 0.0 copy-done.6
  57.1 22.8 %all-to-all-done.1 = bf16[512,8,128]{2,1,0:T(8,128)(2,1)S(1)} async-done(((bf16[512,8,128]{2,1,0:T(8,128)(2,1)}), bf16[512,8,128]{2,1,0:T(8,128)(2,1)S(1)}, u32[]{:S(2)}, u32[]{:S(2)}) %all-to-all-start.1) | async-done | bytes 1048608 | tf_op jit(solution)/shard_map/all_to_all | solution.py:107
  79.9 0.6 gather_fusion
  80.5 2.9 %multiply_reduce_fusion = f32[16,32,128]{2,1,0:T(8,128)S(1)} fusion(f32[16,100,128]{2,1,0:T(8,128)S(1)} %copy.48, f32[16,32,128]{2,1,0:T(8,128)S(1)} %convert_element_type.75, f32[16,100,128]{2,1,0:T(8,128)S(1)} %copy.46), kind=kLoop, calls=%fused_computation.3 | loop fusion | flops 19595264 | bytes 2162688 | tf_op jit(solution)/shard_map/reduce_sum | solution.py:72
  83.4 0.7 add_convert_fusion.src_hbm
  84.0 5.9 %shard_map.65 = bf16[128,32,128]{2,1,0:T(8,128)(2,1)} custom-call(s32[16]{0:T(128)} %copy-done.6, bf16[16,32,128]{2,1,0:T(8,128)(2,1)} %add_convert_fusion.src_hbm), custom_call_target="tpu_custom_call" | custom-call | tf_op jit(solution)/shard_map/pallas_call | solution.py:39
  89.9 0.0 copy-start.5
  89.9 9.2 %all-to-all-start.2 = ((bf16[512,8,128]{2,1,0:T(8,128)(2,1)}), bf16[512,8,128]{2,1,0:T(8,128)(2,1)S(1)}, u32[]{:S(2)}, u32[]{:S(2)}) async-start(bf16[512,8,128]{2,1,0:T(8,128)(2,1)} %bitcast.49), calls=%async_computation.2 | async-start | bytes 2097152 | tf_op jit(solution)/shard_map/all_to_all | solution.py:115
  99.1 0.0 collective-permute-done
  99.1 0.0 collective-permute-done.1
  99.2 0.1 compare_select_fusion
  99.3 0.0 copy-start.2
  99.4 0.1 fusion.76
  99.5 0.1 pad_add_fusion
  99.6 32.1 %all-to-all-done.2 = bf16[512,8,128]{2,1,0:T(8,128)(2,1)S(1)} async-done(((bf16[512,8,128]{2,1,0:T(8,128)(2,1)}), bf16[512,8,128]{2,1,0:T(8,128)(2,1)S(1)}, u32[]{:S(2)}, u32[]{:S(2)}) %all-to-all-start.2) | async-done | bytes 1048608 | tf_op jit(solution)/shard_map/all_to_all | solution.py:115
  131.7 0.6 gather_fusion.1
  132.3 2.9 %collective-permute-start.2 = (bf16[8,4,256]{2,1,0:T(4,128)(2,1)S(1)}, bf16[8,4,256]{2,1,0:T(4,128)(2,1)S(1)}, u32[]{:S(2)}, u32[]{:S(2)}) collective-permute-start(bf16[8,4,256]{2,1,0:T(4,128)(2,1)S(1)} %get-tuple-element.56), channel_id=1, source_target_pairs={{0,4},{4,8},{8,12},{12,16},{16,20},{20,24},{24,28},{28,32},{32,36}... | collective-permute-start | bytes 49160 | tf_op jit(solution)/shard_map/ppermute | solution.py:57
  135.2 1.9 %collective-permute-start.3 = (bf16[8,4,256]{2,1,0:T(4,128)(2,1)S(1)}, bf16[8,4,256]{2,1,0:T(4,128)(2,1)S(1)}, u32[]{:S(2)}, u32[]{:S(2)}) collective-permute-start(bf16[8,4,256]{2,1,0:T(4,128)(2,1)S(1)} %get-tuple-element.57), channel_id=1, source_target_pairs={{4,0},{8,4},{12,8},{16,12},{20,16},{24,20},{28,24},{32,28},{36,32}... | collective-permute-start | bytes 49160 | tf_op jit(solution)/shard_map/ppermute | solution.py:58
  137.1 0.6 gather_fusion.2
  137.7 0.1 copy.50
  137.8 0.1 reshape.75
  137.9 0.2 broadcast_multiply_fusion.2
  138.1 0.2 broadcast_multiply_fusion.1
  138.3 0.0 slice-start
  138.3 0.2 broadcast_multiply_fusion
  138.6 0.2 pad_slice_fusion.3
  138.8 0.3 slice-done
  139.1 0.1 fusion.18
  139.2 0.0 collective-permute-done.2
  139.2 1.0 collective-permute-done.3
  140.3 0.2 broadcast_multiply_fusion.8
  140.5 0.1 broadcast_multiply_fusion.7
  140.7 0.1 broadcast_multiply_fusion.4
  140.8 0.2 broadcast_multiply_fusion.3
  141.0 0.1 pad_slice_fusion.35
  141.2 0.1 pad_slice_fusion.19
  141.4 0.7 pad_maximum_fusion.1
  (31 shorter events, 0.4 us)
Async XLA Ops:
  0.7 56.4 %copy-start.6 = (s32[16]{0:T(128)}, s32[16]{0:T(128)S(1)}, u32[]{:S(2)}) copy-start(s32[16]{0:T(128)S(1)} %get-tuple-element.63.dst_ref) | copy-start | bytes 196
  1.7 29.9 %all-to-all-start = ((bf16[128,1,128]{2,1,0:T(2,128)(2,1)}), bf16[128,1,128]{2,1,0:T(2,128)(2,1)S(1)}, u32[]{:S(2)}, u32[]{:S(2)}) async-start(bf16[128,1,128]{2,1,0:T(2,128)(2,1)} %broadcast_in_dim.45), calls=%async_computation | async-start | bytes 131072 | tf_op jit(solution)/shard_map/all_to_all | solution.py:92
  38.1 9.0 %copy-start.1 = (f32[32,256]{1,0:T(8,128)S(1)}, f32[32,256]{1,0:T(8,128)}, u32[]{:S(2)}) copy-start(f32[32,256]{1,0:T(8,128)} %param.11) | copy-start | bytes 98308
  38.1 9.0 %copy-start.3 = (s32[32,256]{1,0:T(8,128)S(1)}, s32[32,256]{1,0:T(8,128)}, u32[]{:S(2)}) copy-start(s32[32,256]{1,0:T(8,128)} %param.10) | copy-start | bytes 98308
  38.1 16.7 %copy-start.4 = (bf16[16,2,128]{2,1,0:T(2,128)(2,1)S(1)}, bf16[16,2,128]{2,1,0:T(2,128)(2,1)}, u32[]{:S(2)}) copy-start(bf16[16,2,128]{2,1,0:T(2,128)(2,1)} %param.7) | copy-start | bytes 24580
  38.1 16.7 %copy-start = (bf16[16,2,99,128]{3,1,2,0:T(2,128)(2,1)S(1)}, bf16[16,2,99,128]{3,1,2,0:T(2,128)(2,1)}, u32[]{:S(2)}) copy-start(bf16[16,2,99,128]{3,1,2,0:T(2,128)(2,1)} %param.8) | copy-start | bytes 2433028
  38.1 41.7 %all-to-all-start.1 = ((bf16[512,8,128]{2,1,0:T(8,128)(2,1)}), bf16[512,8,128]{2,1,0:T(8,128)(2,1)S(1)}, u32[]{:S(2)}, u32[]{:S(2)}) async-start(bf16[512,8,128]{2,1,0:T(8,128)(2,1)} %bitcast.50), calls=%async_computation.1 | async-start | bytes 2097152 | tf_op jit(solution)/shard_map/all_to_all | solution.py:107
  47.1 52.0 %collective-permute-start = (f32[2,4,256]{2,1,0:T(4,128)S(1)}, f32[2,4,256]{2,1,0:T(4,128)S(1)}, u32[]{:S(2)}, u32[]{:S(2)}) collective-permute-start(f32[2,4,256]{2,1,0:T(4,128)S(1)} %get-tuple-element.48), channel_id=1, source_target_pairs={{0,4},{4,8},{8,12},{12,16},{16,20},{20,24},{24,28},{28,32},{32,36}... | collective-permute-start | bytes 24584 | tf_op jit(solution)/shard_map/ppermute | solution.py:57
  51.2 47.9 %collective-permute-start.1 = (f32[2,4,256]{2,1,0:T(4,128)S(1)}, f32[2,4,256]{2,1,0:T(4,128)S(1)}, u32[]{:S(2)}, u32[]{:S(2)}) collective-permute-start(f32[2,4,256]{2,1,0:T(4,128)S(1)} %get-tuple-element.49), channel_id=1, source_target_pairs={{4,0},{8,4},{12,8},{16,12},{20,16},{24,20},{28,24},{32,28},{36,32}... | collective-permute-start | bytes 24584 | tf_op jit(solution)/shard_map/ppermute | solution.py:58
  89.9 9.5 %copy-start.5 = (s32[16]{0:T(128)S(1)}, s32[16]{0:T(128)}, u32[]{:S(2)}) copy-start(s32[16]{0:T(128)} %select_reduce_fusion.dst_ref) | copy-start | bytes 196
  89.9 41.7 %all-to-all-start.2 = ((bf16[512,8,128]{2,1,0:T(8,128)(2,1)}), bf16[512,8,128]{2,1,0:T(8,128)(2,1)S(1)}, u32[]{:S(2)}, u32[]{:S(2)}) async-start(bf16[512,8,128]{2,1,0:T(8,128)(2,1)} %bitcast.49), calls=%async_computation.2 | async-start | bytes 2097152 | tf_op jit(solution)/shard_map/all_to_all | solution.py:115
  99.3 38.8 %copy-start.2 = (f32[40,256]{1,0:T(8,128)}, f32[40,256]{1,0:T(8,128)S(1)}, u32[]{:S(2)}) copy-start(f32[40,256]{1,0:T(8,128)S(1)} %compare_select_fusion) | copy-start | bytes 122884
  132.3 6.9 %collective-permute-start.2 = (bf16[8,4,256]{2,1,0:T(4,128)(2,1)S(1)}, bf16[8,4,256]{2,1,0:T(4,128)(2,1)S(1)}, u32[]{:S(2)}, u32[]{:S(2)}) collective-permute-start(bf16[8,4,256]{2,1,0:T(4,128)(2,1)S(1)} %get-tuple-element.56), channel_id=1, source_target_pairs={{0,4},{4,8},{8,12},{12,16},{16,20},{20,24},{24,28},{28,32},{32,36}... | collective-permute-start | bytes 49160 | tf_op jit(solution)/shard_map/ppermute | solution.py:57
  135.2 5.1 %collective-permute-start.3 = (bf16[8,4,256]{2,1,0:T(4,128)(2,1)S(1)}, bf16[8,4,256]{2,1,0:T(4,128)(2,1)S(1)}, u32[]{:S(2)}, u32[]{:S(2)}) collective-permute-start(bf16[8,4,256]{2,1,0:T(4,128)(2,1)S(1)} %get-tuple-element.57), channel_id=1, source_target_pairs={{4,0},{8,4},{12,8},{16,12},{20,16},{24,20},{28,24},{32,28},{36,32}... | collective-permute-start | bytes 49160 | tf_op jit(solution)/shard_map/ppermute | solution.py:58
  138.3 0.7 slice-start

commit v12 on v7

--- a/solution.py
+++ b/solution.py
@@ -23,6 +23,18 @@
         padded = jnp.pad(field * weights[None], ((0, 0), (1, 1), (1, 1)))
         field = (center[None] * field + neighbour_sum(padded)) / denom[None]
     return field
+
+
+def select_rows(pick, rows):
+    depth = rows.shape[2]
+    eye = jnp.eye(depth, dtype=pick.dtype)
+    lhs = (pick[:, None, :, None] * eye[None, :, None, :]).reshape(pick.shape[0] * depth, -1)
+    lhs = jnp.broadcast_to(lhs[None], (rows.shape[0],) + lhs.shape)
+    flat = rows.reshape(rows.shape[0], rows.shape[1] * depth, rows.shape[3])
+    picked = lax.dot_general(
+        lhs, flat, (((2,), (1,)), ((0,), (0,))), preferred_element_type=jnp.float32
+    )
+    return picked.astype(jnp.bfloat16).reshape(rows.shape[0], pick.shape[0], depth, rows.shape[3])
 
 
 def with_halo(cells, width, edge_rows=None):
@@ -71,30 +83,32 @@
         "tiles", 0, 0, tiled=True,
     )
 
-    picked = jnp.minimum(recv_rows[:, 0], owned - 1)
     slot_ids = jnp.arange(owned, dtype=jnp.int32)
     holder = jnp.sum(
         jnp.where(recv_rows[:, :owned] == slot_ids[None, :], tile_ids[:, None], 0), axis=0
     )
 
-    local = observed.reshape(day_count, owned, ndays, quarter)
-    outgoing = jnp.take(local, picked, axis=1, mode="clip")
-    outgoing = outgoing.transpose(1, 2, 0, 3).reshape(ntiles * ndays, day_count, quarter)
-    arrived = lax.all_to_all(outgoing, ("tiles", "days"), 0, 0, tiled=True)
-    arrived = arrived.reshape(ntiles, ndays * day_count, quarter)
-    own_rows = jnp.take(arrived, target, axis=0, mode="clip")
+    pair = ("days", "tiles")
+    send_pick = (recv_rows[:, :owned] == slot_ids[None, :]).astype(jnp.bfloat16)
+    local = observed.reshape(day_count, owned, ndays, quarter).transpose(2, 1, 0, 3)
+    outgoing = select_rows(send_pick, local).reshape(ndays * ntiles, day_count, quarter)
+    arrived = lax.all_to_all(outgoing, pair, 0, 0, tiled=True)
+    arrived = arrived.reshape(ndays, ntiles, day_count, quarter)
+    own_rows = jnp.take(arrived, target, axis=1, mode="clip").transpose(1, 0, 2, 3)
+    own_rows = own_rows.reshape(served, ndays * day_count, quarter)
 
     mapped_part = quantile_map(own_rows, knot_base, knot_steps)
 
-    packed = arrived.at[target].set(mapped_part, unique_indices=True, mode="promise_in_bounds")
-    packed = packed.reshape(ntiles * ndays, day_count, quarter)
-    returned = lax.all_to_all(packed, ("tiles", "days"), 0, 0, tiled=True)
-    returned = returned.reshape(ntiles, ndays, day_count, quarter)
-    blocks = jnp.take(returned, holder, axis=0, mode="clip")
-    mapped = blocks.transpose(2, 0, 1, 3).reshape(day_count, row_count, columns)
+    mapped_part = mapped_part.reshape(served, ndays, day_count, quarter).transpose(1, 0, 2, 3)
+    packed = select_rows(match.astype(jnp.bfloat16), mapped_part)
+    packed = packed.reshape(ndays * ntiles, day_count, quarter)
+    returned = lax.all_to_all(packed, pair, 0, 0, tiled=True)
+    returned = returned.reshape(ndays, ntiles, day_count, quarter)
+    blocks = jnp.take(returned, holder, axis=1, mode="clip")
+    mapped = blocks.transpose(2, 1, 0, 3).reshape(day_count, row_count, columns)
     edge_count = PASSES // 2
     edges = jnp.concatenate([holder[:edge_count], holder[owned - edge_count :]])
-    edge_rows = jnp.take(returned, edges, axis=0, mode="clip").transpose(2, 0, 1, 3)
+    edge_rows = jnp.take(returned, edges, axis=1, mode="clip").transpose(2, 1, 0, 3)
     edge_rows = edge_rows.reshape(day_count, 2 * PASSES, columns)
 
     depth = PASSES

time: 137 us -> 143 us (1.044); the launches traced: 135 us -> 143 us
  local copies, waits for them, and re-layouts: 11.5 us -> 17.8 us
  other arithmetic: 7.13 us -> 10.6 us
  waiting for transfers between devices: 63.2 us -> 60.1 us
  matrix products: 0 us -> 2.87 us
  starting transfers between devices: 52.4 us -> 50.9 us
    mul x0 -> x2, local copies, waits for them, and re-layouts: none -> 11.8 us  [select_rows(): pick[:, None, :, None] * eye[None, :, None, :]]
    mul x0 -> x1, other arithmetic: none -> 3.62 us  [select_rows(): pick[:, None, :, None] * eye[None, :, None, :]]
    all_to_all x2, waiting for transfers between devices: 51.3 us -> 48.3 us  [the longest x1 31.9 us: body(): returned = lax.all_to_all(packed, pair, 0, 0, tiled=True)]
    dot_general x0 -> x2, matrix products: none -> 2.87 us  [select_rows(): lax.dot_general(lhs, flat, (((2,), (1,)), ((0,), (0,))), preferred_elemen...]
    gather x4 -> x3, local copies, waits for them, and re-layouts: 4.63 us -> 1.79 us  [the longest x1 0.61 us: body(): blocks = jnp.take(returned, holder, axis=1, mode='clip')]
    all_to_all x2, starting transfers between devices: 20.7 us -> 18.4 us  [the longest x1 9.57 us: body(): returned = lax.all_to_all(packed, pair, 0, 0, tiled=True)]
    scatter x1 -> x0, local copies, waits for them, and re-layouts: 2.21 us -> none  [body(): arrived.at[target]]
  transfers between devices with their start and end apart: 7 -> 7, of which waited for: 4 -> 4; matrix products, arithmetic and copies ran while one was open for 4% -> 11% of each run, Pallas kernels for 0% -> 0%
where the time goes in v12:
time: 143 us
  waiting for transfers between devices  60.1 us (42%)
  starting transfers between devices  50.9 us (36%)
  local copies, waits for them, and re-layouts  17.8 us (12%)
  other arithmetic  10.6 us (7%)
  matrix products  2.87 us (2%)
    all_to_all x1, waiting for transfers between devices, body(): returned = lax.all_to_all(packed, pair, 0, 0, tiled=True)  31.9 us
    all_to_all x1, starting transfers between devices, body(): lax.all_to_all(jnp.broadcast_to(slot_table.astype(jnp.int32)[:, None], (n...  18.4 us
    all_to_all x1, waiting for transfers between devices, body(): arrived = lax.all_to_all(outgoing, pair, 0, 0, tiled=True)  16.4 us
    mul x2, local copies, waits for them, and re-layouts, select_rows(): pick[:, None, :, None] * eye[None, :, None, :]  11.8 us
    all_to_all x1, waiting for transfers between devices, body(): lax.all_to_all(jnp.broadcast_to(slot_table.astype(jnp.int32)[:, None], (n...  10.5 us
    all_to_all x1, starting transfers between devices, body(): returned = lax.all_to_all(packed, pair, 0, 0, tiled=True)  9.57 us
    all_to_all x1, starting transfers between devices, body(): arrived = lax.all_to_all(outgoing, pair, 0, 0, tiled=True)  8.79 us
    ppermute x2, starting transfers between devices, with_halo(): lax.ppermute(tail, 'tiles', [(i, i + 1) for i in range(count - 1)])  8.44 us
  transfers between devices with their start and end apart: 7, of which 4 were waited for; matrix products, arithmetic and copies ran while one was open for 11% of the time, Pallas kernels for 0%

profile of v12, /device:TPU:1, one launch (start us, length us, event | category | flops | bytes accessed | tf_op | source)
XLA Modules:
  0.0 142.8 jit_solution(16541122537446218266)
XLA Ops:
  0.0 0.7 and_select_fusion
  0.7 0.1 fusion.59
  0.8 0.1 select_reduce_fusion.1
  0.9 0.8 broadcast_in_dim.49
  1.7 18.4 %all-to-all-start = ((s32[128,1,128]{2,1,0:T(1,128)}), s32[128,1,128]{2,1,0:T(1,128)S(1)}, u32[]{:S(2)}, u32[]{:S(2)}) async-start(s32[128,1,128]{2,1,0:T(1,128)} %broadcast_in_dim.49), calls=%async_computation | async-start | bytes 131072 | tf_op jit(solution)/shard_map/all_to_all | solution.py:81
  20.2 0.9 reshape.124
  21.1 10.5 %all-to-all-done = s32[128,1,128]{2,1,0:T(1,128)S(1)} async-done(((s32[128,1,128]{2,1,0:T(1,128)}), s32[128,1,128]{2,1,0:T(1,128)S(1)}, u32[]{:S(2)}, u32[]{:S(2)}) %all-to-all-start) | async-done | bytes 65568 | tf_op jit(solution)/shard_map/all_to_all | solution.py:81
  31.7 3.6 %broadcast_multiply_fusion = (bf16[128,8,16,8]{3,2,1,0:T(8,128)(2,1)}, bf16[128,8,16,8]{3,2,1,0:T(8,128)(2,1)}) fusion(bf16[128,16]{1,0:T(8,128)(2,1)S(1)} %convert_element_type.97, bf16[8,8]{1,0:T(8,128)(2,1)S(1)} %fusion.71, bf16[128,16]{1,0:T(8,128)(2,1)S(1)} %get-tuple-element.69), kind=kLoop, calls=%fused_computation.4 | loop fusion | flops 262144 | bytes 532608 | tf_op jit(solution)/shard_map/mul | solution.py:31
  35.3 0.0 copy-start.1
  35.3 0.0 copy-start.2
  35.3 0.0 copy-start.3
  35.3 0.0 copy-start
  35.3 5.9 %mul.117 = bf16[1024,128]{1,0:T(8,128)(2,1)S(1)} reshape(bf16[128,8,16,8]{3,2,1,0:T(8,128)(2,1)} %get-tuple-element.62) | data formatting | bytes 524288 | tf_op jit(solution)/shard_map/mul | solution.py:31
  41.2 1.4 %convolution_convert_fusion.1 = bf16[4,1024,128]{2,1,0:T(8,128)(2,1)} fusion(bf16[1024,128]{1,0:T(8,128)(2,1)S(1)} %mul.117, bf16[4,16,8,128]{3,0,1,2:T(4,128)(2,1)S(1)} %bitcast.79), kind=kOutput, calls=%fused_computation.7 | convolution fusion | flops 134742016 | bytes 1441792 | tf_op jit(solution)/shard_map/dot_general | solution.py:34
  42.7 8.8 %all-to-all-start.1 = ((bf16[512,8,128]{2,1,0:T(8,128)(2,1)}), bf16[512,8,128]{2,1,0:T(8,128)(2,1)S(1)}, u32[]{:S(2)}, u32[]{:S(2)}) async-start(bf16[512,8,128]{2,1,0:T(8,128)(2,1)} %bitcast.12), calls=%async_computation.1 | async-start | bytes 2097152 | tf_op jit(solution)/shard_map/all_to_all | solution.py:95
  51.5 0.0 copy-done.1
  51.5 0.0 copy-done.2
  51.5 4.1 %collective-permute-start = (f32[2,4,256]{2,1,0:T(4,128)S(1)}, f32[2,4,256]{2,1,0:T(4,128)S(1)}, u32[]{:S(2)}, u32[]{:S(2)}) collective-permute-start(f32[2,4,256]{2,1,0:T(4,128)S(1)} %get-tuple-element.50), channel_id=1, source_target_pairs={{0,4},{4,8},{8,12},{12,16},{16,20},{20,24},{24,28},{28,32},{32,36}... | collective-permute-start | bytes 24584 | tf_op jit(solution)/shard_map/ppermute | solution.py:46
  55.6 3.7 %collective-permute-start.1 = (f32[2,4,256]{2,1,0:T(4,128)S(1)}, f32[2,4,256]{2,1,0:T(4,128)S(1)}, u32[]{:S(2)}, u32[]{:S(2)}) collective-permute-start(f32[2,4,256]{2,1,0:T(4,128)S(1)} %get-tuple-element.51), channel_id=1, source_target_pairs={{4,0},{8,4},{12,8},{16,12},{20,16},{24,20},{28,24},{32,28},{36,32}... | collective-permute-start | bytes 24584 | tf_op jit(solution)/shard_map/ppermute | solution.py:47
  59.4 0.0 copy-done.3
  59.4 0.0 copy-done
  59.4 1.1 fusion.82
  60.5 0.2 convert_divide_fusion
  60.7 0.1 broadcast_add_fusion
  60.9 0.2 multiply_reduce_fusion.1
  61.1 0.3 copy.40
  61.4 0.3 copy.42
  61.7 5.8 %mul.112 = bf16[1024,128]{1,0:T(8,128)(2,1)S(1)} reshape(bf16[128,8,16,8]{3,2,1,0:T(8,128)(2,1)} %get-tuple-element.63) | data formatting | bytes 524288 | tf_op jit(solution)/shard_map/mul | solution.py:31
  67.6 16.4 %all-to-all-done.1 = bf16[512,8,128]{2,1,0:T(8,128)(2,1)S(1)} async-done(((bf16[512,8,128]{2,1,0:T(8,128)(2,1)}), bf16[512,8,128]{2,1,0:T(8,128)(2,1)S(1)}, u32[]{:S(2)}, u32[]{:S(2)}) %all-to-all-start.1) | async-done | bytes 1048608 | tf_op jit(solution)/shard_map/all_to_all | solution.py:95
  84.0 0.6 gather_fusion
  84.6 2.9 %multiply_reduce_fusion = f32[16,32,128]{2,1,0:T(8,128)S(1)} fusion(f32[16,100,128]{2,1,0:T(8,128)S(1)} %copy.42, f32[16,32,128]{2,1,0:T(8,128)S(1)} %bitcast_convert_fusion, f32[16,100,128]{2,1,0:T(8,128)S(1)} %copy.40), kind=kLoop, calls=%fused_computation.3 | loop fusion | flops 19595264 | bytes 2162688 | tf_op jit(solution)/shard_map/reduce_sum | solution.py:61
  87.5 1.4 convolution_convert_fusion
  88.9 9.6 %all-to-all-start.2 = ((bf16[512,8,128]{2,1,0:T(8,128)(2,1)}), bf16[512,8,128]{2,1,0:T(8,128)(2,1)S(1)}, u32[]{:S(2)}, u32[]{:S(2)}) async-start(bf16[512,8,128]{2,1,0:T(8,128)(2,1)} %bitcast.18), calls=%async_computation.2 | async-start | bytes 2097152 | tf_op jit(solution)/shard_map/all_to_all | solution.py:105
  98.5 0.0 collective-permute-done
  98.5 0.0 collective-permute-done.1
  98.5 0.1 compare_select_fusion
  98.8 0.1 fusion.86
  98.8 0.1 pad_add_fusion
  98.9 31.9 %all-to-all-done.2 = bf16[512,8,128]{2,1,0:T(8,128)(2,1)S(1)} async-done(((bf16[512,8,128]{2,1,0:T(8,128)(2,1)}), bf16[512,8,128]{2,1,0:T(8,128)(2,1)S(1)}, u32[]{:S(2)}, u32[]{:S(2)}) %all-to-all-start.2) | async-done | bytes 1048608 | tf_op jit(solution)/shard_map/all_to_all | solution.py:105
  130.8 0.6 gather_fusion.1
  131.5 4.4 %collective-permute-start.2 = (bf16[8,4,256]{2,1,0:T(4,128)(2,1)S(1)}, bf16[8,4,256]{2,1,0:T(4,128)(2,1)S(1)}, u32[]{:S(2)}, u32[]{:S(2)}) collective-permute-start(bf16[8,4,256]{2,1,0:T(4,128)(2,1)S(1)} %get-tuple-element.58), channel_id=1, source_target_pairs={{0,4},{4,8},{8,12},{12,16},{16,20},{20,24},{24,28},{28,32},{32,36}... | collective-permute-start | bytes 49160 | tf_op jit(solution)/shard_map/ppermute | solution.py:46
  135.8 1.9 %collective-permute-start.3 = (bf16[8,4,256]{2,1,0:T(4,128)(2,1)S(1)}, bf16[8,4,256]{2,1,0:T(4,128)(2,1)S(1)}, u32[]{:S(2)}, u32[]{:S(2)}) collective-permute-start(bf16[8,4,256]{2,1,0:T(4,128)(2,1)S(1)} %get-tuple-element.59), channel_id=1, source_target_pairs={{4,0},{8,4},{12,8},{16,12},{20,16},{24,20},{28,24},{32,28},{36,32}... | collective-permute-start | bytes 49160 | tf_op jit(solution)/shard_map/ppermute | solution.py:47
  137.8 0.6 gather_fusion.2
  138.4 0.1 copy.45
  138.4 0.1 reshape.130
  138.6 0.2 broadcast_multiply_fusion.4
  138.8 0.2 broadcast_multiply_fusion.3
  139.0 0.2 broadcast_multiply_fusion.2
  139.2 0.2 pad_slice_fusion.3
  139.4 0.1 fusion.21
  139.6 0.0 collective-permute-done.2
  139.6 1.3 collective-permute-done.3
  140.9 0.2 broadcast_multiply_fusion.10
  141.2 0.1 broadcast_multiply_fusion.9
  141.3 0.1 broadcast_multiply_fusion.6
  141.5 0.2 broadcast_multiply_fusion.5
  141.7 0.1 pad_slice_fusion.35
  141.8 0.1 pad_slice_fusion.19
  142.1 0.7 pad_maximum_fusion.1
  (31 shorter events, 0.4 us)
Async XLA Ops:
  1.7 29.9 %all-to-all-start = ((s32[128,1,128]{2,1,0:T(1,128)}), s32[128,1,128]{2,1,0:T(1,128)S(1)}, u32[]{:S(2)}, u32[]{:S(2)}) async-start(s32[128,1,128]{2,1,0:T(1,128)} %broadcast_in_dim.49), calls=%async_computation | async-start | bytes 131072 | tf_op jit(solution)/shard_map/all_to_all | solution.py:81
  35.3 16.2 %copy-start.1 = (f32[32,256]{1,0:T(8,128)S(1)}, f32[32,256]{1,0:T(8,128)}, u32[]{:S(2)}) copy-start(f32[32,256]{1,0:T(8,128)} %param.11) | copy-start | bytes 98308
  35.3 16.2 %copy-start.2 = (s32[32,256]{1,0:T(8,128)S(1)}, s32[32,256]{1,0:T(8,128)}, u32[]{:S(2)}) copy-start(s32[32,256]{1,0:T(8,128)} %param.10) | copy-start | bytes 98308
  35.3 24.1 %copy-start.3 = (bf16[16,2,128]{2,1,0:T(2,128)(2,1)S(1)}, bf16[16,2,128]{2,1,0:T(2,128)(2,1)}, u32[]{:S(2)}) copy-start(bf16[16,2,128]{2,1,0:T(2,128)(2,1)} %param.7) | copy-start | bytes 24580
  35.3 24.1 %copy-start = (bf16[16,2,99,128]{3,1,2,0:T(2,128)(2,1)S(1)}, bf16[16,2,99,128]{3,1,2,0:T(2,128)(2,1)}, u32[]{:S(2)}) copy-start(bf16[16,2,99,128]{3,1,2,0:T(2,128)(2,1)} %param.8) | copy-start | bytes 2433028
  42.7 41.3 %all-to-all-start.1 = ((bf16[512,8,128]{2,1,0:T(8,128)(2,1)}), bf16[512,8,128]{2,1,0:T(8,128)(2,1)S(1)}, u32[]{:S(2)}, u32[]{:S(2)}) async-start(bf16[512,8,128]{2,1,0:T(8,128)(2,1)} %bitcast.12), calls=%async_computation.1 | async-start | bytes 2097152 | tf_op jit(solution)/shard_map/all_to_all | solution.py:95
  51.5 46.9 %collective-permute-start = (f32[2,4,256]{2,1,0:T(4,128)S(1)}, f32[2,4,256]{2,1,0:T(4,128)S(1)}, u32[]{:S(2)}, u32[]{:S(2)}) collective-permute-start(f32[2,4,256]{2,1,0:T(4,128)S(1)} %get-tuple-element.50), channel_id=1, source_target_pairs={{0,4},{4,8},{8,12},{12,16},{16,20},{20,24},{24,28},{28,32},{32,36}... | collective-permute-start | bytes 24584 | tf_op jit(solution)/shard_map/ppermute | solution.py:46
  55.6 42.9 %collective-permute-start.1 = (f32[2,4,256]{2,1,0:T(4,128)S(1)}, f32[2,4,256]{2,1,0:T(4,128)S(1)}, u32[]{:S(2)}, u32[]{:S(2)}) collective-permute-start(f32[2,4,256]{2,1,0:T(4,128)S(1)} %get-tuple-element.51), channel_id=1, source_target_pairs={{4,0},{8,4},{12,8},{16,12},{20,16},{24,20},{28,24},{32,28},{36,32}... | collective-permute-start | bytes 24584 | tf_op jit(solution)/shard_map/ppermute | solution.py:47
  88.9 41.9 %all-to-all-start.2 = ((bf16[512,8,128]{2,1,0:T(8,128)(2,1)}), bf16[512,8,128]{2,1,0:T(8,128)(2,1)S(1)}, u32[]{:S(2)}, u32[]{:S(2)}) async-start(bf16[512,8,128]{2,1,0:T(8,128)(2,1)} %bitcast.18), calls=%async_computation.2 | async-start | bytes 2097152 | tf_op jit(solution)/shard_map/all_to_all | solution.py:105
  131.5 8.1 %collective-permute-start.2 = (bf16[8,4,256]{2,1,0:T(4,128)(2,1)S(1)}, bf16[8,4,256]{2,1,0:T(4,128)(2,1)S(1)}, u32[]{:S(2)}, u32[]{:S(2)}) collective-permute-start(bf16[8,4,256]{2,1,0:T(4,128)(2,1)S(1)} %get-tuple-element.58), channel_id=1, source_target_pairs={{0,4},{4,8},{8,12},{12,16},{16,20},{20,24},{24,28},{28,32},{32,36}... | collective-permute-start | bytes 49160 | tf_op jit(solution)/shard_map/ppermute | solution.py:46
  135.8 5.1 %collective-permute-start.3 = (bf16[8,4,256]{2,1,0:T(4,128)(2,1)S(1)}, bf16[8,4,256]{2,1,0:T(4,128)(2,1)S(1)}, u32[]{:S(2)}, u32[]{:S(2)}) collective-permute-start(bf16[8,4,256]{2,1,0:T(4,128)(2,1)S(1)} %get-tuple-element.59), channel_id=1, source_target_pairs={{4,0},{8,4},{12,8},{16,12},{20,16},{24,20},{28,24},{32,28},{36,32}... | collective-permute-start | bytes 49160 | tf_op jit(solution)/shard_map/ppermute | solution.py:47

commit v13 on v6

--- a/solution.py
+++ b/solution.py
@@ -67,10 +67,10 @@
     local_of = jnp.sum(jnp.where(match, jnp.arange(served, dtype=jnp.int32)[None, :], 0), axis=1)
 
     lanes = 128
-    recv_rows = lax.all_to_all(
-        jnp.broadcast_to(slot_table.astype(jnp.int32)[:, None], (ntiles, lanes)),
-        "tiles", 0, 0, tiled=True,
-    )
+    lane_slots = jnp.broadcast_to(place_slot[None, :, None], (ntiles, served, lanes))
+    send_rows = jnp.sum(jnp.where(match[:, :, None], lane_slots + 1, 0), axis=1) - 1
+    send_rows = jnp.where(send_rows < 0, owned, send_rows)
+    recv_rows = lax.all_to_all(send_rows.astype(jnp.int32), "tiles", 0, 0, tiled=True)
 
     picked = jnp.minimum(recv_rows[:, 0], owned - 1)
     slot_ids = jnp.arange(owned, dtype=jnp.int32)

time: 133 us -> 134 us (level)
  no operation moved by 1% of the time
where the time goes in v13:
time: 134 us; the launch traced here: 133 us
  waiting for transfers between devices  66.9 us (50%)
  starting transfers between devices  49 us (37%)
  local copies, waits for them, and re-layouts  8.87 us (7%)
  other arithmetic  8.07 us (6%)
    all_to_all x1, waiting for transfers between devices, body(): returned = lax.all_to_all(packed, ('tiles', 'days'), 0, 0, tiled=True)  32.1 us
    all_to_all x1, waiting for transfers between devices, body(): arrived = lax.all_to_all(outgoing, ('tiles', 'days'), 0, 0, tiled=True)  22.6 us
    all_to_all x1, starting transfers between devices, body(): lax.all_to_all(send_rows.astype(jnp.int32), 'tiles', 0, 0, tiled=True)  18.4 us
    all_to_all x1, waiting for transfers between devices, body(): lax.all_to_all(send_rows.astype(jnp.int32), 'tiles', 0, 0, tiled=True)  10.4 us
    all_to_all x1, starting transfers between devices, body(): returned = lax.all_to_all(packed, ('tiles', 'days'), 0, 0, tiled=True)  9.16 us
    all_to_all x1, starting transfers between devices, body(): arrived = lax.all_to_all(outgoing, ('tiles', 'days'), 0, 0, tiled=True)  8.93 us
    ppermute x2, starting transfers between devices, with_halo(): lax.ppermute(tail, 'tiles', [(i, i + 1) for i in range(count - 1)])  6.97 us
    ppermute x2, starting transfers between devices, with_halo(): lax.ppermute(head, 'tiles', [(i + 1, i) for i in range(count - 1)])  5.49 us
  transfers between devices with their start and end apart: 7, of which 4 were waited for; matrix products, arithmetic and copies ran while one was open for 4% of the time, Pallas kernels for 0%

profile of v13, /device:TPU:1, one launch (start us, length us, event | category | flops | bytes accessed | tf_op | source)
XLA Modules:
  0.0 133.3 jit_solution(11638322478717266098)
XLA Ops:
  0.0 0.7 and_select_fusion.1
  0.7 0.4 select_reduce_fusion
  1.1 0.6 compare_select_fusion
  1.7 18.4 %all-to-all-start = ((s32[128,1,128]{2,1,0:T(1,128)}), s32[128,1,128]{2,1,0:T(1,128)S(1)}, u32[]{:S(2)}, u32[]{:S(2)}) async-start(s32[128,1,128]{2,1,0:T(1,128)} %bitcast.10), calls=%async_computation | async-start | bytes 131072 | tf_op jit(solution)/shard_map/all_to_all | solution.py:73
  20.1 0.9 reshape.85
  21.1 0.1 copy.57
  21.2 10.4 %all-to-all-done = s32[128,1,128]{2,1,0:T(1,128)S(1)} async-done(((s32[128,1,128]{2,1,0:T(1,128)}), s32[128,1,128]{2,1,0:T(1,128)S(1)}, u32[]{:S(2)}, u32[]{:S(2)}) %all-to-all-start) | async-done | bytes 65568 | tf_op jit(solution)/shard_map/all_to_all | solution.py:73
  31.6 0.1 fusion.51
  31.7 1.7 %gather_fusion = bf16[128,8,4,128]{3,1,2,0:T(8,128)(2,1)} fusion(bf16[8,16,4,128]{3,0,2,1:T(8,128)(2,1)S(1)} %copy.57, s32[1024]{0:T(1024)S(1)} %pad_clamp_fusion.4), kind=kCustom, calls=%fused_computation | custom fusion | bytes 2097664 | tf_op jit(solution)/shard_map/jit(_take)/gather | solution.py:82
  33.4 0.0 copy-start.1
  33.4 0.0 copy-start.3
  33.4 0.0 copy-start.4
  33.4 0.0 copy-start
  33.4 8.9 %all-to-all-start.1 = ((bf16[512,8,128]{2,1,0:T(8,128)(2,1)}), bf16[512,8,128]{2,1,0:T(8,128)(2,1)S(1)}, u32[]{:S(2)}, u32[]{:S(2)}) async-start(bf16[512,8,128]{2,1,0:T(8,128)(2,1)} %bitcast.13), calls=%async_computation.1 | async-start | bytes 2097152 | tf_op jit(solution)/shard_map/all_to_all | solution.py:84
  42.4 0.0 copy-done.1
  42.4 0.0 copy-done.3
  42.4 4.1 %collective-permute-start = (f32[2,4,256]{2,1,0:T(4,128)S(1)}, f32[2,4,256]{2,1,0:T(4,128)S(1)}, u32[]{:S(2)}, u32[]{:S(2)}) collective-permute-start(f32[2,4,256]{2,1,0:T(4,128)S(1)} %get-tuple-element.48), channel_id=1, source_target_pairs={{0,4},{4,8},{8,12},{12,16},{16,20},{20,24},{24,28},{28,32},{32,36}... | collective-permute-start | bytes 24584 | tf_op jit(solution)/shard_map/ppermute | solution.py:34
  46.5 3.6 %collective-permute-start.1 = (f32[2,4,256]{2,1,0:T(4,128)S(1)}, f32[2,4,256]{2,1,0:T(4,128)S(1)}, u32[]{:S(2)}, u32[]{:S(2)}) collective-permute-start(f32[2,4,256]{2,1,0:T(4,128)S(1)} %get-tuple-element.49), channel_id=1, source_target_pairs={{4,0},{8,4},{12,8},{16,12},{20,16},{24,20},{28,24},{32,28},{36,32}... | collective-permute-start | bytes 24584 | tf_op jit(solution)/shard_map/ppermute | solution.py:35
  50.1 0.1 select_reduce_fusion.2
  50.2 0.0 copy-done.4
  50.2 0.0 copy-done
  50.2 1.1 fusion.73
  51.3 0.2 convert_divide_fusion
  51.5 0.1 broadcast_add_fusion
  51.7 0.2 multiply_reduce_fusion.1
  52.0 0.3 copy.58
  52.2 0.3 copy.55
  52.5 0.0 collective-permute-done
  52.5 0.0 collective-permute-done.1
  52.5 22.6 %all-to-all-done.1 = bf16[512,8,128]{2,1,0:T(8,128)(2,1)S(1)} async-done(((bf16[512,8,128]{2,1,0:T(8,128)(2,1)}), bf16[512,8,128]{2,1,0:T(8,128)(2,1)S(1)}, u32[]{:S(2)}, u32[]{:S(2)}) %all-to-all-start.1) | async-done | bytes 1048608 | tf_op jit(solution)/shard_map/all_to_all | solution.py:84
  75.2 0.6 gather_fusion.1
  75.8 2.9 %multiply_reduce_fusion = f32[16,32,128]{2,1,0:T(8,128)S(1)} fusion(f32[16,100,128]{2,1,0:T(8,128)S(1)} %copy.58, f32[16,32,128]{2,1,0:T(8,128)S(1)} %convert_element_type.62, f32[16,100,128]{2,1,0:T(8,128)S(1)} %copy.55), kind=kLoop, calls=%fused_computation.5 | loop fusion | flops 19595264 | bytes 2162688 | tf_op jit(solution)/shard_map/reduce_sum | solution.py:49
  78.7 1.7 %gather_fusion.2 = bf16[128,32,128]{2,1,0:T(8,128)(2,1)} fusion(bf16[16,32,128]{2,1,0:T(8,128)(2,1)S(1)} %add_convert_fusion, s32[1024]{0:T(1024)S(1)} %pad_clamp_fusion.2), kind=kCustom, calls=%fused_computation.2 | custom fusion | bytes 2097664 | tf_op jit(solution)/shard_map/jit(_take)/gather | solution.py:90
  80.4 9.2 %all-to-all-start.2 = ((bf16[512,8,128]{2,1,0:T(8,128)(2,1)}), bf16[512,8,128]{2,1,0:T(8,128)(2,1)S(1)}, u32[]{:S(2)}, u32[]{:S(2)}) async-start(bf16[512,8,128]{2,1,0:T(8,128)(2,1)} %bitcast.15), calls=%async_computation.2 | async-start | bytes 2097152 | tf_op jit(solution)/shard_map/all_to_all | solution.py:92
  89.5 0.1 compare_select_fusion.1
  89.6 0.0 copy-start.2
  89.8 0.1 fusion.77
  89.9 0.1 pad_add_fusion
  90.0 32.1 %all-to-all-done.2 = bf16[512,8,128]{2,1,0:T(8,128)(2,1)S(1)} async-done(((bf16[512,8,128]{2,1,0:T(8,128)(2,1)}), bf16[512,8,128]{2,1,0:T(8,128)(2,1)S(1)}, u32[]{:S(2)}, u32[]{:S(2)}) %all-to-all-start.2) | async-done | bytes 1048608 | tf_op jit(solution)/shard_map/all_to_all | solution.py:92
  122.1 0.6 gather_fusion.3
  122.6 0.6 gather_fusion.4
  123.2 0.1 copy.60
  123.3 0.1 reshape.91
  123.4 2.9 %collective-permute-start.2 = (bf16[8,4,256]{2,1,0:T(4,128)(2,1)S(1)}, bf16[8,4,256]{2,1,0:T(4,128)(2,1)S(1)}, u32[]{:S(2)}, u32[]{:S(2)}) collective-permute-start(bf16[8,4,256]{2,1,0:T(4,128)(2,1)S(1)} %get-tuple-element.56), channel_id=1, source_target_pairs={{0,4},{4,8},{8,12},{12,16},{16,20},{20,24},{24,28},{28,32},{32,36}... | collective-permute-start | bytes 49160 | tf_op jit(solution)/shard_map/ppermute | solution.py:34
  126.3 1.9 %collective-permute-start.3 = (bf16[8,4,256]{2,1,0:T(4,128)(2,1)S(1)}, bf16[8,4,256]{2,1,0:T(4,128)(2,1)S(1)}, u32[]{:S(2)}, u32[]{:S(2)}) collective-permute-start(bf16[8,4,256]{2,1,0:T(4,128)(2,1)S(1)} %get-tuple-element.57), channel_id=1, source_target_pairs={{4,0},{8,4},{12,8},{16,12},{20,16},{24,20},{28,24},{32,28},{36,32}... | collective-permute-start | bytes 49160 | tf_op jit(solution)/shard_map/ppermute | solution.py:35
  128.3 0.2 broadcast_multiply_fusion.2
  128.5 0.0 copy-done.2
  128.5 0.2 broadcast_multiply_fusion.1
  128.7 0.0 slice-start
  128.8 0.2 broadcast_multiply_fusion
  129.0 0.2 pad_slice_fusion.3
  129.2 0.3 slice-done
  129.5 0.1 fusion.18
  129.6 0.0 collective-permute-done.2
  129.6 1.8 %collective-permute-done.3 = bf16[8,4,256]{2,1,0:T(4,128)(2,1)S(1)} collective-permute-done((bf16[8,4,256]{2,1,0:T(4,128)(2,1)S(1)}, bf16[8,4,256]{2,1,0:T(4,128)(2,1)S(1)}, u32[]{:S(2)}, u32[]{:S(2)}) %collective-permute-start.3) | collective-permute-done | bytes 16416 | tf_op jit(solution)/shard_map/ppermute | solution.py:35
  131.4 0.2 broadcast_multiply_fusion.8
  131.7 0.1 broadcast_multiply_fusion.7
  131.8 0.1 broadcast_multiply_fusion.4
  132.0 0.2 broadcast_multiply_fusion.3
  132.2 0.1 pad_slice_fusion.19
  132.3 0.1 pad_slice_fusion.35
  132.6 0.7 pad_maximum_fusion.1
  (31 shorter events, 0.4 us)
Async XLA Ops:
  1.7 29.9 %all-to-all-start = ((s32[128,1,128]{2,1,0:T(1,128)}), s32[128,1,128]{2,1,0:T(1,128)S(1)}, u32[]{:S(2)}, u32[]{:S(2)}) async-start(s32[128,1,128]{2,1,0:T(1,128)} %bitcast.10), calls=%async_computation | async-start | bytes 131072 | tf_op jit(solution)/shard_map/all_to_all | solution.py:73
  33.4 8.9 %copy-start.1 = (f32[32,256]{1,0:T(8,128)S(1)}, f32[32,256]{1,0:T(8,128)}, u32[]{:S(2)}) copy-start(f32[32,256]{1,0:T(8,128)} %param.11) | copy-start | bytes 98308
  33.4 9.0 %copy-start.3 = (s32[32,256]{1,0:T(8,128)S(1)}, s32[32,256]{1,0:T(8,128)}, u32[]{:S(2)}) copy-start(s32[32,256]{1,0:T(8,128)} %param.10) | copy-start | bytes 98308
  33.4 16.8 %copy-start.4 = (bf16[16,2,128]{2,1,0:T(2,128)(2,1)S(1)}, bf16[16,2,128]{2,1,0:T(2,128)(2,1)}, u32[]{:S(2)}) copy-start(bf16[16,2,128]{2,1,0:T(2,128)(2,1)} %param.7) | copy-start | bytes 24580
  33.4 16.8 %copy-start = (bf16[16,2,99,128]{3,1,2,0:T(2,128)(2,1)S(1)}, bf16[16,2,99,128]{3,1,2,0:T(2,128)(2,1)}, u32[]{:S(2)}) copy-start(bf16[16,2,99,128]{3,1,2,0:T(2,128)(2,1)} %param.8) | copy-start | bytes 2433028
  33.4 41.7 %all-to-all-start.1 = ((bf16[512,8,128]{2,1,0:T(8,128)(2,1)}), bf16[512,8,128]{2,1,0:T(8,128)(2,1)S(1)}, u32[]{:S(2)}, u32[]{:S(2)}) async-start(bf16[512,8,128]{2,1,0:T(8,128)(2,1)} %bitcast.13), calls=%async_computation.1 | async-start | bytes 2097152 | tf_op jit(solution)/shard_map/all_to_all | solution.py:84
  42.4 10.1 %collective-permute-start = (f32[2,4,256]{2,1,0:T(4,128)S(1)}, f32[2,4,256]{2,1,0:T(4,128)S(1)}, u32[]{:S(2)}, u32[]{:S(2)}) collective-permute-start(f32[2,4,256]{2,1,0:T(4,128)S(1)} %get-tuple-element.48), channel_id=1, source_target_pairs={{0,4},{4,8},{8,12},{12,16},{16,20},{20,24},{24,28},{28,32},{32,36}... | collective-permute-start | bytes 24584 | tf_op jit(solution)/shard_map/ppermute | solution.py:34
  46.5 6.0 %collective-permute-start.1 = (f32[2,4,256]{2,1,0:T(4,128)S(1)}, f32[2,4,256]{2,1,0:T(4,128)S(1)}, u32[]{:S(2)}, u32[]{:S(2)}) collective-permute-start(f32[2,4,256]{2,1,0:T(4,128)S(1)} %get-tuple-element.49), channel_id=1, source_target_pairs={{4,0},{8,4},{12,8},{16,12},{20,16},{24,20},{28,24},{32,28},{36,32}... | collective-permute-start | bytes 24584 | tf_op jit(solution)/shard_map/ppermute | solution.py:35
  80.4 41.7 %all-to-all-start.2 = ((bf16[512,8,128]{2,1,0:T(8,128)(2,1)}), bf16[512,8,128]{2,1,0:T(8,128)(2,1)S(1)}, u32[]{:S(2)}, u32[]{:S(2)}) async-start(bf16[512,8,128]{2,1,0:T(8,128)(2,1)} %bitcast.15), calls=%async_computation.2 | async-start | bytes 2097152 | tf_op jit(solution)/shard_map/all_to_all | solution.py:92
  89.6 38.9 %copy-start.2 = (f32[40,256]{1,0:T(8,128)}, f32[40,256]{1,0:T(8,128)S(1)}, u32[]{:S(2)}) copy-start(f32[40,256]{1,0:T(8,128)S(1)} %compare_select_fusion.1) | copy-start | bytes 122884
  123.4 6.2 %collective-permute-start.2 = (bf16[8,4,256]{2,1,0:T(4,128)(2,1)S(1)}, bf16[8,4,256]{2,1,0:T(4,128)(2,1)S(1)}, u32[]{:S(2)}, u32[]{:S(2)}) collective-permute-start(bf16[8,4,256]{2,1,0:T(4,128)(2,1)S(1)} %get-tuple-element.56), channel_id=1, source_target_pairs={{0,4},{4,8},{8,12},{12,16},{16,20},{20,24},{24,28},{28,32},{32,36}... | collective-permute-start | bytes 49160 | tf_op jit(solution)/shard_map/ppermute | solution.py:34
  126.3 5.1 %collective-permute-start.3 = (bf16[8,4,256]{2,1,0:T(4,128)(2,1)S(1)}, bf16[8,4,256]{2,1,0:T(4,128)(2,1)S(1)}, u32[]{:S(2)}, u32[]{:S(2)}) collective-permute-start(bf16[8,4,256]{2,1,0:T(4,128)(2,1)S(1)} %get-tuple-element.57), channel_id=1, source_target_pairs={{4,0},{8,4},{12,8},{16,12},{20,16},{24,20},{28,24},{32,28},{36,32}... | collective-permute-start | bytes 49160 | tf_op jit(solution)/shard_map/ppermute | solution.py:35
  128.7 0.7 slice-start

commit v14 on v6

--- a/solution.py
+++ b/solution.py
@@ -19,9 +19,10 @@
 
 
 def smoothed(field, weights, center, denom):
+    edges = [(0, 0)] * (field.ndim - 2) + [(1, 1), (1, 1)]
     for sweep in range(PASSES):
-        padded = jnp.pad(field * weights[None], ((0, 0), (1, 1), (1, 1)))
-        field = (center[None] * field + neighbour_sum(padded)) / denom[None]
+        padded = jnp.pad(field * weights, edges)
+        field = (center * field + neighbour_sum(padded)) / denom
     return field
 
 
@@ -109,18 +110,17 @@
     own_center = wide_center[depth : depth + row_count]
     own_denom = wide_denom[depth : depth + row_count]
     field = mapped.astype(jnp.float32)
-    inner = smoothed(field, own_weights, own_center, own_denom)
+    inner = smoothed(field, own_weights[None], own_center[None], own_denom[None])
     wide_field = with_halo(mapped, depth, edge_rows).astype(jnp.float32)
     strip = 3 * depth
-    top = smoothed(
-        wide_field[:, :strip], wide_weights[:strip], wide_center[:strip], wide_denom[:strip]
-    )
     low = row_count + 2 * depth - strip
-    bottom = smoothed(
-        wide_field[:, low:], wide_weights[low:], wide_center[low:], wide_denom[low:]
+    def ends(rows):
+        return jnp.stack([rows[..., :strip, :], rows[..., low:, :]])
+    strips = smoothed(
+        ends(wide_field), ends(wide_weights)[:, None], ends(wide_center)[:, None], ends(wide_denom)[:, None]
     )
     return jnp.concatenate(
-        [top[:, depth : 2 * depth], inner[:, depth : row_count - depth], bottom[:, depth : 2 * depth]],
+        [strips[0][:, depth : 2 * depth], inner[:, depth : row_count - depth], strips[1][:, depth : 2 * depth]],
         axis=1,
     )
 

time: 133 us -> 134 us (level)
  waiting for transfers between devices: 66.3 us -> 68.2 us
    ppermute x2, waiting for transfers between devices: 1.05 us -> 2.98 us  [with_halo(): lax.ppermute(head, 'tiles', [(i + 1, i) for i in range(count - 1)])]
  transfers between devices with their start and end apart: 7 -> 7, of which waited for: 4 -> 4; matrix products, arithmetic and copies ran while one was open for 4% -> 7% of each run, Pallas kernels for 0% -> 0%
where the time goes in v14:
time: 134 us
  waiting for transfers between devices  68.2 us (51%)
  starting transfers between devices  49 us (37%)
  local copies, waits for them, and re-layouts  9.17 us (7%)
  other arithmetic  7.22 us (5%)
    all_to_all x1, waiting for transfers between devices, body(): returned = lax.all_to_all(packed, ('tiles', 'days'), 0, 0, tiled=True)  32.1 us
    all_to_all x1, waiting for transfers between devices, body(): arrived = lax.all_to_all(outgoing, ('tiles', 'days'), 0, 0, tiled=True)  22.8 us
    all_to_all x1, starting transfers between devices, body(): lax.all_to_all(jnp.broadcast_to(slot_table.astype(jnp.int32)[:, None], (n...  18.4 us
    all_to_all x1, waiting for transfers between devices, body(): lax.all_to_all(jnp.broadcast_to(slot_table.astype(jnp.int32)[:, None], (n...  10.4 us
    all_to_all x1, starting transfers between devices, body(): returned = lax.all_to_all(packed, ('tiles', 'days'), 0, 0, tiled=True)  9.16 us
    all_to_all x1, starting transfers between devices, body(): arrived = lax.all_to_all(outgoing, ('tiles', 'days'), 0, 0, tiled=True)  8.92 us
    ppermute x2, starting transfers between devices, with_halo(): lax.ppermute(tail, 'tiles', [(i, i + 1) for i in range(count - 1)])  6.97 us
    ppermute x2, starting transfers between devices, with_halo(): lax.ppermute(head, 'tiles', [(i + 1, i) for i in range(count - 1)])  5.49 us
  transfers between devices with their start and end apart: 7, of which 4 were waited for; matrix products, arithmetic and copies ran while one was open for 7% of the time, Pallas kernels for 0%

profile of v14, /device:TPU:1, one launch (start us, length us, event | category | flops | bytes accessed | tf_op | source)
XLA Modules:
  0.0 134.1 jit_solution(8967567040271930155)
XLA Ops:
  0.0 0.7 and_select_fusion
  0.7 0.1 fusion.43
  0.8 0.1 select_reduce_fusion.1
  0.9 0.8 broadcast_in_dim.80
  1.7 18.4 %all-to-all-start = ((s32[128,1,128]{2,1,0:T(1,128)}), s32[128,1,128]{2,1,0:T(1,128)S(1)}, u32[]{:S(2)}, u32[]{:S(2)}) async-start(s32[128,1,128]{2,1,0:T(1,128)} %broadcast_in_dim.80), calls=%async_computation | async-start | bytes 131072 | tf_op jit(solution)/shard_map/all_to_all | solution.py:71
  20.2 0.9 reshape.63
  21.1 0.1 copy.52
  21.2 10.4 %all-to-all-done = s32[128,1,128]{2,1,0:T(1,128)S(1)} async-done(((s32[128,1,128]{2,1,0:T(1,128)}), s32[128,1,128]{2,1,0:T(1,128)S(1)}, u32[]{:S(2)}, u32[]{:S(2)}) %all-to-all-start) | async-done | bytes 65568 | tf_op jit(solution)/shard_map/all_to_all | solution.py:71
  31.6 0.1 fusion.42
  31.7 1.7 %gather_fusion = bf16[128,8,4,128]{3,1,2,0:T(8,128)(2,1)} fusion(bf16[8,16,4,128]{3,0,2,1:T(8,128)(2,1)S(1)} %copy.52, s32[1024]{0:T(1024)S(1)} %pad_clamp_fusion.4), kind=kCustom, calls=%fused_computation | custom fusion | bytes 2097664 | tf_op jit(solution)/shard_map/jit(_take)/gather | solution.py:83
  33.4 0.0 copy-start.1
  33.4 0.0 copy-start.3
  33.4 0.0 copy-start.4
  33.4 0.0 copy-start
  33.4 8.9 %all-to-all-start.1 = ((bf16[512,8,128]{2,1,0:T(8,128)(2,1)}), bf16[512,8,128]{2,1,0:T(8,128)(2,1)S(1)}, u32[]{:S(2)}, u32[]{:S(2)}) async-start(bf16[512,8,128]{2,1,0:T(8,128)(2,1)} %bitcast.10), calls=%async_computation.1 | async-start | bytes 2097152 | tf_op jit(solution)/shard_map/all_to_all | solution.py:85
  42.4 0.0 copy-done.1
  42.4 0.0 copy-done.3
  42.4 4.1 %collective-permute-start = (f32[2,4,256]{2,1,0:T(4,128)S(1)}, f32[2,4,256]{2,1,0:T(4,128)S(1)}, u32[]{:S(2)}, u32[]{:S(2)}) collective-permute-start(f32[2,4,256]{2,1,0:T(4,128)S(1)} %get-tuple-element.34), channel_id=1, source_target_pairs={{0,4},{4,8},{8,12},{12,16},{16,20},{20,24},{24,28},{28,32},{32,36}... | collective-permute-start | bytes 24584 | tf_op jit(solution)/shard_map/ppermute | solution.py:35
  46.5 3.6 %collective-permute-start.1 = (f32[2,4,256]{2,1,0:T(4,128)S(1)}, f32[2,4,256]{2,1,0:T(4,128)S(1)}, u32[]{:S(2)}, u32[]{:S(2)}) collective-permute-start(f32[2,4,256]{2,1,0:T(4,128)S(1)} %get-tuple-element.35), channel_id=1, source_target_pairs={{4,0},{8,4},{12,8},{16,12},{20,16},{24,20},{28,24},{32,28},{36,32}... | collective-permute-start | bytes 24584 | tf_op jit(solution)/shard_map/ppermute | solution.py:36
  50.1 0.0 copy-done.4
  50.1 0.0 copy-done
  50.1 1.1 fusion.58
  51.2 0.2 convert_divide_fusion
  51.4 0.1 broadcast_add_fusion
  51.6 0.2 multiply_reduce_fusion.1
  51.8 0.3 copy.51
  52.1 0.3 copy.53
  52.4 22.8 %all-to-all-done.1 = bf16[512,8,128]{2,1,0:T(8,128)(2,1)S(1)} async-done(((bf16[512,8,128]{2,1,0:T(8,128)(2,1)}), bf16[512,8,128]{2,1,0:T(8,128)(2,1)S(1)}, u32[]{:S(2)}, u32[]{:S(2)}) %all-to-all-start.1) | async-done | bytes 1048608 | tf_op jit(solution)/shard_map/all_to_all | solution.py:85
  75.2 0.6 gather_fusion.1
  75.8 2.9 %multiply_reduce_fusion = f32[16,32,128]{2,1,0:T(8,128)S(1)} fusion(f32[16,100,128]{2,1,0:T(8,128)S(1)} %copy.53, f32[16,32,128]{2,1,0:T(8,128)S(1)} %convert_element_type.58, f32[16,100,128]{2,1,0:T(8,128)S(1)} %copy.51), kind=kLoop, calls=%fused_computation.5 | loop fusion | flops 19595264 | bytes 2162688 | tf_op jit(solution)/shard_map/reduce_sum | solution.py:50
  78.7 1.7 %gather_fusion.2 = bf16[128,32,128]{2,1,0:T(8,128)(2,1)} fusion(bf16[16,32,128]{2,1,0:T(8,128)(2,1)S(1)} %add_convert_fusion, s32[1024]{0:T(1024)S(1)} %pad_clamp_fusion.2), kind=kCustom, calls=%fused_computation.2 | custom fusion | bytes 2097664 | tf_op jit(solution)/shard_map/jit(_take)/gather | solution.py:91
  80.4 9.2 %all-to-all-start.2 = ((bf16[512,8,128]{2,1,0:T(8,128)(2,1)}), bf16[512,8,128]{2,1,0:T(8,128)(2,1)S(1)}, u32[]{:S(2)}, u32[]{:S(2)}) async-start(bf16[512,8,128]{2,1,0:T(8,128)(2,1)} %bitcast.12), calls=%async_computation.2 | async-start | bytes 2097152 | tf_op jit(solution)/shard_map/all_to_all | solution.py:93
  89.5 0.0 collective-permute-done
  89.6 0.0 collective-permute-done.1
  89.6 0.1 compare_select_fusion
  89.7 0.0 copy-start.2
  89.9 0.1 fusion.61
  89.9 0.1 pad_add_fusion
  90.0 32.1 %all-to-all-done.2 = bf16[512,8,128]{2,1,0:T(8,128)(2,1)S(1)} async-done(((bf16[512,8,128]{2,1,0:T(8,128)(2,1)}), bf16[512,8,128]{2,1,0:T(8,128)(2,1)S(1)}, u32[]{:S(2)}, u32[]{:S(2)}) %all-to-all-start.2) | async-done | bytes 1048608 | tf_op jit(solution)/shard_map/all_to_all | solution.py:93
  122.1 0.6 gather_fusion.4
  122.7 0.1 copy.55
  122.7 0.1 reshape.69
  122.8 0.2 broadcast_multiply_fusion.2
  123.1 0.0 copy-done.2
  123.1 0.2 broadcast_multiply_fusion.1
  123.3 0.2 broadcast_multiply_fusion
  123.5 0.0 slice-start
  123.5 0.2 pad_slice_fusion.3
  123.7 0.6 gather_fusion.3
  124.4 2.9 %collective-permute-start.2 = (bf16[8,4,256]{2,1,0:T(4,128)(2,1)S(1)}, bf16[8,4,256]{2,1,0:T(4,128)(2,1)S(1)}, u32[]{:S(2)}, u32[]{:S(2)}) collective-permute-start(bf16[8,4,256]{2,1,0:T(4,128)(2,1)S(1)} %get-tuple-element.40), channel_id=1, source_target_pairs={{0,4},{4,8},{8,12},{12,16},{16,20},{20,24},{24,28},{28,32},{32,36}... | collective-permute-start | bytes 49160 | tf_op jit(solution)/shard_map/ppermute | solution.py:35
  127.3 1.9 %collective-permute-start.3 = (bf16[8,4,256]{2,1,0:T(4,128)(2,1)S(1)}, bf16[8,4,256]{2,1,0:T(4,128)(2,1)S(1)}, u32[]{:S(2)}, u32[]{:S(2)}) collective-permute-start(bf16[8,4,256]{2,1,0:T(4,128)(2,1)S(1)} %get-tuple-element.41), channel_id=1, source_target_pairs={{4,0},{8,4},{12,8},{16,12},{20,16},{24,20},{28,24},{32,28},{36,32}... | collective-permute-start | bytes 49160 | tf_op jit(solution)/shard_map/ppermute | solution.py:36
  129.2 0.0 slice-done
  129.2 0.1 fusion.39
  129.4 0.0 collective-permute-done.2
  129.4 3.0 %collective-permute-done.3 = bf16[8,4,256]{2,1,0:T(4,128)(2,1)S(1)} collective-permute-done((bf16[8,4,256]{2,1,0:T(4,128)(2,1)S(1)}, bf16[8,4,256]{2,1,0:T(4,128)(2,1)S(1)}, u32[]{:S(2)}, u32[]{:S(2)}) %collective-permute-start.3) | collective-permute-done | bytes 16416 | tf_op jit(solution)/shard_map/ppermute | solution.py:36
  132.4 0.2 broadcast_multiply_fusion.5
  132.6 0.2 broadcast_multiply_fusion.4
  132.9 0.2 broadcast_multiply_fusion.3
  133.1 0.2 fusion.23
  133.4 0.7 pad_maximum_fusion.2
  (31 shorter events, 0.4 us)
Async XLA Ops:
  1.7 29.9 %all-to-all-start = ((s32[128,1,128]{2,1,0:T(1,128)}), s32[128,1,128]{2,1,0:T(1,128)S(1)}, u32[]{:S(2)}, u32[]{:S(2)}) async-start(s32[128,1,128]{2,1,0:T(1,128)} %broadcast_in_dim.80), calls=%async_computation | async-start | bytes 131072 | tf_op jit(solution)/shard_map/all_to_all | solution.py:71
  33.4 8.9 %copy-start.1 = (f32[32,256]{1,0:T(8,128)S(1)}, f32[32,256]{1,0:T(8,128)}, u32[]{:S(2)}) copy-start(f32[32,256]{1,0:T(8,128)} %param.11) | copy-start | bytes 98308
  33.4 9.0 %copy-start.3 = (s32[32,256]{1,0:T(8,128)S(1)}, s32[32,256]{1,0:T(8,128)}, u32[]{:S(2)}) copy-start(s32[32,256]{1,0:T(8,128)} %param.10) | copy-start | bytes 98308
  33.4 16.6 %copy-start.4 = (bf16[16,2,128]{2,1,0:T(2,128)(2,1)S(1)}, bf16[16,2,128]{2,1,0:T(2,128)(2,1)}, u32[]{:S(2)}) copy-start(bf16[16,2,128]{2,1,0:T(2,128)(2,1)} %param.7) | copy-start | bytes 24580
  33.4 16.7 %copy-start = (bf16[16,2,99,128]{3,1,2,0:T(2,128)(2,1)S(1)}, bf16[16,2,99,128]{3,1,2,0:T(2,128)(2,1)}, u32[]{:S(2)}) copy-start(bf16[16,2,99,128]{3,1,2,0:T(2,128)(2,1)} %param.8) | copy-start | bytes 2433028
  33.4 41.7 %all-to-all-start.1 = ((bf16[512,8,128]{2,1,0:T(8,128)(2,1)}), bf16[512,8,128]{2,1,0:T(8,128)(2,1)S(1)}, u32[]{:S(2)}, u32[]{:S(2)}) async-start(bf16[512,8,128]{2,1,0:T(8,128)(2,1)} %bitcast.10), calls=%async_computation.1 | async-start | bytes 2097152 | tf_op jit(solution)/shard_map/all_to_all | solution.py:85
  42.4 47.1 %collective-permute-start = (f32[2,4,256]{2,1,0:T(4,128)S(1)}, f32[2,4,256]{2,1,0:T(4,128)S(1)}, u32[]{:S(2)}, u32[]{:S(2)}) collective-permute-start(f32[2,4,256]{2,1,0:T(4,128)S(1)} %get-tuple-element.34), channel_id=1, source_target_pairs={{0,4},{4,8},{8,12},{12,16},{16,20},{20,24},{24,28},{28,32},{32,36}... | collective-permute-start | bytes 24584 | tf_op jit(solution)/shard_map/ppermute | solution.py:35
  46.5 43.1 %collective-permute-start.1 = (f32[2,4,256]{2,1,0:T(4,128)S(1)}, f32[2,4,256]{2,1,0:T(4,128)S(1)}, u32[]{:S(2)}, u32[]{:S(2)}) collective-permute-start(f32[2,4,256]{2,1,0:T(4,128)S(1)} %get-tuple-element.35), channel_id=1, source_target_pairs={{4,0},{8,4},{12,8},{16,12},{20,16},{24,20},{28,24},{32,28},{36,32}... | collective-permute-start | bytes 24584 | tf_op jit(solution)/shard_map/ppermute | solution.py:36
  80.4 41.7 %all-to-all-start.2 = ((bf16[512,8,128]{2,1,0:T(8,128)(2,1)}), bf16[512,8,128]{2,1,0:T(8,128)(2,1)S(1)}, u32[]{:S(2)}, u32[]{:S(2)}) async-start(bf16[512,8,128]{2,1,0:T(8,128)(2,1)} %bitcast.12), calls=%async_computation.2 | async-start | bytes 2097152 | tf_op jit(solution)/shard_map/all_to_all | solution.py:93
  89.7 33.4 %copy-start.2 = (f32[40,256]{1,0:T(8,128)}, f32[40,256]{1,0:T(8,128)S(1)}, u32[]{:S(2)}) copy-start(f32[40,256]{1,0:T(8,128)S(1)} %compare_select_fusion) | copy-start | bytes 122884
  123.5 5.7 %slice-start = ((f32[40,256]{1,0:T(8,128)}), f32[24,256]{1,0:T(8,128)S(1)}, s32[]{:S(2)}) async-start(f32[40,256]{1,0:T(8,128)} %copy-done.2), calls=%async_computation.3 | async-start | bytes 49152 | tf_op jit(solution)/shard_map/slice | solution.py:123
  124.4 5.0 %collective-permute-start.2 = (bf16[8,4,256]{2,1,0:T(4,128)(2,1)S(1)}, bf16[8,4,256]{2,1,0:T(4,128)(2,1)S(1)}, u32[]{:S(2)}, u32[]{:S(2)}) collective-permute-start(bf16[8,4,256]{2,1,0:T(4,128)(2,1)S(1)} %get-tuple-element.40), channel_id=1, source_target_pairs={{0,4},{4,8},{8,12},{12,16},{16,20},{20,24},{24,28},{28,32},{32,36}... | collective-permute-start | bytes 49160 | tf_op jit(solution)/shard_map/ppermute | solution.py:35
  127.3 5.1 %collective-permute-start.3 = (bf16[8,4,256]{2,1,0:T(4,128)(2,1)S(1)}, bf16[8,4,256]{2,1,0:T(4,128)(2,1)S(1)}, u32[]{:S(2)}, u32[]{:S(2)}) collective-permute-start(bf16[8,4,256]{2,1,0:T(4,128)(2,1)S(1)} %get-tuple-element.41), channel_id=1, source_target_pairs={{4,0},{8,4},{12,8},{16,12},{20,16},{24,20},{28,24},{32,28},{36,32}... | collective-permute-start | bytes 49160 | tf_op jit(solution)/shard_map/ppermute | solution.py:36
